TPU v7x, 32 devices: a whole 2x2x4 slice. The times are simulated.
32 devices in a mesh: groups: 2 (over x), rows: 16 (over z, y, core).
Axes of the slice: x: 2, y: 2, z: 4, core: 2. Of those that a mesh axis runs over, the one named last changes fastest.
Arguments:
- student: float32 [8192, 512], P(('groups', 'rows')), parts along dimension 0, may hold values from -6 to 6
- teacher: float32 [8192, 6144], P(('groups', 'rows')), parts along dimension 0, may hold values from -6 to 6
- heads: bfloat16 [512, 6144], P(None, 'rows'), may hold values from -0.25 to 0.25
Outputs:
- grad_student: float32 [8192, 512], P(('groups', 'rows')), parts along dimension 0
- grad_heads: float32 [1024, 6144], P('groups', 'rows'), parts along dimension 0
There are 2 independent parts, one for each index of `groups`. A program takes and returns all parts, laid end to end along the dimension named above; an argument that names none is the same for every part. Nothing has to cross between parts.
All inputs are finite; a program needn't handle non-finite values.
Results may differ from a plain program's by a relative error of at most 0.0026.
Values may be sent and summed in bfloat16 or wider, within the bound.
No kernel may reach another device: no remote copies, remote signals or barrier semaphores. Data moves between devices by JAX's collectives and lax.ppermute only.
A program may use at most 128 MiB of HBM per device.

v0:
```python
import jax
import jax.numpy as jnp
from jax import lax
from jax.sharding import PartitionSpec as P

reg_weight = 0.0625
head_scale = 0.015625


def contract(left, right, left_dim, right_dim):
    return lax.dot_general(
        left,
        right,
        (((left_dim,), (right_dim,)), ((), ())),
        precision=lax.Precision.HIGHEST,
        preferred_element_type=jnp.float32,
    )


def per_device(student, teacher, heads):
    devices = lax.axis_size("rows")
    rows_here, model_width = student.shape
    total_rows = rows_here * devices
    positions = jnp.arange(model_width)
    weights = (
        1.0
        + (positions < model_width // 4).astype(jnp.float32)
        + (positions < model_width // 2).astype(jnp.float32)
    )
    nested = jnp.minimum(weights[:, None], weights[None, :])
    gram_scale = 0.5 / total_rows
    wide_here = heads.astype(jnp.float32)
    moment = lax.psum(contract(student, student, 0, 0), "rows")
    cross_here = lax.psum_scatter(
        contract(teacher, student, 0, 0), "rows", scatter_dimension=0, tiled=True
    )
    grad_heads = head_scale * (contract(moment, wide_here, 1, 0) - cross_here.T)
    cross_sent = cross_here.T.astype(jnp.bfloat16)
    gathered = (
        lax.all_gather(heads, "rows", axis=1, tiled=True),
        lax.all_gather(cross_sent, "rows", axis=1, tiled=True),
    )
    wide_all = gathered[0].astype(jnp.float32)
    cross_all = gathered[1].astype(jnp.float32)
    error = contract(student, wide_all, 1, 0) - teacher
    shared = (
        reg_weight * contract(error, wide_all, 1, 1)
        - gram_scale * contract(teacher, cross_all, 1, 1) * weights[None, :]
    )
    grad_student = shared + gram_scale * contract(student, moment * nested, 1, 0)
    return (grad_student, grad_heads)


def solution(mesh):
    in_specs = (P(("groups", "rows"), None), P(("groups", "rows"), None), P(None, "rows"))
    out_specs = (P(("groups", "rows"), None), P("groups", "rows"))
    return jax.shard_map(
        per_device, mesh=mesh, in_specs=in_specs, out_specs=out_specs, check_vma=False
    )
```

profile of v0, /device:TPU:0, one launch (start us, length us, event | category | flops | bytes accessed | tf_op | source)
XLA Modules:
  0.0 414.8 jit_solution(12258084241356141119)
XLA Ops:
  7.2 0.0 copy-start
  7.2 0.0 reduce-scatter.2.cloned.1.call-start
  7.2 1.0 copy-done
  8.2 14.8 %fusion.9 = f32[6144,512]{1,0:T(8,128)} fusion(f32[256,6144]{1,0:T(8,128)} %param.4, f32[256,512]{1,0:T(8,128)S(1)} %copy-done), kind=kOutput, calls=%fused_computation.19 | convolution fusion | flops 9663676416 | bytes 19398656 | tf_op jit(solution)/shard_map/dot_general | solution.py:11
  23.0 0.0 reduce-scatter.2.cloned.1.call-update
  23.0 0.0 all-gather.3.cloned.1.call-start
  23.0 0.7 all-gather.3.cloned.1.call-update
  23.8 0.0 all-reduce.2.cloned.1.call-start
  23.8 2.0 fusion.10
  25.8 0.0 all-reduce.2.cloned.1.call-update
  25.9 0.2 all-gather.5.cloned.1.call-start
  26.1 134.4 %reduce-scatter.2.cloned.1.call-done = f32[384,512]{1,0:T(8,128)} async-done(((f32[6144,512]{1,0:T(8,128)}), f32[384,512]{1,0:T(8,128)}) %reduce-scatter.2.cloned.1.call-update) | async-done | bytes 786448 | tf_op jit(solution)/shard_map/reduce_scatter | solution.py:34
  160.5 1.9 bitcast_convert_fusion
  162.4 0.0 all-gather.5.cloned.1.call-update
  162.4 0.0 copy-start.2
  162.5 0.0 copy-start.3
  162.5 65.0 %all-gather.3.cloned.1.call-done = bf16[512,6144]{1,0:T(8,128)(2,1)} async-done(((bf16[512,384]{1,0:T(8,128)(2,1)}), bf16[512,6144]{1,0:T(8,128)(2,1)}) %all-gather.3.cloned.1.call-update) | async-done | bytes 6291472 | tf_op jit(solution)/shard_map/all_gather | solution.py:40
  227.5 10.7 %convolution_subtract_fusion = f32[256,6144]{1,0:T(8,128)} fusion(f32[256,6144]{1,0:T(8,128)} %param.4, f32[256,512]{1,0:T(8,128)S(1)} %copy-done, bf16[512,6144]{1,0:T(8,128)(2,1)} %all-gather.3.cloned.1.call-done), kind=kOutput, calls=%fused_computation | convolution fusion | flops 9665249280 | bytes 19398656 | tf_op jit(solution)/shard_map/dot_general | solution.py:11
  238.2 84.2 %all-reduce.2.cloned.1.call-done = f32[512,512]{1,0:T(8,128)} async-done(((f32[512,512]{1,0:T(8,128)}), f32[512,512]{1,0:T(8,128)}) %all-reduce.2.cloned.1.call-update) | async-done | bytes 1048592 | tf_op jit(solution)/shard_map/psum | solution.py:33
  322.4 0.0 copy-done.2
  322.4 0.0 copy-done.3
  322.4 2.1 fusion
  324.5 1.1 copy.8
  325.7 60.6 %all-gather.5.cloned.1.call-done = bf16[512,6144]{0,1:T(8,128)(2,1)} async-done(((bf16[512,384]{0,1:T(8,128)(2,1)}), bf16[512,6144]{0,1:T(8,128)(2,1)}) %all-gather.5.cloned.1.call-update) | async-done | bytes 6291472 | tf_op jit(solution)/shard_map/all_gather | solution.py:41
  386.3 9.8 %fusion.3 = f32[256,512]{1,0:T(8,128)S(1)} fusion(bf16[512,6144]{0,1:T(8,128)(2,1)} %all-gather.5.cloned.1.call-done, f32[256,6144]{1,0:T(8,128)} %param.4, f32[512]{0:T(512)S(1)} %broadcast_multiply_fusion), kind=kOutput, calls=%fused_computation.7 | convolution fusion | flops 9663807488 | bytes 13109248 | tf_op jit(solution)/shard_map/dot_general | solution.py:11
  396.1 0.0 copy-start.1
  396.1 10.1 %fusion.4 = f32[256,512]{1,0:T(8,128)S(1)} fusion(f32[256,512]{1,0:T(8,128)S(1)} %fusion.3, f32[256,6144]{1,0:T(8,128)} %convolution_subtract_fusion, bf16[512,6144]{1,0:T(8,128)(2,1)} %all-gather.3.cloned.1.call-done), kind=kOutput, calls=%fused_computation.9 | convolution fusion | flops 9663938560 | bytes 13631488 | tf_op jit(solution)/shard_map/dot_general | solution.py:11
  406.2 0.0 copy-done.1
  406.2 2.1 fusion.2
  (2 shorter events, 0.0 us)
Async XLA Ops:
  7.2 1.0 copy-start
  7.2 153.3 %reduce-scatter.2.cloned.1.call-start = ((), (), s32[]{:S(2)}) async-start(), calls=%async_computation.2 | async-start | bytes 13369344 | tf_op jit(solution)/shard_map/reduce_scatter | solution.py:34
  23.0 204.5 %all-gather.3.cloned.1.call-start = ((), (), s32[]{:S(2)}) async-start(), calls=%async_computation.1 | async-start | bytes 6684672 | tf_op jit(solution)/shard_map/all_gather | solution.py:40
  23.8 298.7 %all-reduce.2.cloned.1.call-start = ((), (), s32[]{:S(2)}) async-start(), calls=%async_computation.4 | async-start | bytes 2097152 | tf_op jit(solution)/shard_map/psum | solution.py:33
  25.9 360.4 %all-gather.5.cloned.1.call-start = ((), (), s32[]{:S(2)}) async-start(), calls=%async_computation.3 | async-start | bytes 6684672 | tf_op jit(solution)/shard_map/all_gather | solution.py:41
  162.4 160.0 %copy-start.2 = (f32[384,512]{1,0:T(8,128)S(1)}, f32[384,512]{1,0:T(8,128)}, u32[]{:S(2)}) copy-start(f32[384,512]{1,0:T(8,128)} %reduce-scatter.2.cloned.1.call-done) | copy-start | bytes 2359300
  162.5 160.0 %copy-start.3 = (bf16[512,384]{1,0:T(8,128)(2,1)S(1)}, bf16[512,384]{1,0:T(8,128)(2,1)}, u32[]{:S(2)}) copy-start(bf16[512,384]{1,0:T(8,128)(2,1)} %param.5) | copy-start | bytes 1179652
  396.1 10.1 %copy-start.1 = (f32[512,512]{1,0:T(8,128)S(1)}, f32[512,512]{1,0:T(8,128)}, u32[]{:S(2)}) copy-start(f32[512,512]{1,0:T(8,128)} %all-reduce.2.cloned.1.call-done) | copy-start | bytes 3145732
Sparse Core Ops, SparseCore 0:
  23.1 137.3 reduce-scatter.1
  162.6 64.7 all-gather.2
  230.9 91.4 all-reduce.1
  325.1 61.0 all-gather.4
where the time goes:
time: 415 us
  waiting for transfers between devices  345 us (83%)
  matrix products  51.6 us (12%)
  between operations  13.8 us (3%)
    reduce_scatter x1, waiting for transfers between devices, per_device(): lax.psum_scatter(contract(teacher, student, 0, 0), 'rows', scatter_dimens...  134 us
    psum x1, waiting for transfers between devices, per_device(): moment = lax.psum(contract(student, student, 0, 0), 'rows')  84.2 us
    all_gather x1, waiting for transfers between devices, per_device(): lax.all_gather(heads, 'rows', axis=1, tiled=True)  65 us
    all_gather x1, waiting for transfers between devices, per_device(): lax.all_gather(cross_sent, 'rows', axis=1, tiled=True)  60.6 us
    dot_general x7, matrix products, contract(): lax.dot_general(left, right, (((left_dim,), (right_dim,)), ((), ())), pre...  51.6 us
  transfers between devices with their start and end apart: 4, of which 4 were waited for; matrix products, arithmetic and copies ran while one was open for 4% of the time, Pallas kernels for 0%

commit v1 on v0

v1 whole, which is shorter than its diff:
```python
import jax
import jax.numpy as jnp
from jax import lax
from jax.sharding import PartitionSpec as P

reg_weight = 0.0625
head_scale = 0.015625


def contract(left, right, left_dim, right_dim, precision=lax.Precision.HIGHEST):
    return lax.dot_general(
        left,
        right,
        (((left_dim,), (right_dim,)), ((), ())),
        precision=precision,
        preferred_element_type=jnp.float32,
    )


def split_bf16(x):
    high = x.astype(jnp.bfloat16)
    low = (x - high.astype(jnp.float32)).astype(jnp.bfloat16)
    return high, low


def per_device(student, teacher, heads):
    devices = lax.axis_size("rows")
    rows_here, model_width = student.shape
    teacher_width = teacher.shape[1]
    total_rows = rows_here * devices
    f_here = teacher_width // devices
    d_here = model_width // devices
    positions = jnp.arange(model_width)
    weights = (
        1.0
        + (positions < model_width // 4).astype(jnp.float32)
        + (positions < model_width // 2).astype(jnp.float32)
    )
    nested = jnp.minimum(weights[:, None], weights[None, :])
    gram_scale = 0.5 / total_rows

    heads_all = lax.all_gather(heads, "rows", axis=1, tiled=True)

    left = jnp.concatenate(
        [
            teacher.reshape(rows_here, devices, f_here),
            student.reshape(rows_here, devices, d_here),
        ],
        axis=2,
    ).reshape(rows_here, devices * (f_here + d_here))
    partial = contract(left, student, 0, 0, lax.Precision.HIGH)
    reduced = lax.psum_scatter(partial, "rows", scatter_dimension=0, tiled=True)
    cross_here = reduced[:f_here]
    moment_here = reduced[f_here:]

    moment_high, moment_low = split_bf16(moment_here)
    packed = jnp.concatenate(
        [cross_here.astype(jnp.bfloat16), moment_high, moment_low], axis=0
    )
    gathered = lax.all_gather(packed, "rows", axis=0, tiled=False)
    cross_low = gathered[:, :f_here].reshape(teacher_width, model_width)
    moment = (
        gathered[:, f_here : f_here + d_here].astype(jnp.float32)
        + gathered[:, f_here + d_here :].astype(jnp.float32)
    ).reshape(model_width, model_width)

    grad_heads = head_scale * (
        contract(moment, heads.astype(jnp.float32), 1, 0) - cross_here.T
    )

    gram_heads = contract(heads_all, heads_all, 1, 1, lax.Precision.DEFAULT)
    teacher_high, teacher_low = split_bf16(teacher)
    teacher_heads = contract(teacher_high, heads_all, 1, 1, lax.Precision.DEFAULT) + contract(
        teacher_low, heads_all, 1, 1, lax.Precision.DEFAULT
    )
    teacher_cross = contract(teacher_high, cross_low, 1, 0, lax.Precision.DEFAULT) + contract(
        teacher_low, cross_low, 1, 0, lax.Precision.DEFAULT
    )
    student_side = reg_weight * gram_heads + gram_scale * (moment * nested)
    grad_student = (
        contract(student, student_side, 1, 0)
        - reg_weight * teacher_heads
        - gram_scale * teacher_cross * weights[None, :]
    )
    return (grad_student, grad_heads)


def solution(mesh):
    in_specs = (P(("groups", "rows"), None), P(("groups", "rows"), None), P(None, "rows"))
    out_specs = (P(("groups", "rows"), None), P("groups", "rows"))
    return jax.shard_map(
        per_device, mesh=mesh, in_specs=in_specs, out_specs=out_specs, check_vma=False
    )
```

time: 415 us -> 340 us (0.82)
  waiting for transfers between devices: 345 us -> 264 us
  local copies, waits for them, and re-layouts: 2.16 us -> 13.6 us
  matrix products: 51.6 us -> 41.4 us
  other arithmetic: 1.94 us -> 6.48 us
    psum x1 -> x0, waiting for transfers between devices: 84.2 us -> none  [per_device(): moment = lax.psum(contract(student, student, 0, 0), 'rows')]
    dot_general x7 -> x8, matrix products: 51.6 us -> 41.4 us  [contract(): lax.dot_general(left, right, (((left_dim,), (right_dim,)), ((), ())), pre...]
    reduce_scatter x1, waiting for transfers between devices: 134 us -> 144 us  [per_device(): reduced = lax.psum_scatter(partial, 'rows', scatter_dimension=0, tiled=True)]
    unnamed x9 -> x20, local copies, waits for them, and re-layouts: 2.16 us -> 9.04 us
    all_gather x2, waiting for transfers between devices: 126 us -> 119 us  [the longest x1 64.2 us: per_device(): heads_all = lax.all_gather(heads, 'rows', axis=1, tiled=True)]
    slice x0 -> x2, local copies, waits for them, and re-layouts: none -> 4.6 us  [the longest x1 3.42 us: per_device(): cross_low = gathered[:, :f_here].reshape(teacher_width, model_width)]
  transfers between devices with their start and end apart: 4 -> 3, of which waited for: 4 -> 3; matrix products, arithmetic and copies ran while one was open for 4% -> 5% of each run, Pallas kernels for 0% -> 0%
where the time goes in v1:
time: 340 us
  waiting for transfers between devices  264 us (78%)
  matrix products  41.4 us (12%)
  between operations  14 us (4%)
  local copies, waits for them, and re-layouts  13.6 us (4%)
  other arithmetic  6.48 us (2%)
    reduce_scatter x1, waiting for transfers between devices, per_device(): reduced = lax.psum_scatter(partial, 'rows', scatter_dimension=0, tiled=True)  144 us
    all_gather x1, waiting for transfers between devices, per_device(): heads_all = lax.all_gather(heads, 'rows', axis=1, tiled=True)  64.2 us
    all_gather x1, waiting for transfers between devices, per_device(): gathered = lax.all_gather(packed, 'rows', axis=0, tiled=False)  55 us
    dot_general x8, matrix products, contract(): lax.dot_general(left, right, (((left_dim,), (right_dim,)), ((), ())), pre...  41.4 us
    unnamed x20, local copies, waits for them, and re-layouts  9.04 us
  transfers between devices with their start and end apart: 3, of which 3 were waited for; matrix products, arithmetic and copies ran while one was open for 5% of the time, Pallas kernels for 0%

profile of v1, /device:TPU:0, one launch (start us, length us, event | category | flops | bytes accessed | tf_op | source)
XLA Modules:
  0.0 339.6 jit_solution(16316722309336753488)
XLA Ops:
  7.2 0.0 reduce-scatter.2.cloned.1.call-start
  7.2 6.7 %copy.11 = f32[256,6144]{0,1:T(8,128)} copy(f32[256,6144]{1,0:T(8,128)} %param.4) | data formatting | bytes 12582912 | tf_op args[1]
  13.9 0.2 copy.12
  14.1 3.2 pad_maximum_fusion
  17.3 8.6 %fusion.11 = f32[6656,512]{1,0:T(8,128)} fusion(f32[256,6656]{0,1:T(8,128)S(1)} %bitcast.34, f32[256,512]{1,0:T(8,128)S(1)} %copy-done.1), kind=kOutput, calls=%fused_computation.27 | convolution fusion | flops 5234491392 | bytes 20971520 | tf_op jit(solution)/shard_map/dot_general | solution.py:11
  25.9 0.0 reduce-scatter.2.cloned.1.call-update
  25.9 0.0 all-gather.4.cloned.1.call-start
  26.0 0.7 all-gather.4.cloned.1.call-update
  26.7 0.2 all-gather.6.cloned.1.call-start
  26.9 143.9 %reduce-scatter.2.cloned.1.call-done = f32[416,512]{1,0:T(8,128)} async-done(((f32[6656,512]{1,0:T(8,128)}), f32[416,512]{1,0:T(8,128)}) %reduce-scatter.2.cloned.1.call-update) | async-done | bytes 851984 | tf_op jit(solution)/shard_map/reduce_scatter | solution.py:52
  170.8 1.2 slice.31
  172.0 0.9 subtract_convert_fusion.1
  172.9 0.8 pad_maximum_fusion.1
  173.7 0.0 all-gather.6.cloned.1.call-update
  173.7 64.2 %all-gather.4.cloned.1.call-done = bf16[512,6144]{1,0:T(8,128)(2,1)} async-done(((bf16[512,384]{1,0:T(8,128)(2,1)}), bf16[512,6144]{1,0:T(8,128)(2,1)}) %all-gather.4.cloned.1.call-update) | async-done | bytes 6291472 | tf_op jit(solution)/shard_map/all_gather | solution.py:42
  237.9 6.6 %fusion.8 = f32[256,512]{0,1:T(8,128)S(1)} fusion(bf16[512,6144]{1,0:T(8,128)(2,1)} %all-gather.4.cloned.1.call-done, f32[256,6144]{1,0:T(8,128)} %param.4), kind=kOutput, calls=%fused_computation.24 | convolution fusion | flops 1612185600 | bytes 13107200 | tf_op jit(solution)/shard_map/dot_general | solution.py:11
  244.5 8.0 %fusion.6 = f32[256,512]{0,1:T(8,128)} fusion(f32[256,512]{0,1:T(8,128)S(1)} %fusion.8, bf16[512,6144]{1,0:T(8,128)(2,1)S(1)} %copy-done, f32[256,6144]{1,0:T(8,128)} %param.4), kind=kOutput, calls=%fused_computation.13 | convolution fusion | flops 1617166336 | bytes 13631488 | tf_op jit(solution)/shard_map/dot_general | solution.py:11
  252.5 55.0 %all-gather.6.cloned.1.call-done = bf16[7168,512]{1,0:T(8,128)(2,1)} async-done(((bf16[448,512]{1,0:T(8,128)(2,1)}), bf16[7168,512]{1,0:T(8,128)(2,1)}) %all-gather.6.cloned.1.call-update) | async-done | bytes 7340048 | tf_op jit(solution)/shard_map/all_gather | solution.py:60
  307.5 3.4 %slice.24 = bf16[16,384,512]{2,1,0:T(8,128)(2,1)S(1)} slice(bf16[16,448,512]{2,1,0:T(8,128)(2,1)} %bitcast.38), slice={[0:16], [0:384], [0:512]} | slice | bytes 12582912 | tf_op jit(solution)/shard_map/slice | solution.py:61
  311.0 0.0 slice-start
  311.0 0.0 slice-start.2
  311.0 1.5 convert_add_fusion
  312.5 0.0 slice-start.1
  312.5 0.0 slice-start.3
  312.5 8.5 %fusion.10 = f32[256,512]{0,1:T(8,128)S(1)} fusion(bf16[6144,512]{1,0:T(8,128)(2,1)S(1)} %bitcast.35, f32[256,6144]{1,0:T(8,128)} %param.4), kind=kOutput, calls=%fused_computation.26 | convolution fusion | flops 1616904192 | bytes 13107200 | tf_op jit(solution)/shard_map/dot_general | solution.py:11
  321.1 1.8 fusion.5
  322.9 0.0 copy-start.3
  323.0 3.5 %fusion = f32[512,512]{1,0:T(8,128)S(1)} fusion(bf16[512,6144]{1,0:T(8,128)(2,1)S(1)} %bitcast.41, f32[512,512]{1,0:T(8,128)S(1)} %bitcast.42, f32[512]{0:T(512)S(1)} %convert_add_fusion.1), kind=kOutput, calls=%fused_computation.3 | convolution fusion | flops 3222536192 | bytes 8390656 | tf_op jit(solution)/shard_map/dot_general | solution.py:11
  326.4 2.0 fusion.3
  328.5 1.0 copy.17
  329.5 2.4 fusion.1
  331.9 1.1 copy.18
  (15 shorter events, 0.0 us)
Async XLA Ops:
  7.2 163.6 %reduce-scatter.2.cloned.1.call-start = ((), (), s32[]{:S(2)}) async-start(), calls=%async_computation.2 | async-start | bytes 14483456 | tf_op jit(solution)/shard_map/reduce_scatter | solution.py:52
  7.2 6.7 %copy-start.1 = (f32[256,512]{1,0:T(8,128)S(1)}, f32[256,512]{1,0:T(8,128)}, u32[]{:S(2)}) copy-start(f32[256,512]{1,0:T(8,128)} %param.3) | copy-start | bytes 1572868
  25.9 212.0 %all-gather.4.cloned.1.call-start = ((), (), s32[]{:S(2)}) async-start(), calls=%async_computation.1 | async-start | bytes 6684672 | tf_op jit(solution)/shard_map/all_gather | solution.py:42
  26.7 280.8 %all-gather.6.cloned.1.call-start = ((), (), s32[]{:S(2)}) async-start(), calls=%async_computation.3 | async-start | bytes 7798784 | tf_op jit(solution)/shard_map/all_gather | solution.py:60
  237.9 6.6 %copy-start = (bf16[512,6144]{1,0:T(8,128)(2,1)S(1)}, bf16[512,6144]{1,0:T(8,128)(2,1)}, u32[]{:S(2)}) copy-start(bf16[512,6144]{1,0:T(8,128)(2,1)} %all-gather.4.cloned.1.call-done) | copy-start | bytes 18874372
  311.0 10.1 %slice-start = ((s8[6291456]{0:T(1024)(128)(4,1)}), s8[4194304]{0:T(1024)(128)(4,1)S(1)}, s32[]{:S(2)}) async-start(s8[6291456]{0:T(1024)(128)(4,1)} %bitcast.32), calls=%async_computation.4 | async-start | bytes 8388608
  311.0 12.0 %slice-start.2 = ((s8[6291456]{0:T(1024)(128)(4,1)}), s8[4194304]{0:T(1024)(128)(4,1)S(1)}, s32[]{:S(2)}) async-start(s8[6291456]{0:T(1024)(128)(4,1)} %bitcast.40), calls=%async_computation.6 | async-start | bytes 8388608
  312.5 10.4 %copy-start.2 = (f32[16,32,512]{2,1,0:T(8,128)}, f32[16,32,512]{2,1,0:T(8,128)S(1)}, u32[]{:S(2)}) copy-start(f32[16,32,512]{2,1,0:T(8,128)S(1)} %convert_add_fusion) | copy-start | bytes 3145732
  312.5 8.5 %slice-start.1 = ((s8[6291456]{0:T(1024)(128)(4,1)}), s8[2097152]{0:T(1024)(128)(4,1)S(1)}, s32[]{:S(2)}) async-start(s8[6291456]{0:T(1024)(128)(4,1)} %bitcast.32), calls=%async_computation.5 | async-start | bytes 4194304
  312.5 10.4 %slice-start.3 = ((s8[6291456]{0:T(1024)(128)(4,1)}), s8[2097152]{0:T(1024)(128)(4,1)S(1)}, s32[]{:S(2)}) async-start(s8[6291456]{0:T(1024)(128)(4,1)} %bitcast.40), calls=%async_computation.7 | async-start | bytes 4194304
  322.9 3.5 %copy-start.3 = (f32[256,512]{0,1:T(8,128)S(1)}, f32[256,512]{0,1:T(8,128)}, u32[]{:S(2)}) copy-start(f32[256,512]{0,1:T(8,128)} %fusion.6) | copy-start | bytes 1572868
Sparse Core Ops, SparseCore 0:
  26.1 144.6 reduce-scatter.1
  173.2 64.7 all-gather.3
  241.0 66.4 all-gather.5

commit v2 on v1

--- a/solution.py
+++ b/solution.py
@@ -18,9 +18,32 @@
 
 
 def split_bf16(x):
-    high = x.astype(jnp.bfloat16)
-    low = (x - high.astype(jnp.float32)).astype(jnp.bfloat16)
-    return high, low
+    high = lax.reduce_precision(x, exponent_bits=8, mantissa_bits=7)
+    low = (x - high).astype(jnp.bfloat16)
+    return high.astype(jnp.bfloat16), low
+
+
+def bit_reverse_table(n):
+    bits = n.bit_length() - 1
+    return [int(format(j, "0%db" % bits)[::-1], 2) if bits else 0 for j in range(n)]
+
+
+def gather_by_doubling(block, axis_name, axis):
+    n = lax.axis_size(axis_name)
+    me = lax.axis_index(axis_name)
+    held = block
+    bit = n.bit_length() - 2
+    while bit >= 0:
+        step = 1 << bit
+        pairs = [(i, i ^ step) for i in range(n)]
+        held = jnp.concatenate([held, lax.ppermute(held, axis_name, pairs)], axis=axis)
+        bit -= 1
+    rev = jnp.array(bit_reverse_table(n), jnp.int32)
+    order = rev[me] ^ rev
+    shape = held.shape
+    blocks = held.reshape(shape[:axis] + (n, shape[axis] // n) + shape[axis + 1 :])
+    blocks = jnp.take(blocks, order, axis=axis)
+    return blocks.reshape(shape)
 
 
 def per_device(student, teacher, heads):
@@ -39,7 +62,7 @@
     nested = jnp.minimum(weights[:, None], weights[None, :])
     gram_scale = 0.5 / total_rows
 
-    heads_all = lax.all_gather(heads, "rows", axis=1, tiled=True)
+    heads_all = gather_by_doubling(heads, "rows", 1)
 
     left = jnp.concatenate(
         [

time: 340 us -> 359 us (1.056); the launches traced: 340 us -> 352 us
  local copies, waits for them, and re-layouts: 13.6 us -> 46.7 us
  waiting for transfers between devices: 264 us -> 248 us
  matrix products: 41.4 us -> 26 us
  other arithmetic: 6.48 us -> 14.4 us
    ppermute x0 -> x4, waiting for transfers between devices: none -> 103 us  [gather_by_doubling(): lax.ppermute(held, axis_name, pairs)]
    all_gather x1 -> x0, waiting for transfers between devices: 64.2 us -> none  [per_device(): heads_all = lax.all_gather(heads, 'rows', axis=1, tiled=True)]
    all_gather x1, waiting for transfers between devices: 55 us -> 0.02 us  [per_device(): gathered = lax.all_gather(packed, 'rows', axis=0, tiled=False)]
    gather x0 -> x2, local copies, waits for them, and re-layouts: none -> 15.7 us  [gather_by_doubling(): blocks = jnp.take(blocks, order, axis=axis)]
    dot_general x8, matrix products: 41.4 us -> 26 us  [contract(): lax.dot_general(left, right, (((left_dim,), (right_dim,)), ((), ())), pre...]
    reshape x0 -> x1, local copies, waits for them, and re-layouts: none -> 8.63 us  [gather_by_doubling(): held.reshape(shape[:axis] + (n, shape[axis] // n) + shape[axis + 1:])]
    select_n x0 -> x1, other arithmetic: none -> 4.47 us  [gather_by_doubling(): blocks = jnp.take(blocks, order, axis=axis)]
    unnamed x20 -> x31, local copies, waits for them, and re-layouts: 9.04 us -> 13.1 us
  transfers between devices with their start and end apart: 3 -> 6, of which waited for: 3 -> 5; matrix products, arithmetic and copies ran while one was open for 5% -> 13% of each run, Pallas kernels for 0% -> 0%
where the time goes in v2:
time: 359 us; the launch traced here: 352 us
  waiting for transfers between devices  248 us (69%)
  local copies, waits for them, and re-layouts  46.7 us (13%)
  matrix products  26 us (7%)
  other arithmetic  14.4 us (4%)
  between operations  14.3 us (4%)
    reduce_scatter x1, waiting for transfers between devices, per_device(): reduced = lax.psum_scatter(partial, 'rows', scatter_dimension=0, tiled=True)  145 us
    ppermute x4, waiting for transfers between devices, gather_by_doubling(): lax.ppermute(held, axis_name, pairs)  103 us
    dot_general x8, matrix products, contract(): lax.dot_general(left, right, (((left_dim,), (right_dim,)), ((), ())), pre...  26 us
    gather x2, local copies, waits for them, and re-layouts, gather_by_doubling(): blocks = jnp.take(blocks, order, axis=axis)  15.7 us
    unnamed x31, local copies, waits for them, and re-layouts  13.1 us
    reshape x1, local copies, waits for them, and re-layouts, gather_by_doubling(): held.reshape(shape[:axis] + (n, shape[axis] // n) + shape[axis + 1:])  8.63 us
  transfers between devices with their start and end apart: 6, of which 5 were waited for; matrix products, arithmetic and copies ran while one was open for 13% of the time, Pallas kernels for 0%

profile of v2, /device:TPU:0, one launch (start us, length us, event | category | flops | bytes accessed | tf_op | source)
XLA Modules:
  0.0 352.4 jit_solution(3337772542994202299)
XLA Ops:
  7.2 6.6 %copy.24 = f32[256,6144]{0,1:T(8,128)} copy(f32[256,6144]{1,0:T(8,128)} %param.5) | data formatting | bytes 12582912 | tf_op args[1]
  14.1 3.2 pad_maximum_fusion
  17.3 8.6 %fusion.28 = f32[6656,512]{1,0:T(8,128)} fusion(f32[256,6656]{0,1:T(8,128)S(1)} %bitcast.55, f32[256,512]{1,0:T(8,128)S(1)} %copy-done), kind=kOutput, calls=%fused_computation.49 | convolution fusion | flops 5234491392 | bytes 20971520 | tf_op jit(solution)/shard_map/dot_general | solution.py:11
  26.0 144.8 %reduce-scatter.2.cloned.1.call-done = f32[416,512]{1,0:T(8,128)} async-done(((f32[6656,512]{1,0:T(8,128)}), f32[416,512]{1,0:T(8,128)}) %reduce-scatter.2.cloned.1.call-update) | async-done | bytes 851984 | tf_op jit(solution)/shard_map/reduce_scatter | solution.py:75
  170.8 0.8 reduce-precision_convert_fusion.3
  171.6 1.2 slice.33
  172.8 0.8 pad_maximum_fusion.4
  173.8 1.6 collective-permute-start
  175.4 32.6 %collective-permute-done = bf16[512,384]{0,1:T(8,128)(2,1)S(1)} collective-permute-done((bf16[512,384]{0,1:T(8,128)(2,1)S(1)}, bf16[512,384]{0,1:T(8,128)(2,1)S(1)}, u32[]{:S(2)}, u32[]{:S(2)}) %collective-permute-start) | collective-permute-done | bytes 393248 | tf_op jit(solution)/shard_map/ppermute | solution.py:39
  208.1 45.9 %collective-permute-done.1 = bf16[512,768]{0,1:T(8,128)(2,1)S(1)} collective-permute-done((bf16[512,768]{0,1:T(8,128)(2,1)S(1)}, bf16[512,768]{0,1:T(8,128)(2,1)S(1)}, u32[]{:S(2)}, u32[]{:S(2)}) %collective-permute-start.1) | collective-permute-done | bytes 786464 | tf_op jit(solution)/shard_map/ppermute | solution.py:39
  254.1 1.6 collective-permute-start.2
  255.7 23.5 %collective-permute-done.2 = bf16[512,1536]{0,1:T(8,128)(2,1)S(1)} collective-permute-done((bf16[512,1536]{0,1:T(8,128)(2,1)S(1)}, bf16[512,1536]{0,1:T(8,128)(2,1)S(1)}, u32[]{:S(2)}, u32[]{:S(2)}) %collective-permute-start.2) | collective-permute-done | bytes 1572896 | tf_op jit(solution)/shard_map/ppermute | solution.py:39
  279.2 1.8 pad_maximum_fusion.1
  283.1 0.8 constant_dynamic-update-slice_fusion.3
  284.0 1.0 constant_dynamic-update-slice_fusion.2
  285.0 1.3 constant_dynamic-update-slice_fusion.1
  287.0 3.9 %constant_dynamic-update-slice_fusion = bf16[512,6144]{0,1:T(8,128)(2,1)} fusion(bf16[512,6144]{0,1:T(8,128)(2,1)} %constant_dynamic-update-slice_fusion.1, bf16[512,3072]{0,1:T(8,128)(2,1)} %collective-permute-done.3), kind=kLoop, calls=%fused_computation.35 | loop fusion | bytes 6291456 | tf_op jit(solution)/shard_map/concatenate | solution.py:39
  290.8 8.6 %copy.23 = bf16[512,16,384]{2,0,1:T(8,128)(2,1)} copy(bf16[512,16,384]{0,2,1:T(8,128)(2,1)} %bitcast.1) | data formatting | bytes 12582912 | tf_op jit(solution)/shard_map/reshape | solution.py:44
  299.5 7.0 %gather_fusion = bf16[16,512,384]{2,1,0:T(8,128)(2,1)} fusion(bf16[512,16,384]{2,0,1:T(8,128)(2,1)} %copy.23, s32[1024]{0:T(1024)S(1)} %pad_clamp_fusion), kind=kCustom, calls=%fused_computation | custom fusion | bytes 12582976 | tf_op jit(solution)/shard_map/jit(_take)/gather | solution.py:45
  306.4 8.8 %copy.26 = bf16[512,16,384]{0,2,1:T(8,128)(2,1)} copy(bf16[512,16,384]{2,0,1:T(8,128)(2,1)} %bitcast.56) | data formatting | bytes 12582912 | tf_op jit(solution)/shard_map/jit(_take)/gather | solution.py:45
  315.2 4.5 %bitcast_select_fusion = bf16[512,6144]{0,1:T(8,128)(2,1)S(1)} fusion(bf16[512,16,384]{0,2,1:T(8,128)(2,1)} %copy.26, pred[6144]{0:T(1024)(128)(4,1)S(1)} %broadcast_in_dim.27), kind=kLoop, calls=%fused_computation.5 | loop fusion | flops 3145728 | bytes 12589056 | tf_op jit(solution)/shard_map/jit(_take)/select_n | solution.py:45
  319.7 2.7 fusion.23
  322.4 2.0 fusion.18
  324.5 2.5 convert_add_fusion
  327.0 3.6 %slice.26 = bf16[16,384,512]{2,1,0:T(8,128)(2,1)S(1)} slice(bf16[16,448,512]{2,1,0:T(8,128)(2,1)} %bitcast.63), slice={[0:16], [0:384], [0:512]} | slice | bytes 12582912 | tf_op jit(solution)/shard_map/slice | solution.py:84
  330.6 2.8 fusion.21
  333.4 3.6 %fusion.11 = f32[512,512]{1,0:T(8,128)S(1)} fusion(pred[16]{0:T(512)(128)(4,1)S(1)} %get-tuple-element.8, f32[512,512]{1,0:T(8,128)S(1)} %bitcast.65, f32[512]{0:T(512)S(1)} %convert_add_fusion.1, bf16[16,512,384]{2,1,0:T(8,128)(2,1)S(1)} %bitcast.58), kind=kOutput, calls=%fused_computation.14 | convolution fusion | flops 3225681920 | bytes 8390672 | tf_op jit(solution)/shard_map/dot_general | solution.py:11
  337.0 2.1 fusion.20
  339.1 1.9 fusion.16
  341.0 1.0 copy.30
  342.0 2.4 fusion.14
  344.4 1.1 copy.31
  (45 shorter events, 3.7 us)
Async XLA Ops:
  7.2 6.7 %copy-start = (f32[256,512]{1,0:T(8,128)S(1)}, f32[256,512]{1,0:T(8,128)}, u32[]{:S(2)}) copy-start(f32[256,512]{1,0:T(8,128)} %param.4) | copy-start | bytes 1572868
  7.2 163.6 %reduce-scatter.2.cloned.1.call-start = ((), (), s32[]{:S(2)}) async-start(), calls=%async_computation.1 | async-start | bytes 14483456 | tf_op jit(solution)/shard_map/reduce_scatter | solution.py:75
  25.9 147.7 %copy-start.3 = (bf16[512,384]{1,0:T(8,128)(2,1)S(1)}, bf16[512,384]{1,0:T(8,128)(2,1)}, u32[]{:S(2)}) copy-start(bf16[512,384]{1,0:T(8,128)(2,1)} %param.6) | copy-start | bytes 1179652
  25.9 298.5 %all-gather.3.cloned.1.call-start = ((), (), s32[]{:S(2)}) async-start(), calls=%async_computation.2 | async-start | bytes 7798784 | tf_op jit(solution)/shard_map/all_gather | solution.py:83
  173.6 107.4 %copy-start.4 = (s32[16]{0:T(128)S(1)}, s32[16]{0:T(128)}, u32[]{:S(2)}) copy-start(s32[16]{0:T(128)} %constant.38.clone) | copy-start | bytes 196
  173.8 34.1 %collective-permute-start = (bf16[512,384]{0,1:T(8,128)(2,1)S(1)}, bf16[512,384]{0,1:T(8,128)(2,1)S(1)}, u32[]{:S(2)}, u32[]{:S(2)}) collective-permute-start(bf16[512,384]{0,1:T(8,128)(2,1)S(1)} %copy.22), channel_id=1, source_target_pairs={{0,8},{1,9},{2,10},{3,11},{4,12},{5,13},{6,14},{7,15},{8,0},{9,1},... | collective-permute-start | bytes 1179656 | tf_op jit(solution)/shard_map/ppermute | solution.py:39
  208.0 46.0 %collective-permute-start.1 = (bf16[512,768]{0,1:T(8,128)(2,1)S(1)}, bf16[512,768]{0,1:T(8,128)(2,1)S(1)}, u32[]{:S(2)}, u32[]{:S(2)}) collective-permute-start(bf16[512,768]{0,1:T(8,128)(2,1)S(1)} %pad_maximum_fusion.3), channel_id=1, source_target_pairs={{0,4},{1,5},{2,6},{3,7},{4,0},{5,1},{6,2},{7,3},{8,12},{9,13},{10,... | collective-permute-start | bytes 2359304 | tf_op jit(solution)/shard_map/ppermute | solution.py:39
  254.1 25.1 %collective-permute-start.2 = (bf16[512,1536]{0,1:T(8,128)(2,1)S(1)}, bf16[512,1536]{0,1:T(8,128)(2,1)S(1)}, u32[]{:S(2)}, u32[]{:S(2)}) collective-permute-start(bf16[512,1536]{0,1:T(8,128)(2,1)S(1)} %pad_maximum_fusion.2), channel_id=1, source_target_pairs={{0,2},{1,3},{2,0},{3,1},{4,6},{5,7},{6,4},{7,5},{8,10},{9,11},{10,... | collective-permute-start | bytes 4718600 | tf_op jit(solution)/shard_map/ppermute | solution.py:39
  281.0 6.0 %collective-permute-start.3 = (bf16[512,3072]{0,1:T(8,128)(2,1)}, bf16[512,3072]{0,1:T(8,128)(2,1)}, u32[]{:S(2)}, u32[]{:S(2)}) collective-permute-start(bf16[512,3072]{0,1:T(8,128)(2,1)} %pad_maximum_fusion.1), channel_id=1, source_target_pairs={{0,1},{1,0},{2,3},{3,2},{4,5},{5,4},{6,7},{7,6},{8,9},{9,8},{10,11... | collective-permute-start | bytes 9437192 | tf_op jit(solution)/shard_map/ppermute | solution.py:39
  306.4 13.3 %slice-start = ((s8[6291456]{0:T(1024)(128)(4,1)}), s8[2097152]{0:T(1024)(128)(4,1)S(1)}, s32[]{:S(2)}) async-start(s8[6291456]{0:T(1024)(128)(4,1)} %bitcast.51), calls=%async_computation.3 | async-start | bytes 4194304
  315.2 4.5 %slice-start.1 = ((s8[6291456]{0:T(1024)(128)(4,1)}), s8[4194304]{0:T(1024)(128)(4,1)S(1)}, s32[]{:S(2)}) async-start(s8[6291456]{0:T(1024)(128)(4,1)} %bitcast.51), calls=%async_computation.4 | async-start | bytes 8388608
  324.5 6.1 %slice-start.2 = ((s8[6291456]{0:T(1024)(128)(4,1)}), s8[4194304]{0:T(1024)(128)(4,1)S(1)}, s32[]{:S(2)}) async-start(s8[6291456]{0:T(1024)(128)(4,1)} %bitcast.53), calls=%async_computation.5 | async-start | bytes 8388608
  327.0 3.6 %slice-start.3 = ((s8[6291456]{0:T(1024)(128)(4,1)}), s8[2097152]{0:T(1024)(128)(4,1)S(1)}, s32[]{:S(2)}) async-start(s8[6291456]{0:T(1024)(128)(4,1)} %bitcast.53), calls=%async_computation.6 | async-start | bytes 4194304
  327.0 6.4 %slice-start.4 = ((s8[6291456]{0:T(1024)(128)(4,1)}), s8[4194304]{0:T(1024)(128)(4,1)S(1)}, s32[]{:S(2)}) async-start(s8[6291456]{0:T(1024)(128)(4,1)} %bitcast.57), calls=%async_computation.7 | async-start | bytes 8388608
  330.6 2.8 slice-start.5
  330.6 2.8 copy-start.2
  337.0 2.1 copy-start.1
Sparse Core Ops, SparseCore 0:
  26.0 144.6 reduce-scatter.1
  173.9 83.7 all-gather.2

commit v3 on v2

--- a/solution.py
+++ b/solution.py
@@ -62,7 +62,7 @@
     nested = jnp.minimum(weights[:, None], weights[None, :])
     gram_scale = 0.5 / total_rows
 
-    heads_all = gather_by_doubling(heads, "rows", 1)
+    heads_all = lax.all_gather(heads, "rows", axis=1, tiled=True)
 
     left = jnp.concatenate(
         [
@@ -72,6 +72,7 @@
         axis=2,
     ).reshape(rows_here, devices * (f_here + d_here))
     partial = contract(left, student, 0, 0, lax.Precision.HIGH)
+    heads_all, partial = lax.optimization_barrier((heads_all, partial))
     reduced = lax.psum_scatter(partial, "rows", scatter_dimension=0, tiled=True)
     cross_here = reduced[:f_here]
     moment_here = reduced[f_here:]

time: 359 us -> 324 us (0.903); the launches traced: 352 us -> 324 us
  local copies, waits for them, and re-layouts: 46.7 us -> 15 us
  matrix products: 26 us -> 34.3 us
  other arithmetic: 14.4 us -> 6.4 us
  waiting for transfers between devices: 248 us -> 253 us
    ppermute x4 -> x0, waiting for transfers between devices: 103 us -> none  [gather_by_doubling(): lax.ppermute(held, axis_name, pairs)]
    all_gather x1, waiting for transfers between devices: 0.02 us -> 56.8 us  [per_device(): gathered = lax.all_gather(packed, 'rows', axis=0, tiled=False)]
    all_gather x0 -> x1, waiting for transfers between devices: none -> 52 us  [per_device(): heads_all = lax.all_gather(heads, 'rows', axis=1, tiled=True)]
    gather x2 -> x0, local copies, waits for them, and re-layouts: 15.7 us -> none  [gather_by_doubling(): blocks = jnp.take(blocks, order, axis=axis)]
    reshape x1 -> x0, local copies, waits for them, and re-layouts: 8.63 us -> none  [gather_by_doubling(): held.reshape(shape[:axis] + (n, shape[axis] // n) + shape[axis + 1:])]
    dot_general x8, matrix products: 26 us -> 34.3 us  [contract(): lax.dot_general(left, right, (((left_dim,), (right_dim,)), ((), ())), pre...]
    select_n x1 -> x0, other arithmetic: 4.47 us -> none  [gather_by_doubling(): blocks = jnp.take(blocks, order, axis=axis)]
    concatenate x1 -> x0, local copies, waits for them, and re-layouts: 3.87 us -> none  [gather_by_doubling(): jnp.concatenate([held, lax.ppermute(held, axis_name, pairs)], axis=axis)]
  transfers between devices with their start and end apart: 6 -> 3, of which waited for: 5 -> 3; matrix products, arithmetic and copies ran while one was open for 13% -> 9% of each run, Pallas kernels for 0% -> 0%
where the time goes in v3:
time: 324 us
  waiting for transfers between devices  253 us (78%)
  matrix products  34.3 us (11%)
  local copies, waits for them, and re-layouts  15 us (5%)
  between operations  14 us (4%)
  other arithmetic  6.4 us (2%)
    reduce_scatter x1, waiting for transfers between devices, per_device(): reduced = lax.psum_scatter(partial, 'rows', scatter_dimension=0, tiled=True)  144 us
    all_gather x1, waiting for transfers between devices, per_device(): gathered = lax.all_gather(packed, 'rows', axis=0, tiled=False)  56.8 us
    all_gather x1, waiting for transfers between devices, per_device(): heads_all = lax.all_gather(heads, 'rows', axis=1, tiled=True)  52 us
    dot_general x8, matrix products, contract(): lax.dot_general(left, right, (((left_dim,), (right_dim,)), ((), ())), pre...  34.3 us
    unnamed x24, local copies, waits for them, and re-layouts  10.4 us
  transfers between devices with their start and end apart: 3, of which 3 were waited for; matrix products, arithmetic and copies ran while one was open for 9% of the time, Pallas kernels for 0%

profile of v3, /device:TPU:0, one launch (start us, length us, event | category | flops | bytes accessed | tf_op | source)
XLA Modules:
  0.0 323.5 jit_solution(11316943391770196176)
XLA Ops:
  7.2 0.0 all-gather.4.cloned.1.call-start
  7.2 0.7 all-gather.4.cloned.1.call-update
  7.9 0.0 reduce-scatter.2.cloned.1.call-start
  8.0 6.6 %copy.10 = f32[256,6144]{0,1:T(8,128)} copy(f32[256,6144]{1,0:T(8,128)} %param.4) | data formatting | bytes 12582912 | tf_op args[1]
  14.6 0.2 copy.11
  14.8 3.2 pad_maximum_fusion
  18.0 8.6 %fusion.14 = f32[6656,512]{1,0:T(8,128)} fusion(f32[256,6656]{0,1:T(8,128)S(1)} %bitcast.42, f32[256,512]{1,0:T(8,128)S(1)} %copy-done.1), kind=kOutput, calls=%fused_computation.29 | convolution fusion | flops 5234491392 | bytes 20971520 | tf_op jit(solution)/shard_map/dot_general | solution.py:11
  26.6 52.0 %all-gather.4.cloned.1.call-done = bf16[512,6144]{1,0:T(8,128)(2,1)} async-done(((bf16[512,384]{1,0:T(8,128)(2,1)}), bf16[512,6144]{1,0:T(8,128)(2,1)}) %all-gather.4.cloned.1.call-update) | async-done | bytes 6291472 | tf_op jit(solution)/shard_map/all_gather | solution.py:65
  78.6 0.0 reduce-scatter.2.cloned.1.call-update
  78.6 0.2 all-gather.6.cloned.1.call-start
  78.8 144.0 %reduce-scatter.2.cloned.1.call-done = f32[416,512]{1,0:T(8,128)} async-done(((f32[6656,512]{1,0:T(8,128)}), f32[416,512]{1,0:T(8,128)}) %reduce-scatter.2.cloned.1.call-update) | async-done | bytes 851984 | tf_op jit(solution)/shard_map/reduce_scatter | solution.py:76
  222.8 0.8 reduce-precision_convert_fusion.3
  223.7 1.2 slice.31
  224.9 0.0 slice-start
  224.9 0.8 pad_maximum_fusion.1
  225.7 0.0 all-gather.6.cloned.1.call-update
  225.7 0.0 slice-start.1
  225.7 6.6 %fusion.11 = f32[256,512]{0,1:T(8,128)S(1)} fusion(bf16[512,6144]{1,0:T(8,128)(2,1)} %all-gather.4.cloned.1.call-done, f32[256,6144]{1,0:T(8,128)} %param.4), kind=kOutput, calls=%fused_computation.19 | convolution fusion | flops 1615331328 | bytes 13107200 | tf_op jit(solution)/shard_map/dot_general | solution.py:11
  232.4 1.4 copy-done
  233.8 2.7 fusion.6
  236.5 56.8 %all-gather.6.cloned.1.call-done = bf16[7168,512]{1,0:T(8,128)(2,1)} async-done(((bf16[448,512]{1,0:T(8,128)(2,1)}), bf16[7168,512]{1,0:T(8,128)(2,1)}) %all-gather.6.cloned.1.call-update) | async-done | bytes 7340048 | tf_op jit(solution)/shard_map/all_gather | solution.py:84
  293.3 3.4 %slice.24 = bf16[16,384,512]{2,1,0:T(8,128)(2,1)S(1)} slice(bf16[16,448,512]{2,1,0:T(8,128)(2,1)} %bitcast.46), slice={[0:16], [0:384], [0:512]} | slice | bytes 12582912 | tf_op jit(solution)/shard_map/slice | solution.py:85
  296.7 0.0 slice-start.2
  296.8 1.5 convert_add_fusion
  298.3 0.0 slice-start.3
  298.3 6.6 %fusion.9 = f32[256,512]{0,1:T(8,128)S(1)} fusion(bf16[6144,512]{1,0:T(8,128)(2,1)S(1)} %bitcast.43, f32[256,6144]{1,0:T(8,128)} %param.4), kind=kOutput, calls=%fused_computation.18 | convolution fusion | flops 1615331328 | bytes 13107200 | tf_op jit(solution)/shard_map/dot_general | solution.py:11
  305.0 1.8 fusion.8
  306.9 3.5 %fusion.1 = f32[512,512]{1,0:T(8,128)S(1)} fusion(bf16[512,6144]{1,0:T(8,128)(2,1)S(1)} %bitcast.49, f32[512,512]{1,0:T(8,128)S(1)} %bitcast.50, f32[512]{0:T(512)S(1)} %convert_add_fusion.1), kind=kOutput, calls=%fused_computation.5 | convolution fusion | flops 3222536192 | bytes 8390656 | tf_op jit(solution)/shard_map/dot_general | solution.py:11
  310.3 2.0 fusion.4
  312.4 1.0 copy.15
  313.4 2.4 fusion.2
  315.8 1.1 copy.16
  (20 shorter events, 0.0 us)
Async XLA Ops:
  7.2 71.4 %all-gather.4.cloned.1.call-start = ((), (), s32[]{:S(2)}) async-start(), calls=%async_computation.1 | async-start | bytes 6684672 | tf_op jit(solution)/shard_map/all_gather | solution.py:65
  7.9 6.7 %copy-start.1 = (f32[256,512]{1,0:T(8,128)S(1)}, f32[256,512]{1,0:T(8,128)}, u32[]{:S(2)}) copy-start(f32[256,512]{1,0:T(8,128)} %param.3) | copy-start | bytes 1572868
  7.9 214.9 %reduce-scatter.2.cloned.1.call-start = ((), (), s32[]{:S(2)}) async-start(), calls=%async_computation.2 | async-start | bytes 14483456 | tf_op jit(solution)/shard_map/reduce_scatter | solution.py:76
  78.6 214.7 %all-gather.6.cloned.1.call-start = ((), (), s32[]{:S(2)}) async-start(), calls=%async_computation.3 | async-start | bytes 7798784 | tf_op jit(solution)/shard_map/all_gather | solution.py:84
  224.9 7.5 %slice-start = ((s8[6291456]{0:T(1024)(128)(4,1)}), s8[2097152]{0:T(1024)(128)(4,1)S(1)}, s32[]{:S(2)}) async-start(s8[6291456]{0:T(1024)(128)(4,1)} %bitcast.38), calls=%async_computation.4 | async-start | bytes 4194304
  225.7 6.6 %slice-start.1 = ((s8[6291456]{0:T(1024)(128)(4,1)}), s8[4194304]{0:T(1024)(128)(4,1)S(1)}, s32[]{:S(2)}) async-start(s8[6291456]{0:T(1024)(128)(4,1)} %bitcast.38), calls=%async_computation.5 | async-start | bytes 8388608
  225.7 8.0 %copy-start = (bf16[512,6144]{1,0:T(8,128)(2,1)S(1)}, bf16[512,6144]{1,0:T(8,128)(2,1)}, u32[]{:S(2)}) copy-start(bf16[512,6144]{1,0:T(8,128)(2,1)} %all-gather.4.cloned.1.call-done) | copy-start | bytes 18874372
  296.7 8.2 %slice-start.2 = ((s8[6291456]{0:T(1024)(128)(4,1)}), s8[4194304]{0:T(1024)(128)(4,1)S(1)}, s32[]{:S(2)}) async-start(s8[6291456]{0:T(1024)(128)(4,1)} %bitcast.40), calls=%async_computation.6 | async-start | bytes 8388608
  296.7 10.1 %slice-start.4 = ((s8[6291456]{0:T(1024)(128)(4,1)}), s8[4194304]{0:T(1024)(128)(4,1)S(1)}, s32[]{:S(2)}) async-start(s8[6291456]{0:T(1024)(128)(4,1)} %bitcast.48), calls=%async_computation.8 | async-start | bytes 8388608
  298.3 8.5 %copy-start.2 = (f32[16,32,512]{2,1,0:T(8,128)}, f32[16,32,512]{2,1,0:T(8,128)S(1)}, u32[]{:S(2)}) copy-start(f32[16,32,512]{2,1,0:T(8,128)S(1)} %convert_add_fusion) | copy-start | bytes 3145732
  298.3 6.7 %slice-start.3 = ((s8[6291456]{0:T(1024)(128)(4,1)}), s8[2097152]{0:T(1024)(128)(4,1)S(1)}, s32[]{:S(2)}) async-start(s8[6291456]{0:T(1024)(128)(4,1)} %bitcast.40), calls=%async_computation.7 | async-start | bytes 4194304
  298.3 8.5 %slice-start.5 = ((s8[6291456]{0:T(1024)(128)(4,1)}), s8[2097152]{0:T(1024)(128)(4,1)S(1)}, s32[]{:S(2)}) async-start(s8[6291456]{0:T(1024)(128)(4,1)} %bitcast.48), calls=%async_computation.9 | async-start | bytes 4194304
  306.8 3.5 %copy-start.3 = (f32[256,512]{0,1:T(8,128)S(1)}, f32[256,512]{0,1:T(8,128)}, u32[]{:S(2)}) copy-start(f32[256,512]{0,1:T(8,128)} %fusion.6) | copy-start | bytes 1572868
Sparse Core Ops, SparseCore 0:
  10.2 68.3 all-gather.3
  82.7 140.1 reduce-scatter.1
  225.9 67.3 all-gather.5

commit v4 on v3

--- a/solution.py
+++ b/solution.py
@@ -47,7 +47,9 @@
 
 
 def per_device(student, teacher, heads):
-    devices = lax.axis_size("rows")
+    chips = lax.axis_size("chips")
+    cores = lax.axis_size("core")
+    devices = chips * cores
     rows_here, model_width = student.shape
     teacher_width = teacher.shape[1]
     total_rows = rows_here * devices
@@ -62,18 +64,22 @@
     nested = jnp.minimum(weights[:, None], weights[None, :])
     gram_scale = 0.5 / total_rows
 
-    heads_all = lax.all_gather(heads, "rows", axis=1, tiled=True)
+    def core_major(x, width):
+        return x.reshape(rows_here, chips, cores, width).transpose(0, 2, 1, 3)
+
+    teacher_cm = core_major(teacher, f_here)
+
+    heads_chips = lax.all_gather(heads, "chips", axis=0, tiled=False)
+    heads_all = lax.all_gather(heads_chips, "core", axis=0, tiled=False)
+    heads_all = heads_all.transpose(2, 0, 1, 3).reshape(model_width, teacher_width)
 
     left = jnp.concatenate(
-        [
-            teacher.reshape(rows_here, devices, f_here),
-            student.reshape(rows_here, devices, d_here),
-        ],
-        axis=2,
+        [teacher_cm, core_major(student, d_here)], axis=3
     ).reshape(rows_here, devices * (f_here + d_here))
     partial = contract(left, student, 0, 0, lax.Precision.HIGH)
     heads_all, partial = lax.optimization_barrier((heads_all, partial))
-    reduced = lax.psum_scatter(partial, "rows", scatter_dimension=0, tiled=True)
+    reduced = lax.psum_scatter(partial, "core", scatter_dimension=0, tiled=True)
+    reduced = lax.psum_scatter(reduced, "chips", scatter_dimension=0, tiled=True)
     cross_here = reduced[:f_here]
     moment_here = reduced[f_here:]
 
@@ -81,19 +87,21 @@
     packed = jnp.concatenate(
         [cross_here.astype(jnp.bfloat16), moment_high, moment_low], axis=0
     )
-    gathered = lax.all_gather(packed, "rows", axis=0, tiled=False)
-    cross_low = gathered[:, :f_here].reshape(teacher_width, model_width)
+    gathered = lax.all_gather(packed, "chips", axis=0, tiled=False)
+    gathered = lax.all_gather(gathered, "core", axis=0, tiled=False)
+    cross_low = gathered[:, :, :f_here].reshape(teacher_width, model_width)
     moment = (
-        gathered[:, f_here : f_here + d_here].astype(jnp.float32)
-        + gathered[:, f_here + d_here :].astype(jnp.float32)
-    ).reshape(model_width, model_width)
+        gathered[:, :, f_here : f_here + d_here].astype(jnp.float32)
+        + gathered[:, :, f_here + d_here :].astype(jnp.float32)
+    )
+    moment = moment.transpose(1, 0, 2, 3).reshape(model_width, model_width)
 
     grad_heads = head_scale * (
         contract(moment, heads.astype(jnp.float32), 1, 0) - cross_here.T
     )
 
     gram_heads = contract(heads_all, heads_all, 1, 1, lax.Precision.DEFAULT)
-    teacher_high, teacher_low = split_bf16(teacher)
+    teacher_high, teacher_low = split_bf16(teacher_cm.reshape(rows_here, teacher_width))
     teacher_heads = contract(teacher_high, heads_all, 1, 1, lax.Precision.DEFAULT) + contract(
         teacher_low, heads_all, 1, 1, lax.Precision.DEFAULT
     )
@@ -110,8 +118,14 @@
 
 
 def solution(mesh):
-    in_specs = (P(("groups", "rows"), None), P(("groups", "rows"), None), P(None, "rows"))
-    out_specs = (P(("groups", "rows"), None), P("groups", "rows"))
+    groups, devices = mesh.devices.shape
+    cores = 2 if devices % 2 == 0 else 1
+    chip_mesh = jax.sharding.Mesh(
+        mesh.devices.reshape(groups, devices // cores, cores), ("groups", "chips", "core")
+    )
+    rows = ("groups", "chips", "core")
+    in_specs = (P(rows, None), P(rows, None), P(None, ("chips", "core")))
+    out_specs = (P(rows, None), P("groups", ("chips", "core")))
     return jax.shard_map(
-        per_device, mesh=mesh, in_specs=in_specs, out_specs=out_specs, check_vma=False
+        per_device, mesh=chip_mesh, in_specs=in_specs, out_specs=out_specs, check_vma=False
     )

time: 324 us -> 392 us (1.21)
  waiting for transfers between devices: 253 us -> 286 us
  local copies, waits for them, and re-layouts: 15 us -> 40.3 us
  other arithmetic: 6.4 us -> 17.1 us
    all_gather x2 -> x4, waiting for transfers between devices: 109 us -> 134 us  [the longest x1 65.8 us: per_device(): gathered = lax.all_gather(packed, 'chips', axis=0, tiled=False)]
    all_gather x0 -> x2, local copies, waits for them, and re-layouts: none -> 20.5 us  [the longest x1 11.9 us: per_device(): gathered = lax.all_gather(gathered, 'core', axis=0, tiled=False)]
    reduce_scatter x1 -> x2, waiting for transfers between devices: 144 us -> 151 us  [the longest x1 130 us: per_device(): lax.psum_scatter(reduced, 'chips', scatter_dimension=0, tiled=True)]
    transpose x0 -> x2, local copies, waits for them, and re-layouts: none -> 6.38 us  [the longest x1 3.57 us: core_major(): return x.reshape(rows_here, chips, cores, width).transpose(0, 2, 1, 3)]
    transpose x0 -> x1, other arithmetic: none -> 5.19 us  [per_device(): moment = moment.transpose(1, 0, 2, 3).reshape(model_width, model_width)]
    convert_element_type x0 -> x1, other arithmetic: none -> 4.6 us  [split_bf16(): low = (x - high).astype(jnp.bfloat16)]
    unnamed x24 -> x20, local copies, waits for them, and re-layouts: 10.4 us -> 11.5 us
  transfers between devices with their start and end apart: 3 -> 6, of which waited for: 3 -> 5; matrix products, arithmetic and copies ran while one was open for 9% -> 9% of each run, Pallas kernels for 0% -> 0%
where the time goes in v4:
time: 392 us; the launch traced here: 391 us
  waiting for transfers between devices  286 us (73%)
  local copies, waits for them, and re-layouts  40.3 us (10%)
  matrix products  33.4 us (9%)
  other arithmetic  17.1 us (4%)
  between operations  14.3 us (4%)
    reduce_scatter x1, waiting for transfers between devices, per_device(): lax.psum_scatter(reduced, 'chips', scatter_dimension=0, tiled=True)  130 us
    all_gather x1, waiting for transfers between devices, per_device(): gathered = lax.all_gather(packed, 'chips', axis=0, tiled=False)  65.8 us
    all_gather x1, waiting for transfers between devices, per_device(): heads_chips = lax.all_gather(heads, 'chips', axis=0, tiled=False)  65.4 us
    dot_general x8, matrix products, contract(): lax.dot_general(left, right, (((left_dim,), (right_dim,)), ((), ())), pre...  33.4 us
    reduce_scatter x1, waiting for transfers between devices, per_device(): reduced = lax.psum_scatter(partial, 'core', scatter_dimension=0, tiled=True)  21.3 us
    all_gather x1, local copies, waits for them, and re-layouts, per_device(): gathered = lax.all_gather(gathered, 'core', axis=0, tiled=False)  11.9 us
    unnamed x20, local copies, waits for them, and re-layouts  11.5 us
    all_gather x1, local copies, waits for them, and re-layouts, per_device(): heads_all = lax.all_gather(heads_chips, 'core', axis=0, tiled=False)  8.62 us
  transfers between devices with their start and end apart: 6, of which 5 were waited for; matrix products, arithmetic and copies ran while one was open for 9% of the time, Pallas kernels for 0%

profile of v4, /device:TPU:0, one launch (start us, length us, event | category | flops | bytes accessed | tf_op | source)
XLA Modules:
  0.0 391.3 jit_solution(10173492894685906591)
XLA Ops:
  7.2 0.7 all-gather.9.cloned.1.call-update
  7.9 65.4 %all-gather.9.cloned.1.call-done = bf16[4096,384]{1,0:T(8,128)(2,1)} async-done(((bf16[512,384]{1,0:T(8,128)(2,1)}), bf16[4096,384]{1,0:T(8,128)(2,1)}) %all-gather.9.cloned.1.call-update) | async-done | bytes 3145744 | tf_op jit(solution)/shard_map/all_gather | solution.py:72
  73.4 6.6 %copy.43 = f32[256,6144]{0,1:T(8,128)} copy(f32[256,6144]{1,0:T(8,128)} %param.4) | data formatting | bytes 12582912 | tf_op args[1]
  80.3 4.3 %pad_maximum_fusion = f32[256,2,8,416]{0,3,1,2:T(8,128)S(1)} fusion(f32[256,2,8,32]{0,3,1,2:T(8,128)S(1)} %bitcast.77, f32[256,2,8,384]{0,3,1,2:T(8,128)} %bitcast.59), kind=kLoop, calls=%fused_computation.4 | loop fusion | flops 1703936 | bytes 13631488 | tf_op jit(solution)/shard_map/concatenate | solution.py:76
  84.6 0.7 copy.45
  85.3 8.6 %fusion.35 = f32[6656,512]{1,0:T(8,128)} fusion(f32[256,6656]{0,1:T(8,128)S(1)} %bitcast.69, f32[256,512]{1,0:T(8,128)S(1)} %copy-done.1), kind=kOutput, calls=%fused_computation.37 | convolution fusion | flops 5234491392 | bytes 20971520 | tf_op jit(solution)/shard_map/dot_general | solution.py:11
  93.9 8.6 %copy.42 = bf16[16,512,384]{1,2,0:T(8,128)(2,1)} copy(bf16[16,512,384]{2,1,0:T(8,128)(2,1)} %all-gather.11.cloned.1.call-done) | data formatting | bytes 12582912 | tf_op jit(solution)/shard_map/all_gather | solution.py:73
  102.5 21.3 %reduce-scatter.3.cloned.1.call-done = f32[3328,512]{1,0:T(8,128)} async-done(((f32[6656,512]{1,0:T(8,128)}), f32[3328,512]{1,0:T(8,128)}) %reduce-scatter.3.cloned.1.call-update) | async-done | bytes 6815760 | tf_op jit(solution)/shard_map/reduce_scatter | solution.py:81
  123.9 130.0 %reduce-scatter.5.cloned.1.call-done = f32[416,512]{1,0:T(8,128)} async-done(((f32[3328,512]{1,0:T(8,128)}), f32[416,512]{1,0:T(8,128)}) %reduce-scatter.5.cloned.1.call-update) | async-done | bytes 851984 | tf_op jit(solution)/shard_map/reduce_scatter | solution.py:82
  253.9 0.8 reduce-precision_convert_fusion.2
  254.8 1.2 slice.43
  256.0 0.8 pad_maximum_fusion.1
  257.0 65.8 %all-gather.13.cloned.1.call-done = bf16[3584,512]{1,0:T(8,128)(2,1)} async-done(((bf16[448,512]{1,0:T(8,128)(2,1)}), bf16[3584,512]{1,0:T(8,128)(2,1)}) %all-gather.13.cloned.1.call-update) | async-done | bytes 3670032 | tf_op jit(solution)/shard_map/all_gather | solution.py:90
  322.8 3.6 copy.48
  326.5 1.0 slice-done.1
  327.5 4.6 %fusion.1 = (bf16[256,2,8,384]{0,3,1,2:T(8,128)(2,1)}, bf16[256,2,8,384]{0,3,1,2:T(8,128)(2,1)}) fusion(f32[256,2,8,384]{0,3,1,2:T(8,128)S(1)} %bitcast.63), kind=kLoop, calls=%fused_computation.6 | loop fusion | flops 6291456 | bytes 12582912 | tf_op jit(solution)/shard_map/convert_element_type | solution.py:22
  332.1 1.4 reduce-precision_convert_fusion.1
  333.4 0.6 slice-done.3
  334.0 2.5 fusion.36
  336.6 1.8 fusion.33
  338.4 2.6 all-gather.15.cloned.1.call-done
  341.0 11.9 %copy.46 = bf16[16,448,512]{1,2,0:T(8,128)(2,1)} copy(bf16[16,448,512]{2,1,0:T(8,128)(2,1)} %all-gather.15.cloned.1.call-done) | data formatting | bytes 14680064 | tf_op jit(solution)/shard_map/all_gather | solution.py:91
  352.9 5.2 %add_bitcast_fusion = f32[8,2,32,512]{2,3,0,1:T(8,128)} fusion(bf16[2,8,448,512]{2,3,1,0:T(8,128)(2,1)} %bitcast.70), kind=kLoop, calls=%fused_computation.11 | loop fusion | flops 786432 | bytes 2097152 | tf_op jit(solution)/shard_map/transpose | solution.py:97
  358.1 0.9 copy-done
  359.0 3.7 fusion.10
  362.7 2.8 copy.47
  365.5 8.4 %fusion.8 = f32[512,512]{1,0:T(8,128)S(1)} fusion(bf16[512,6144]{0,1:T(8,128)(2,1)} %bitcast.64, f32[512,512]{1,0:T(8,128)S(1)} %bitcast.73, f32[512]{0:T(512)S(1)} %convert_add_fusion), kind=kOutput, calls=%fused_computation.15 | convolution fusion | flops 3222536192 | bytes 8390656 | tf_op jit(solution)/shard_map/dot_general | solution.py:11
  373.9 4.7 %fusion.27 = f32[256,512]{0,1:T(8,128)S(1)} fusion(f32[256,512]{0,1:T(8,128)S(1)} %fusion.10, bf16[256,2,8,384]{0,3,1,2:T(8,128)(2,1)S(1)} %copy-done.2, bf16[2,8,448,512]{2,3,1,0:T(8,128)(2,1)} %bitcast.71, f32[512]{0:T(512)S(1)} %broadcast_multiply_fusion), kind=kOutput, calls=%fused_computation.25 | convolution fusion | flops 1610874880 | bytes 10487808 | tf_op jit(solution)/shard_map/dot_general | solution.py:11
  378.6 1.9 fusion.21
  380.4 1.0 copy.55
  381.4 1.9 fusion.9
  383.3 1.1 copy.56
  (30 shorter events, 0.7 us)
Async XLA Ops:
  7.2 66.2 %all-gather.9.cloned.1.call-start = ((), (), s32[]{:S(2)}) async-start(), calls=%async_computation.4 | async-start | bytes 3538944 | tf_op jit(solution)/shard_map/all_gather | solution.py:72
  7.9 86.0 %all-gather.11.cloned.1.call-start = ((), (), s32[]{:S(2)}) async-start(), calls=%async_computation.5 | async-start | bytes 9437184 | tf_op jit(solution)/shard_map/all_gather | solution.py:73
  73.4 6.7 %copy-start.1 = (f32[256,512]{1,0:T(8,128)S(1)}, f32[256,512]{1,0:T(8,128)}, u32[]{:S(2)}) copy-start(f32[256,512]{1,0:T(8,128)} %param.3) | copy-start | bytes 1572868
  73.4 50.5 %reduce-scatter.3.cloned.1.call-start = ((), (), s32[]{:S(2)}) async-start(), calls=%async_computation.2 | async-start | bytes 20447232 | tf_op jit(solution)/shard_map/reduce_scatter | solution.py:81
  102.5 151.4 %reduce-scatter.5.cloned.1.call-start = ((), (), s32[]{:S(2)}) async-start(), calls=%async_computation.3 | async-start | bytes 7667712 | tf_op jit(solution)/shard_map/reduce_scatter | solution.py:82
  123.9 198.9 %all-gather.13.cloned.1.call-start = ((), (), s32[]{:S(2)}) async-start(), calls=%async_computation.6 | async-start | bytes 4128768 | tf_op jit(solution)/shard_map/all_gather | solution.py:90
  256.8 84.2 %all-gather.15.cloned.1.call-start = ((), (), s32[]{:S(2)}) async-start(), calls=%async_computation.7 | async-start | bytes 11010048 | tf_op jit(solution)/shard_map/all_gather | solution.py:91
  322.8 3.6 slice-start
  322.8 4.6 %slice-start.1 = ((s8[6291456]{0:T(1024)(128)(4,1)}), s8[4194304]{0:T(1024)(128)(4,1)S(1)}, s32[]{:S(2)}) async-start(s8[6291456]{0:T(1024)(128)(4,1)} %bitcast.61), calls=%async_computation.9 | async-start | bytes 8388608
  327.5 6.0 %slice-start.2 = ((s8[6291456]{0:T(1024)(128)(4,1)}), s8[4194304]{0:T(1024)(128)(4,1)S(1)}, s32[]{:S(2)}) async-start(s8[6291456]{0:T(1024)(128)(4,1)} %bitcast.65), calls=%async_computation.10 | async-start | bytes 8388608
  332.1 2.0 slice-start.3
  352.9 6.1 %copy-start = (bf16[16,448,512]{1,2,0:T(8,128)(2,1)S(1)}, bf16[16,448,512]{1,2,0:T(8,128)(2,1)}, u32[]{:S(2)}) copy-start(bf16[16,448,512]{1,2,0:T(8,128)(2,1)} %copy.46) | copy-start | bytes 22020100
  365.5 8.4 %copy-start.2 = (bf16[256,2,8,384]{0,3,1,2:T(8,128)(2,1)S(1)}, bf16[256,2,8,384]{0,3,1,2:T(8,128)(2,1)}, u32[]{:S(2)}) copy-start(bf16[256,2,8,384]{0,3,1,2:T(8,128)(2,1)} %get-tuple-element.16) | copy-start | bytes 9437188
  373.9 7.6 %copy-start.3 = (f32[416,512]{1,0:T(8,128)S(1)}, f32[416,512]{1,0:T(8,128)}, u32[]{:S(2)}) copy-start(f32[416,512]{1,0:T(8,128)} %reduce-scatter.5.cloned.1.call-done) | copy-start | bytes 2555908
Sparse Core Ops, SparseCore 0:
  10.2 63.1 all-gather.8
  74.9 15.3 all-gather.10
  102.6 21.1 reduce-scatter.2
  127.4 126.5 reduce-scatter.4
  256.9 65.8 all-gather.12
  324.2 16.7 all-gather.14

commit v5 on v2

--- a/solution.py
+++ b/solution.py
@@ -62,7 +62,10 @@
     nested = jnp.minimum(weights[:, None], weights[None, :])
     gram_scale = 0.5 / total_rows
 
-    heads_all = gather_by_doubling(heads, "rows", 1)
+    group = lax.axis_index("groups")
+    half = heads.shape[1] // 2
+    mine = lax.dynamic_slice_in_dim(heads, group * half, half, axis=1)
+    mine = lax.all_gather(mine, "rows", axis=0, tiled=False)
 
     left = jnp.concatenate(
         [
@@ -72,6 +75,13 @@
         axis=2,
     ).reshape(rows_here, devices * (f_here + d_here))
     partial = contract(left, student, 0, 0, lax.Precision.HIGH)
+    mine, partial = lax.optimization_barrier((mine, partial))
+    theirs = lax.ppermute(mine, "groups", [(0, 1), (1, 0)])
+    first = group == 0
+    heads_all = jnp.stack(
+        [jnp.where(first, mine, theirs), jnp.where(first, theirs, mine)], axis=1
+    )
+    heads_all = heads_all.transpose(2, 0, 1, 3).reshape(model_width, teacher_width)
     reduced = lax.psum_scatter(partial, "rows", scatter_dimension=0, tiled=True)
     cross_here = reduced[:f_here]
     moment_here = reduced[f_here:]

time: 359 us -> 328 us (0.914); the launches traced: 352 us -> 327 us
  local copies, waits for them, and re-layouts: 46.7 us -> 25.3 us
    all_gather x0 -> x1, waiting for transfers between devices: none -> 36.2 us  [per_device(): mine = lax.all_gather(mine, 'rows', axis=0, tiled=False)]
    ppermute x4 -> x1, waiting for transfers between devices: 103 us -> 67.8 us  [per_device(): theirs = lax.ppermute(mine, 'groups', [(0, 1), (1, 0)])]
    gather x2 -> x0, local copies, waits for them, and re-layouts: 15.7 us -> none  [gather_by_doubling(): blocks = jnp.take(blocks, order, axis=axis)]
    another operation x0 -> x2, other arithmetic: none -> 10.9 us  [per_device(): jnp.stack([jnp.where(first, mine, theirs), jnp.where(first, theirs, mine)...]
    reshape x1 -> x0, local copies, waits for them, and re-layouts: 8.63 us -> none  [gather_by_doubling(): held.reshape(shape[:axis] + (n, shape[axis] // n) + shape[axis + 1:])]
    all_gather x0 -> x1, local copies, waits for them, and re-layouts: none -> 6.1 us  [per_device(): mine = lax.all_gather(mine, 'rows', axis=0, tiled=False)]
    select_n x1 -> x0, other arithmetic: 4.47 us -> none  [gather_by_doubling(): blocks = jnp.take(blocks, order, axis=axis)]
    reduce_scatter x1, waiting for transfers between devices: 145 us -> 140 us  [per_device(): reduced = lax.psum_scatter(partial, 'rows', scatter_dimension=0, tiled=True)]
  transfers between devices with their start and end apart: 6 -> 4, of which waited for: 5 -> 3; matrix products, arithmetic and copies ran while one was open for 13% -> 12% of each run, Pallas kernels for 0% -> 0%
where the time goes in v5:
time: 328 us; the launch traced here: 327 us
  waiting for transfers between devices  245 us (75%)
  local copies, waits for them, and re-layouts  25.3 us (8%)
  matrix products  24.2 us (7%)
  other arithmetic  17.3 us (5%)
  between operations  14 us (4%)
    reduce_scatter x1, waiting for transfers between devices, per_device(): reduced = lax.psum_scatter(partial, 'rows', scatter_dimension=0, tiled=True)  140 us
    ppermute x1, waiting for transfers between devices, per_device(): theirs = lax.ppermute(mine, 'groups', [(0, 1), (1, 0)])  67.8 us
    all_gather x1, waiting for transfers between devices, per_device(): mine = lax.all_gather(mine, 'rows', axis=0, tiled=False)  36.2 us
    dot_general x8, matrix products, contract(): lax.dot_general(left, right, (((left_dim,), (right_dim,)), ((), ())), pre...  24.2 us
    another operation x2, other arithmetic, per_device(): jnp.stack([jnp.where(first, mine, theirs), jnp.where(first, theirs, mine)...  10.9 us
    unnamed x26, local copies, waits for them, and re-layouts  10.1 us
  transfers between devices with their start and end apart: 4, of which 3 were waited for; matrix products, arithmetic and copies ran while one was open for 12% of the time, Pallas kernels for 0%

profile of v5, /device:TPU:0, one launch (start us, length us, event | category | flops | bytes accessed | tf_op | source)
XLA Modules:
  0.0 327.1 jit_solution(8974880285099703394)
XLA Ops:
  7.2 0.0 all-gather.5.cloned.1.call-start
  7.2 0.9 copy-done
  8.2 0.8 constant_dynamic-slice_fusion
  9.1 0.0 reduce-scatter.2.cloned.1.call-start
  9.1 6.6 %copy.19 = f32[256,6144]{0,1:T(8,128)} copy(f32[256,6144]{1,0:T(8,128)} %param.4) | data formatting | bytes 12582912 | tf_op args[1]
  15.7 0.2 copy.20
  15.9 3.2 pad_maximum_fusion
  19.2 8.6 %fusion.24 = f32[6656,512]{1,0:T(8,128)} fusion(f32[256,6656]{0,1:T(8,128)S(1)} %bitcast.66, f32[256,512]{1,0:T(8,128)S(1)} %copy-done.4), kind=kOutput, calls=%fused_computation.36 | convolution fusion | flops 5234491392 | bytes 20971520 | tf_op jit(solution)/shard_map/dot_general | solution.py:11
  27.8 36.2 %all-gather.5.cloned.1.call-done = bf16[8192,192]{1,0:T(8,128)(2,1)} async-done(((bf16[512,192]{1,0:T(8,128)(2,1)}), bf16[8192,192]{1,0:T(8,128)(2,1)}) %all-gather.5.cloned.1.call-update) | async-done | bytes 3145744 | tf_op jit(solution)/shard_map/all_gather | solution.py:68
  64.0 6.1 %copy.34 = bf16[16,512,192]{1,0,2:T(8,128)(2,1)S(1)} copy(bf16[16,512,192]{2,1,0:T(8,128)(2,1)} %bitcast.74) | data formatting | bytes 6291456 | tf_op jit(solution)/shard_map/all_gather | solution.py:68
  70.2 0.2 all-gather.7.cloned.1.call-start
  70.4 140.4 %reduce-scatter.2.cloned.1.call-done = f32[416,512]{1,0:T(8,128)} async-done(((f32[6656,512]{1,0:T(8,128)}), f32[416,512]{1,0:T(8,128)}) %reduce-scatter.2.cloned.1.call-update) | async-done | bytes 851984 | tf_op jit(solution)/shard_map/reduce_scatter | solution.py:85
  210.8 0.8 reduce-precision_convert_fusion.3
  211.7 1.2 slice.31
  212.8 0.8 pad_maximum_fusion.2
  213.7 3.5 %copy.22 = bf16[16,512,192]{1,2,0:T(8,128)(2,1)} copy(bf16[16,512,192]{1,0,2:T(8,128)(2,1)S(1)} %copy.34) | data formatting | bytes 6291456 | tf_op jit(solution)/shard_map/optimization_barrier | solution.py:78
  217.2 1.5 collective-permute-start
  218.7 67.8 %collective-permute-done = bf16[16,512,192]{1,2,0:T(8,128)(2,1)} collective-permute-done((bf16[16,512,192]{1,2,0:T(8,128)(2,1)}, bf16[16,512,192]{1,2,0:T(8,128)(2,1)}, u32[]{:S(2)}, u32[]{:S(2)}) %collective-permute-start) | collective-permute-done | bytes 3145760 | tf_op jit(solution)/shard_map/ppermute | solution.py:79
  286.5 7.2 %select_bitcast_fusion.1 = (bf16[16,1,512,192]{2,3,1,0:T(8,128)(2,1)S(1)}, bf16[16,1,512,192]{2,3,1,0:T(8,128)(2,1)}) fusion(bf16[16,512,192]{1,2,0:T(8,128)(2,1)} %collective-permute-done, pred[]{:T(512)S(6)} %eq.3, bf16[16,512,192]{1,0,2:T(8,128)(2,1)S(1)} %copy.34), kind=kLoop, calls=%fused_computation.8 | loop fusion | flops 3145728 | bytes 12582913 | tf_op jit(solution)/shard_map/stack | solution.py:81
  293.7 3.7 %pad_maximum_fusion.1 = bf16[16,2,512,192]{2,3,1,0:T(8,128)(2,1)S(1)} fusion(bf16[16,1,512,192]{2,3,1,0:T(8,128)(2,1)} %get-tuple-element.13, bf16[16,1,512,192]{2,3,1,0:T(8,128)(2,1)S(1)} %get-tuple-element.12), kind=kLoop, calls=%fused_computation.4 | loop fusion | flops 3145728 | bytes 12582912 | tf_op jit(solution)/shard_map/stack | solution.py:81
  297.4 2.8 fusion.21
  300.2 1.8 fusion.16
  302.1 1.5 convert_add_fusion
  303.6 3.6 %slice.24 = bf16[16,384,512]{2,1,0:T(8,128)(2,1)S(1)} slice(bf16[16,448,512]{2,1,0:T(8,128)(2,1)} %bitcast.73), slice={[0:16], [0:384], [0:512]} | slice | bytes 12582912 | tf_op jit(solution)/shard_map/slice | solution.py:94
  307.2 0.1 slice-done.3
  307.3 3.0 fusion.19
  310.3 3.5 %fusion.9 = f32[512,512]{1,0:T(8,128)S(1)} fusion(f32[512,512]{1,0:T(8,128)S(1)} %bitcast.75, f32[512]{0:T(512)S(1)} %convert_add_fusion.1, bf16[16,1,512,192]{2,3,1,0:T(8,128)(2,1)S(1)} %copy-done.3, bf16[16,1,512,192]{2,3,1,0:T(8,128)(2,1)S(1)} %copy-done.2), kind=kOutput, calls=%fused_computation.11 | convolution fusion | flops 3225681920 | bytes 8390656 | tf_op jit(solution)/shard_map/dot_general | solution.py:11
  313.8 1.8 fusion.18
  315.6 1.9 fusion.14
  317.5 1.0 copy.28
  318.5 0.9 fusion.12
  319.4 1.1 copy.29
  (28 shorter events, 0.1 us)
Async XLA Ops:
  7.2 1.0 copy-start
  7.2 56.9 %all-gather.5.cloned.1.call-start = ((), (), s32[]{:S(2)}) async-start(), calls=%async_computation.2 | async-start | bytes 4456448 | tf_op jit(solution)/shard_map/all_gather | solution.py:68
  9.0 6.7 %copy-start.4 = (f32[256,512]{1,0:T(8,128)S(1)}, f32[256,512]{1,0:T(8,128)}, u32[]{:S(2)}) copy-start(f32[256,512]{1,0:T(8,128)} %param.3) | copy-start | bytes 1572868
  9.1 201.8 %reduce-scatter.2.cloned.1.call-start = ((), (), s32[]{:S(2)}) async-start(), calls=%async_computation.1 | async-start | bytes 14483456 | tf_op jit(solution)/shard_map/reduce_scatter | solution.py:85
  70.2 231.9 %all-gather.7.cloned.1.call-start = ((), (), s32[]{:S(2)}) async-start(), calls=%async_computation.3 | async-start | bytes 7798784 | tf_op jit(solution)/shard_map/all_gather | solution.py:93
  217.2 69.3 %collective-permute-start = (bf16[16,512,192]{1,2,0:T(8,128)(2,1)}, bf16[16,512,192]{1,2,0:T(8,128)(2,1)}, u32[]{:S(2)}, u32[]{:S(2)}) collective-permute-start(bf16[16,512,192]{1,2,0:T(8,128)(2,1)} %copy.22), channel_id=1, source_target_pairs={{0,16},{16,0},{1,17},{17,1},{2,18},{18,2},{3,19},{19,3},{4,20},{20... | collective-permute-start | bytes 9437192 | tf_op jit(solution)/shard_map/ppermute | solution.py:79
  286.5 10.9 %slice-start = ((s8[6291456]{0:T(1024)(128)(4,1)}), s8[4194304]{0:T(1024)(128)(4,1)S(1)}, s32[]{:S(2)}) async-start(s8[6291456]{0:T(1024)(128)(4,1)} %bitcast.62), calls=%async_computation.4 | async-start | bytes 8388608
  293.7 3.7 %copy-start.1 = (bf16[16,1,512,192]{2,3,1,0:T(8,128)(2,1)}, bf16[16,1,512,192]{2,3,1,0:T(8,128)(2,1)S(1)}, u32[]{:S(2)}) copy-start(bf16[16,1,512,192]{2,3,1,0:T(8,128)(2,1)S(1)} %get-tuple-element.12) | copy-start | bytes 9437188
  293.7 3.7 %slice-start.1 = ((s8[6291456]{0:T(1024)(128)(4,1)}), s8[2097152]{0:T(1024)(128)(4,1)S(1)}, s32[]{:S(2)}) async-start(s8[6291456]{0:T(1024)(128)(4,1)} %bitcast.62), calls=%async_computation.5 | async-start | bytes 4194304
  302.1 5.1 %slice-start.2 = ((s8[6291456]{0:T(1024)(128)(4,1)}), s8[4194304]{0:T(1024)(128)(4,1)S(1)}, s32[]{:S(2)}) async-start(s8[6291456]{0:T(1024)(128)(4,1)} %bitcast.64), calls=%async_computation.6 | async-start | bytes 8388608
  303.6 3.7 %slice-start.3 = ((s8[6291456]{0:T(1024)(128)(4,1)}), s8[2097152]{0:T(1024)(128)(4,1)S(1)}, s32[]{:S(2)}) async-start(s8[6291456]{0:T(1024)(128)(4,1)} %bitcast.64), calls=%async_computation.7 | async-start | bytes 4194304
  307.3 3.0 copy-start.2
  307.3 3.0 copy-start.3
  313.8 1.9 copy-start.5
  313.8 4.7 %copy-start.6 = (f32[416,512]{1,0:T(8,128)S(1)}, f32[416,512]{1,0:T(8,128)}, u32[]{:S(2)}) copy-start(f32[416,512]{1,0:T(8,128)} %reduce-scatter.2.cloned.1.call-done) | copy-start | bytes 2555908
Sparse Core Ops, SparseCore 0:
  10.7 53.2 all-gather.4
  70.3 140.4 reduce-scatter.1
  213.9 67.3 all-gather.6

commit v6 on v2

--- a/solution.py
+++ b/solution.py
@@ -52,7 +52,6 @@
     teacher_width = teacher.shape[1]
     total_rows = rows_here * devices
     f_here = teacher_width // devices
-    d_here = model_width // devices
     positions = jnp.arange(model_width)
     weights = (
         1.0
@@ -62,43 +61,47 @@
     nested = jnp.minimum(weights[:, None], weights[None, :])
     gram_scale = 0.5 / total_rows
 
-    heads_all = gather_by_doubling(heads, "rows", 1)
-
-    left = jnp.concatenate(
+    cross_part = contract(teacher, student, 0, 0, lax.Precision.HIGH)
+    moment_part = contract(student, student, 0, 0)
+    d_here = model_width // devices
+    partial = jnp.concatenate(
         [
-            teacher.reshape(rows_here, devices, f_here),
-            student.reshape(rows_here, devices, d_here),
+            cross_part.reshape(devices, f_here, model_width),
+            moment_part.reshape(devices, d_here, model_width),
         ],
-        axis=2,
-    ).reshape(rows_here, devices * (f_here + d_here))
-    partial = contract(left, student, 0, 0, lax.Precision.HIGH)
+        axis=1,
+    ).reshape(devices * (f_here + d_here), model_width)
     reduced = lax.psum_scatter(partial, "rows", scatter_dimension=0, tiled=True)
     cross_here = reduced[:f_here]
     moment_here = reduced[f_here:]
 
     moment_high, moment_low = split_bf16(moment_here)
-    packed = jnp.concatenate(
-        [cross_here.astype(jnp.bfloat16), moment_high, moment_low], axis=0
+    pair = jnp.concatenate([moment_high, moment_low], axis=1).reshape(-1)
+    spare = -(-pair.shape[0] // (f_here * 128)) * 128
+    pair = jnp.pad(pair, (0, f_here * spare - pair.shape[0])).reshape(f_here, spare)
+    wide_here = jnp.concatenate([cross_here.astype(jnp.bfloat16), heads.T, pair], axis=1)
+    wide_all = lax.all_gather(wide_here, "rows", axis=0, tiled=True)
+    moment_all = wide_all[:, 2 * model_width :].reshape(devices, f_here * spare)
+    moment_all = moment_all[:, : 2 * d_here * model_width].reshape(
+        devices, d_here, 2 * model_width
     )
-    gathered = lax.all_gather(packed, "rows", axis=0, tiled=False)
-    cross_low = gathered[:, :f_here].reshape(teacher_width, model_width)
     moment = (
-        gathered[:, f_here : f_here + d_here].astype(jnp.float32)
-        + gathered[:, f_here + d_here :].astype(jnp.float32)
+        moment_all[:, :, :model_width].astype(jnp.float32)
+        + moment_all[:, :, model_width:].astype(jnp.float32)
     ).reshape(model_width, model_width)
+    heads_all = wide_all[:, model_width : 2 * model_width]
 
     grad_heads = head_scale * (
         contract(moment, heads.astype(jnp.float32), 1, 0) - cross_here.T
     )
 
-    gram_heads = contract(heads_all, heads_all, 1, 1, lax.Precision.DEFAULT)
+    gram_heads = contract(heads_all, heads_all, 0, 0, lax.Precision.DEFAULT)
     teacher_high, teacher_low = split_bf16(teacher)
-    teacher_heads = contract(teacher_high, heads_all, 1, 1, lax.Precision.DEFAULT) + contract(
-        teacher_low, heads_all, 1, 1, lax.Precision.DEFAULT
+    teacher_wide = contract(teacher_high, wide_all, 1, 0, lax.Precision.DEFAULT) + contract(
+        teacher_low, wide_all, 1, 0, lax.Precision.DEFAULT
     )
-    teacher_cross = contract(teacher_high, cross_low, 1, 0, lax.Precision.DEFAULT) + contract(
-        teacher_low, cross_low, 1, 0, lax.Precision.DEFAULT
-    )
+    teacher_cross = teacher_wide[:, :model_width]
+    teacher_heads = teacher_wide[:, model_width : 2 * model_width]
     student_side = reg_weight * gram_heads + gram_scale * (moment * nested)
     grad_student = (
         contract(student, student_side, 1, 0)

time: 359 us -> 328 us (0.914); the launches traced: 352 us -> 328 us
  local copies, waits for them, and re-layouts: 46.7 us -> 13.7 us
  waiting for transfers between devices: 248 us -> 258 us
  matrix products: 26 us -> 34.7 us
  other arithmetic: 14.4 us -> 7.48 us
    all_gather x1, waiting for transfers between devices: 0.02 us -> 113 us  [per_device(): wide_all = lax.all_gather(wide_here, 'rows', axis=0, tiled=True)]
    ppermute x4 -> x0, waiting for transfers between devices: 103 us -> none  [gather_by_doubling(): lax.ppermute(held, axis_name, pairs)]
    gather x2 -> x0, local copies, waits for them, and re-layouts: 15.7 us -> none  [gather_by_doubling(): blocks = jnp.take(blocks, order, axis=axis)]
    unnamed x31 -> x14, local copies, waits for them, and re-layouts: 13.1 us -> 2.86 us
    dot_general x8 -> x7, matrix products: 26 us -> 34.7 us  [contract(): lax.dot_general(left, right, (((left_dim,), (right_dim,)), ((), ())), pre...]
    reshape x1 -> x3, local copies, waits for them, and re-layouts: 8.63 us -> 2.83 us  [the longest x1 2.69 us: per_device(): moment_all = wide_all[:, 2 * model_width:].reshape(devices, f_here * spare)]
    select_n x1 -> x0, other arithmetic: 4.47 us -> none  [gather_by_doubling(): blocks = jnp.take(blocks, order, axis=axis)]
    concatenate x1 -> x0, local copies, waits for them, and re-layouts: 3.87 us -> none  [gather_by_doubling(): jnp.concatenate([held, lax.ppermute(held, axis_name, pairs)], axis=axis)]
  transfers between devices with their start and end apart: 6 -> 2, of which waited for: 5 -> 2; matrix products, arithmetic and copies ran while one was open for 13% -> 0% of each run, Pallas kernels for 0% -> 0%
where the time goes in v6:
time: 328 us
  waiting for transfers between devices  258 us (79%)
  matrix products  34.7 us (11%)
  between operations  14.2 us (4%)
  local copies, waits for them, and re-layouts  13.7 us (4%)
  other arithmetic  7.48 us (2%)
    reduce_scatter x1, waiting for transfers between devices, per_device(): reduced = lax.psum_scatter(partial, 'rows', scatter_dimension=0, tiled=True)  145 us
    all_gather x1, waiting for transfers between devices, per_device(): wide_all = lax.all_gather(wide_here, 'rows', axis=0, tiled=True)  113 us
    dot_general x7, matrix products, contract(): lax.dot_general(left, right, (((left_dim,), (right_dim,)), ((), ())), pre...  34.7 us
  transfers between devices with their start and end apart: 2, of which 2 were waited for; matrix products, arithmetic and copies ran while one was open for 0% of the time, Pallas kernels for 0%

profile of v6, /device:TPU:0, one launch (start us, length us, event | category | flops | bytes accessed | tf_op | source)
XLA Modules:
  0.0 328.0 jit_solution(5604425876153434056)
XLA Ops:
  7.2 0.0 copy-start
  7.2 0.0 reduce-scatter.4.cloned.1.call-start
  7.2 1.0 copy-done
  8.2 1.0 fusion.21
  9.3 7.4 %fusion.20 = f32[6144,512]{1,0:T(8,128)S(1)} fusion(f32[256,6144]{1,0:T(8,128)} %param.4, f32[256,512]{1,0:T(8,128)S(1)} %copy-done), kind=kOutput, calls=%fused_computation.30 | convolution fusion | flops 4831838208 | bytes 19398656 | tf_op jit(solution)/shard_map/dot_general | solution.py:11
  16.7 5.4 %pad_maximum_fusion = f32[16,416,512]{2,1,0:T(8,128)} fusion(f32[16,32,512]{2,1,0:T(8,128)S(1)} %bitcast.41, f32[16,384,512]{2,1,0:T(8,128)S(1)} %bitcast.33), kind=kLoop, calls=%fused_computation | loop fusion | flops 3407872 | bytes 27262976 | tf_op jit(solution)/shard_map/concatenate | solution.py:67
  22.1 0.0 reduce-scatter.4.cloned.1.call-update
  22.1 0.2 all-gather.2.cloned.1.call-start
  22.3 144.6 %reduce-scatter.4.cloned.1.call-done = f32[416,512]{1,0:T(8,128)} async-done(((f32[6656,512]{1,0:T(8,128)}), f32[416,512]{1,0:T(8,128)}) %reduce-scatter.4.cloned.1.call-update) | async-done | bytes 851984 | tf_op jit(solution)/shard_map/reduce_scatter | solution.py:74
  166.9 0.8 reduce-precision_convert_fusion.4
  167.9 0.1 copy.23
  168.0 1.2 slice.36
  169.2 0.3 copy.30
  169.5 0.0 copy-done.1
  169.5 1.0 pad_maximum_fusion.1
  170.5 0.0 all-gather.2.cloned.1.call-update
  170.6 113.0 %all-gather.2.cloned.1.call-done = bf16[6144,1152]{0,1:T(8,128)(2,1)} async-done(((bf16[384,1152]{0,1:T(8,128)(2,1)}), bf16[6144,1152]{0,1:T(8,128)(2,1)}) %all-gather.2.cloned.1.call-update) | async-done | bytes 14155792 | tf_op jit(solution)/shard_map/all_gather | solution.py:83
  283.6 2.7 slice.39
  286.3 2.7 copy.24
  289.0 2.7 reshape.53
  291.7 1.4 slice.40
  293.2 0.6 copy.32
  293.7 0.2 convert_add_fusion
  293.9 0.0 copy-done.2
  293.9 1.9 fusion.16
  295.8 0.0 slice-done
  295.8 0.0 slice-done.1
  295.8 7.1 %fusion.9 = f32[256,1152]{0,1:T(8,128)S(1)} fusion(bf16[6144,1152]{0,1:T(8,128)(2,1)} %all-gather.2.cloned.1.call-done, f32[256,6144]{1,0:T(8,128)S(1)} %bitcast.36), kind=kOutput, calls=%fused_computation.9 | convolution fusion | flops 3627024384 | bytes 21626880 | tf_op jit(solution)/shard_map/dot_general | solution.py:11
  302.9 8.3 %fusion.13 = f32[512,512]{1,0:T(8,128)S(1)} fusion(bf16[6144,1152]{0,1:T(8,128)(2,1)} %all-gather.2.cloned.1.call-done, f32[512,512]{1,0:T(8,128)S(1)} %bitcast.38, f32[512]{0:T(512)S(1)} %convert_add_fusion.1), kind=kOutput, calls=%fused_computation.11 | convolution fusion | flops 3222536192 | bytes 8392704 | tf_op jit(solution)/shard_map/dot_general | solution.py:11
  311.2 7.1 %fusion.6 = f32[256,1152]{0,1:T(8,128)S(1)} fusion(f32[256,1152]{0,1:T(8,128)S(1)} %fusion.9, bf16[6144,1152]{0,1:T(8,128)(2,1)} %all-gather.2.cloned.1.call-done, f32[256,6144]{1,0:T(8,128)S(1)} %bitcast.36), kind=kOutput, calls=%fused_computation.8 | convolution fusion | flops 3628892160 | bytes 22806528 | tf_op jit(solution)/shard_map/dot_general | solution.py:11
  318.3 1.9 fusion.18
  320.2 1.0 copy.26
  (11 shorter events, 0.1 us)
Async XLA Ops:
  7.2 1.0 copy-start
  7.2 159.8 %reduce-scatter.4.cloned.1.call-start = ((), (), s32[]{:S(2)}) async-start(), calls=%async_computation.2 | async-start | bytes 14483456 | tf_op jit(solution)/shard_map/reduce_scatter | solution.py:74
  22.1 147.4 %copy-start.1 = (bf16[512,384]{1,0:T(8,128)(2,1)S(1)}, bf16[512,384]{1,0:T(8,128)(2,1)}, u32[]{:S(2)}) copy-start(bf16[512,384]{1,0:T(8,128)(2,1)} %param.5) | copy-start | bytes 1179652
  22.1 261.5 %all-gather.2.cloned.1.call-start = ((), (), s32[]{:S(2)}) async-start(), calls=%async_computation.1 | async-start | bytes 15040512 | tf_op jit(solution)/shard_map/all_gather | solution.py:83
  286.3 9.5 %slice-start = ((s8[6291456]{0:T(1024)(128)(4,1)}), s8[2097152]{0:T(1024)(128)(4,1)S(1)}, s32[]{:S(2)}) async-start(s8[6291456]{0:T(1024)(128)(4,1)} %bitcast.35), calls=%async_computation.3 | async-start | bytes 4194304
  291.7 2.2 copy-start.2
  291.7 4.1 %slice-start.1 = ((s8[6291456]{0:T(1024)(128)(4,1)}), s8[4194304]{0:T(1024)(128)(4,1)S(1)}, s32[]{:S(2)}) async-start(s8[6291456]{0:T(1024)(128)(4,1)} %bitcast.35), calls=%async_computation.4 | async-start | bytes 8388608
Sparse Core Ops, SparseCore 0:
  22.2 144.6 reduce-scatter.3
  170.7 112.8 all-gather.1

commit v7 on v6

--- a/solution.py
+++ b/solution.py
@@ -76,15 +76,14 @@
     moment_here = reduced[f_here:]
 
     moment_high, moment_low = split_bf16(moment_here)
-    pair = jnp.concatenate([moment_high, moment_low], axis=1).reshape(-1)
-    spare = -(-pair.shape[0] // (f_here * 128)) * 128
-    pair = jnp.pad(pair, (0, f_here * spare - pair.shape[0])).reshape(f_here, spare)
+    pair = jnp.concatenate([moment_high, moment_low], axis=1)
+    pair_rows = pair.size // 128
+    pair = pair.reshape(pair_rows, 128)
+    pair = jnp.pad(pair, ((0, f_here - pair_rows), (0, 0)))
     wide_here = jnp.concatenate([cross_here.astype(jnp.bfloat16), heads.T, pair], axis=1)
     wide_all = lax.all_gather(wide_here, "rows", axis=0, tiled=True)
-    moment_all = wide_all[:, 2 * model_width :].reshape(devices, f_here * spare)
-    moment_all = moment_all[:, : 2 * d_here * model_width].reshape(
-        devices, d_here, 2 * model_width
-    )
+    moment_all = wide_all[:, 2 * model_width :].reshape(devices, f_here, 128)[:, :pair_rows]
+    moment_all = moment_all.reshape(devices, d_here, 2 * model_width)
     moment = (
         moment_all[:, :, :model_width].astype(jnp.float32)
         + moment_all[:, :, model_width:].astype(jnp.float32)

time: 328 us -> 326 us (level)
  local copies, waits for them, and re-layouts: 13.7 us -> 8.47 us
  matrix products: 34.7 us -> 38 us
    slice x3 -> x2, local copies, waits for them, and re-layouts: 6.86 us -> 2.8 us  [per_device(): wide_all[:, 2 * model_width:].reshape(devices, f_here, 128)[:, :pair_rows]]
    dot_general x7, matrix products: 34.7 us -> 38 us  [contract(): lax.dot_general(left, right, (((left_dim,), (right_dim,)), ((), ())), pre...]
where the time goes in v7:
time: 326 us
  waiting for transfers between devices  258 us (79%)
  matrix products  38 us (12%)
  between operations  14.2 us (4%)
  local copies, waits for them, and re-layouts  8.47 us (3%)
  other arithmetic  7.45 us (2%)
    reduce_scatter x1, waiting for transfers between devices, per_device(): reduced = lax.psum_scatter(partial, 'rows', scatter_dimension=0, tiled=True)  145 us
    all_gather x1, waiting for transfers between devices, per_device(): wide_all = lax.all_gather(wide_here, 'rows', axis=0, tiled=True)  113 us
    dot_general x7, matrix products, contract(): lax.dot_general(left, right, (((left_dim,), (right_dim,)), ((), ())), pre...  38 us
  transfers between devices with their start and end apart: 2, of which 2 were waited for; matrix products, arithmetic and copies ran while one was open for 0% of the time, Pallas kernels for 0%

profile of v7, /device:TPU:0, one launch (start us, length us, event | category | flops | bytes accessed | tf_op | source)
XLA Modules:
  0.0 326.1 jit_solution(1016990920046528835)
XLA Ops:
  7.2 0.0 copy-start
  7.2 0.0 reduce-scatter.4.cloned.1.call-start
  7.2 1.0 copy-done
  8.2 1.0 fusion.23
  9.3 7.4 %fusion.22 = f32[6144,512]{1,0:T(8,128)S(1)} fusion(f32[256,6144]{1,0:T(8,128)} %param.4, f32[256,512]{1,0:T(8,128)S(1)} %copy-done), kind=kOutput, calls=%fused_computation.31 | convolution fusion | flops 4831838208 | bytes 19398656 | tf_op jit(solution)/shard_map/dot_general | solution.py:11
  16.7 5.4 %pad_maximum_fusion = f32[16,416,512]{2,1,0:T(8,128)} fusion(f32[16,32,512]{2,1,0:T(8,128)S(1)} %bitcast.34, f32[16,384,512]{2,1,0:T(8,128)S(1)} %bitcast.27), kind=kLoop, calls=%fused_computation | loop fusion | flops 3407872 | bytes 27262976 | tf_op jit(solution)/shard_map/concatenate | solution.py:67
  22.1 0.0 copy-start.1
  22.1 0.0 reduce-scatter.4.cloned.1.call-update
  22.1 0.2 all-gather.2.cloned.1.call-start
  22.3 144.6 %reduce-scatter.4.cloned.1.call-done = f32[416,512]{1,0:T(8,128)} async-done(((f32[6656,512]{1,0:T(8,128)}), f32[416,512]{1,0:T(8,128)}) %reduce-scatter.4.cloned.1.call-update) | async-done | bytes 851984 | tf_op jit(solution)/shard_map/reduce_scatter | solution.py:74
  166.9 0.8 reduce-precision_convert_fusion.4
  167.8 0.1 copy.23
  167.9 1.2 slice.36
  169.1 0.3 copy.31
  169.5 0.0 copy-done.1
  169.5 1.0 fusion.20
  170.5 0.0 all-gather.2.cloned.1.call-update
  170.5 113.0 %all-gather.2.cloned.1.call-done = bf16[6144,1152]{0,1:T(8,128)(2,1)} async-done(((bf16[384,1152]{0,1:T(8,128)(2,1)}), bf16[6144,1152]{0,1:T(8,128)(2,1)}) %all-gather.2.cloned.1.call-update) | async-done | bytes 14155792 | tf_op jit(solution)/shard_map/all_gather | solution.py:84
  283.6 1.5 slice.39
  285.1 1.6 copy.28
  286.6 1.3 slice.40
  288.0 0.5 reshape.50
  288.5 0.1 convert_add_fusion
  288.6 0.0 slice-start
  288.6 3.0 fusion.17
  291.7 9.0 %fusion.9 = f32[256,1152]{0,1:T(8,128)S(1)} fusion(bf16[6144,1152]{0,1:T(8,128)(2,1)} %all-gather.2.cloned.1.call-done, f32[256,6144]{1,0:T(8,128)} %param.4), kind=kOutput, calls=%fused_computation.9 | convolution fusion | flops 3627024384 | bytes 21626880 | tf_op jit(solution)/shard_map/dot_general | solution.py:11
  300.7 8.3 %fusion.14 = f32[512,512]{1,0:T(8,128)S(1)} fusion(bf16[6144,1152]{0,1:T(8,128)(2,1)} %all-gather.2.cloned.1.call-done, f32[512,512]{1,0:T(8,128)S(1)} %bitcast.33, f32[512]{0:T(512)S(1)} %convert_add_fusion.1), kind=kOutput, calls=%fused_computation.13 | convolution fusion | flops 3222536192 | bytes 8392704 | tf_op jit(solution)/shard_map/dot_general | solution.py:11
  309.0 0.0 slice-done
  309.0 0.0 slice-done.1
  309.0 7.3 %fusion.6 = f32[256,1152]{0,1:T(8,128)S(1)} fusion(f32[256,1152]{0,1:T(8,128)S(1)} %fusion.9, bf16[6144,1152]{0,1:T(8,128)(2,1)} %all-gather.2.cloned.1.call-done, f32[256,6144]{1,0:T(8,128)S(1)} %bitcast.30), kind=kOutput, calls=%fused_computation.8 | convolution fusion | flops 3628892160 | bytes 22806528 | tf_op jit(solution)/shard_map/dot_general | solution.py:11
  316.4 1.9 fusion.19
  318.2 1.0 copy.26
  (7 shorter events, 0.1 us)
Async XLA Ops:
  7.2 1.0 copy-start
  7.2 159.7 %reduce-scatter.4.cloned.1.call-start = ((), (), s32[]{:S(2)}) async-start(), calls=%async_computation.2 | async-start | bytes 14483456 | tf_op jit(solution)/shard_map/reduce_scatter | solution.py:74
  22.1 147.4 %copy-start.1 = (bf16[512,384]{1,0:T(8,128)(2,1)S(1)}, bf16[512,384]{1,0:T(8,128)(2,1)}, u32[]{:S(2)}) copy-start(bf16[512,384]{1,0:T(8,128)(2,1)} %param.5) | copy-start | bytes 1179652
  22.1 261.5 %all-gather.2.cloned.1.call-start = ((), (), s32[]{:S(2)}) async-start(), calls=%async_computation.1 | async-start | bytes 15040512 | tf_op jit(solution)/shard_map/all_gather | solution.py:84
  288.6 20.4 %slice-start = ((s8[6291456]{0:T(1024)(128)(4,1)}), s8[4194304]{0:T(1024)(128)(4,1)S(1)}, s32[]{:S(2)}) async-start(s8[6291456]{0:T(1024)(128)(4,1)} %bitcast.29), calls=%async_computation.3 | async-start | bytes 8388608
  291.7 17.3 %slice-start.1 = ((s8[6291456]{0:T(1024)(128)(4,1)}), s8[2097152]{0:T(1024)(128)(4,1)S(1)}, s32[]{:S(2)}) async-start(s8[6291456]{0:T(1024)(128)(4,1)} %bitcast.29), calls=%async_computation.4 | async-start | bytes 4194304
Sparse Core Ops, SparseCore 0:
  22.2 144.6 reduce-scatter.3
  170.6 112.8 all-gather.1

commit v8 on v7

--- a/solution.py
+++ b/solution.py
@@ -96,14 +96,15 @@
 
     gram_heads = contract(heads_all, heads_all, 0, 0, lax.Precision.DEFAULT)
     teacher_high, teacher_low = split_bf16(teacher)
-    teacher_wide = contract(teacher_high, wide_all, 1, 0, lax.Precision.DEFAULT) + contract(
-        teacher_low, wide_all, 1, 0, lax.Precision.DEFAULT
+    teacher_wide = contract(
+        jnp.concatenate([teacher_high, teacher_low], axis=0), wide_all, 1, 0, lax.Precision.DEFAULT
     )
+    teacher_wide = teacher_wide[:rows_here] + teacher_wide[rows_here:]
     teacher_cross = teacher_wide[:, :model_width]
     teacher_heads = teacher_wide[:, model_width : 2 * model_width]
     student_side = reg_weight * gram_heads + gram_scale * (moment * nested)
     grad_student = (
-        contract(student, student_side, 1, 0)
+        contract(student, student_side, 1, 0, lax.Precision.HIGH)
         - reg_weight * teacher_heads
         - gram_scale * teacher_cross * weights[None, :]
     )

time: 326 us -> 321 us (0.985)
  waiting for transfers between devices: 258 us -> 251 us
  other arithmetic: 7.45 us -> 14.2 us
  matrix products: 38 us -> 32.2 us
    all_gather x1, waiting for transfers between devices: 113 us -> 106 us  [per_device(): wide_all = lax.all_gather(wide_here, 'rows', axis=0, tiled=True)]
    convert_element_type x1 -> x2, other arithmetic: 0.85 us -> 7.46 us  [split_bf16(): return (high.astype(jnp.bfloat16), low)]
    dot_general x7 -> x6, matrix products: 38 us -> 32.2 us  [contract(): lax.dot_general(left, right, (((left_dim,), (right_dim,)), ((), ())), pre...]
  transfers between devices with their start and end apart: 2 -> 2, of which waited for: 2 -> 2; matrix products, arithmetic and copies ran while one was open for 0% -> 2% of each run, Pallas kernels for 0% -> 0%
where the time goes in v8:
time: 321 us; the launch traced here: 320 us
  waiting for transfers between devices  251 us (78%)
  matrix products  32.2 us (10%)
  other arithmetic  14.2 us (4%)
  between operations  14.2 us (4%)
  local copies, waits for them, and re-layouts  8.45 us (3%)
    reduce_scatter x1, waiting for transfers between devices, per_device(): reduced = lax.psum_scatter(partial, 'rows', scatter_dimension=0, tiled=True)  145 us
    all_gather x1, waiting for transfers between devices, per_device(): wide_all = lax.all_gather(wide_here, 'rows', axis=0, tiled=True)  106 us
    dot_general x6, matrix products, contract(): lax.dot_general(left, right, (((left_dim,), (right_dim,)), ((), ())), pre...  32.2 us
    convert_element_type x2, other arithmetic, split_bf16(): return (high.astype(jnp.bfloat16), low)  7.46 us
  transfers between devices with their start and end apart: 2, of which 2 were waited for; matrix products, arithmetic and copies ran while one was open for 2% of the time, Pallas kernels for 0%

profile of v8, /device:TPU:0, one launch (start us, length us, event | category | flops | bytes accessed | tf_op | source)
XLA Modules:
  0.0 320.3 jit_solution(6400336228618980917)
XLA Ops:
  7.2 0.0 copy-start
  7.2 0.0 reduce-scatter.4.cloned.1.call-start
  7.2 1.0 copy-done
  8.2 1.0 fusion.21
  9.3 7.4 %fusion.20 = f32[6144,512]{1,0:T(8,128)S(1)} fusion(f32[256,6144]{1,0:T(8,128)} %param.4, f32[256,512]{1,0:T(8,128)S(1)} %copy-done), kind=kOutput, calls=%fused_computation.33 | convolution fusion | flops 4831838208 | bytes 19398656 | tf_op jit(solution)/shard_map/dot_general | solution.py:11
  16.7 5.3 %pad_maximum_fusion = f32[16,416,512]{2,1,0:T(8,128)} fusion(f32[16,32,512]{2,1,0:T(8,128)S(1)} %bitcast.29, f32[16,384,512]{2,1,0:T(8,128)S(1)} %bitcast.24), kind=kLoop, calls=%fused_computation | loop fusion | flops 3407872 | bytes 27262976 | tf_op jit(solution)/shard_map/concatenate | solution.py:67
  22.0 0.0 copy-start.1
  22.0 0.0 reduce-scatter.4.cloned.1.call-update
  22.1 0.2 all-gather.2.cloned.1.call-start
  22.3 144.6 %reduce-scatter.4.cloned.1.call-done = f32[416,512]{1,0:T(8,128)} async-done(((f32[6656,512]{1,0:T(8,128)}), f32[416,512]{1,0:T(8,128)}) %reduce-scatter.4.cloned.1.call-update) | async-done | bytes 851984 | tf_op jit(solution)/shard_map/reduce_scatter | solution.py:74
  166.9 0.8 reduce-precision_convert_fusion.1
  167.8 0.1 copy.26
  167.9 1.2 slice.44
  169.1 0.3 copy.35
  169.4 0.0 copy-done.1
  169.5 1.0 fusion.17
  170.5 0.0 all-gather.2.cloned.1.call-update
  170.5 6.6 %reduce-precision_convert_fusion = (bf16[256,6144]{1,0:T(8,128)(2,1)}, bf16[256,6144]{1,0:T(8,128)(2,1)}) fusion(f32[256,6144]{1,0:T(8,128)} %param.4), kind=kLoop, calls=%fused_computation.2 | loop fusion | flops 6291456 | bytes 12582912 | tf_op jit(solution)/shard_map/convert_element_type | solution.py:23
  177.1 106.4 %all-gather.2.cloned.1.call-done = bf16[6144,1152]{0,1:T(8,128)(2,1)} async-done(((bf16[384,1152]{0,1:T(8,128)(2,1)}), bf16[6144,1152]{0,1:T(8,128)(2,1)}) %all-gather.2.cloned.1.call-update) | async-done | bytes 14155792 | tf_op jit(solution)/shard_map/all_gather | solution.py:84
  283.5 1.5 slice.47
  285.0 1.6 copy.32
  286.6 1.3 slice.48
  287.9 0.5 reshape.50
  288.4 0.2 convert_add_fusion
  288.6 0.0 copy-start.2
  288.6 12.6 %fusion.3 = f32[512,1152]{0,1:T(8,128)S(1)} fusion(bf16[6144,1152]{0,1:T(8,128)(2,1)} %all-gather.2.cloned.1.call-done, bf16[256,6144]{1,0:T(8,128)(2,1)} %get-tuple-element.11, bf16[256,6144]{1,0:T(8,128)(2,1)} %get-tuple-element.10), kind=kOutput, calls=%fused_computation.6 | convolution fusion | flops 7260340224 | bytes 22806528 | tf_op jit(solution)/shard_map/dot_general | solution.py:11
  301.2 0.2 slice_add_fusion
  301.3 0.0 copy-done.2
  301.3 1.9 fusion.14
  303.2 8.2 %fusion.11 = f32[512,512]{1,0:T(8,128)S(1)} fusion(bf16[6144,1152]{0,1:T(8,128)(2,1)} %all-gather.2.cloned.1.call-done, f32[512,512]{1,0:T(8,128)S(1)} %bitcast.28, f32[512]{0:T(512)S(1)} %convert_add_fusion.1), kind=kOutput, calls=%fused_computation.13 | convolution fusion | flops 3222536192 | bytes 8392704 | tf_op jit(solution)/shard_map/dot_general | solution.py:11
  311.4 1.0 fusion.16
  312.5 1.0 copy.30
  (5 shorter events, 0.1 us)
Async XLA Ops:
  7.2 1.0 copy-start
  7.2 159.7 %reduce-scatter.4.cloned.1.call-start = ((), (), s32[]{:S(2)}) async-start(), calls=%async_computation.2 | async-start | bytes 14483456 | tf_op jit(solution)/shard_map/reduce_scatter | solution.py:74
  22.0 147.4 %copy-start.1 = (bf16[512,384]{1,0:T(8,128)(2,1)S(1)}, bf16[512,384]{1,0:T(8,128)(2,1)}, u32[]{:S(2)}) copy-start(bf16[512,384]{1,0:T(8,128)(2,1)} %param.5) | copy-start | bytes 1179652
  22.1 261.4 %all-gather.2.cloned.1.call-start = ((), (), s32[]{:S(2)}) async-start(), calls=%async_computation.1 | async-start | bytes 15040512 | tf_op jit(solution)/shard_map/all_gather | solution.py:84
  288.6 12.8 %copy-start.2 = (bf16[512,384]{1,0:T(8,128)(2,1)S(1)}, bf16[512,384]{1,0:T(8,128)(2,1)}, u32[]{:S(2)}) copy-start(bf16[512,384]{1,0:T(8,128)(2,1)} %param.5) | copy-start | bytes 1179652
Sparse Core Ops, SparseCore 0:
  22.2 144.6 reduce-scatter.3
  170.6 112.8 all-gather.1

commit v9 on v8

--- a/solution.py
+++ b/solution.py
@@ -61,6 +61,11 @@
     nested = jnp.minimum(weights[:, None], weights[None, :])
     gram_scale = 0.5 / total_rows
 
+    group = lax.axis_index("groups")
+    half = heads.shape[1] // 2
+    mine = lax.dynamic_slice_in_dim(heads, group * half, half, axis=1)
+    heads_parts = lax.all_gather(mine, ("groups", "rows"), axis=0, tiled=False)
+
     cross_part = contract(teacher, student, 0, 0, lax.Precision.HIGH)
     moment_part = contract(student, student, 0, 0)
     d_here = model_width // devices
@@ -71,6 +76,9 @@
         ],
         axis=1,
     ).reshape(devices * (f_here + d_here), model_width)
+    heads_parts, partial = lax.optimization_barrier((heads_parts, partial))
+    heads_all = heads_parts.reshape(2, devices, model_width, half).transpose(2, 1, 0, 3)
+    heads_all = heads_all.reshape(model_width, teacher_width)
     reduced = lax.psum_scatter(partial, "rows", scatter_dimension=0, tiled=True)
     cross_here = reduced[:f_here]
     moment_here = reduced[f_here:]
@@ -80,28 +88,26 @@
     pair_rows = pair.size // 128
     pair = pair.reshape(pair_rows, 128)
     pair = jnp.pad(pair, ((0, f_here - pair_rows), (0, 0)))
-    wide_here = jnp.concatenate([cross_here.astype(jnp.bfloat16), heads.T, pair], axis=1)
+    wide_here = jnp.concatenate([cross_here.astype(jnp.bfloat16), pair], axis=1)
     wide_all = lax.all_gather(wide_here, "rows", axis=0, tiled=True)
-    moment_all = wide_all[:, 2 * model_width :].reshape(devices, f_here, 128)[:, :pair_rows]
+    moment_all = wide_all[:, model_width:].reshape(devices, f_here, 128)[:, :pair_rows]
     moment_all = moment_all.reshape(devices, d_here, 2 * model_width)
     moment = (
         moment_all[:, :, :model_width].astype(jnp.float32)
         + moment_all[:, :, model_width:].astype(jnp.float32)
     ).reshape(model_width, model_width)
-    heads_all = wide_all[:, model_width : 2 * model_width]
 
     grad_heads = head_scale * (
         contract(moment, heads.astype(jnp.float32), 1, 0) - cross_here.T
     )
 
-    gram_heads = contract(heads_all, heads_all, 0, 0, lax.Precision.DEFAULT)
+    gram_heads = contract(heads_all, heads_all, 1, 1, lax.Precision.DEFAULT)
     teacher_high, teacher_low = split_bf16(teacher)
-    teacher_wide = contract(
-        jnp.concatenate([teacher_high, teacher_low], axis=0), wide_all, 1, 0, lax.Precision.DEFAULT
-    )
-    teacher_wide = teacher_wide[:rows_here] + teacher_wide[rows_here:]
-    teacher_cross = teacher_wide[:, :model_width]
-    teacher_heads = teacher_wide[:, model_width : 2 * model_width]
+    teacher_pair = jnp.concatenate([teacher_high, teacher_low], axis=0)
+    teacher_heads = contract(teacher_pair, heads_all, 1, 1, lax.Precision.DEFAULT)
+    teacher_heads = teacher_heads[:rows_here] + teacher_heads[rows_here:]
+    teacher_cross = contract(teacher_pair, wide_all, 1, 0, lax.Precision.DEFAULT)
+    teacher_cross = (teacher_cross[:rows_here] + teacher_cross[rows_here:])[:, :model_width]
     student_side = reg_weight * gram_heads + gram_scale * (moment * nested)
     grad_student = (
         contract(student, student_side, 1, 0, lax.Precision.HIGH)

time: 321 us -> 375 us (1.17)
  matrix products: 32.2 us -> 54.3 us
  local copies, waits for them, and re-layouts: 8.45 us -> 26.1 us
  waiting for transfers between devices: 251 us -> 266 us
    all_gather x0 -> x1, waiting for transfers between devices: none -> 68.6 us  [per_device(): heads_parts = lax.all_gather(mine, ('groups', 'rows'), axis=0, tiled=False)]
    all_gather x1, waiting for transfers between devices: 106 us -> 56.5 us  [per_device(): wide_all = lax.all_gather(wide_here, 'rows', axis=0, tiled=True)]
    dot_general x6 -> x7, matrix products: 32.2 us -> 54.3 us  [contract(): lax.dot_general(left, right, (((left_dim,), (right_dim,)), ((), ())), pre...]
    all_gather x0 -> x1, local copies, waits for them, and re-layouts: none -> 13.1 us  [per_device(): heads_parts = lax.all_gather(mine, ('groups', 'rows'), axis=0, tiled=False)]
    reduce_scatter x1, waiting for transfers between devices: 145 us -> 140 us  [per_device(): reduced = lax.psum_scatter(partial, 'rows', scatter_dimension=0, tiled=True)]
  transfers between devices with their start and end apart: 2 -> 3, of which waited for: 2 -> 3; matrix products, arithmetic and copies ran while one was open for 2% -> 8% of each run, Pallas kernels for 0% -> 0%
where the time goes in v9:
time: 375 us
  waiting for transfers between devices  266 us (71%)
  matrix products  54.3 us (14%)
  local copies, waits for them, and re-layouts  26.1 us (7%)
  other arithmetic  14.3 us (4%)
  between operations  13.9 us (4%)
    reduce_scatter x1, waiting for transfers between devices, per_device(): reduced = lax.psum_scatter(partial, 'rows', scatter_dimension=0, tiled=True)  140 us
    all_gather x1, waiting for transfers between devices, per_device(): heads_parts = lax.all_gather(mine, ('groups', 'rows'), axis=0, tiled=False)  68.6 us
    all_gather x1, waiting for transfers between devices, per_device(): wide_all = lax.all_gather(wide_here, 'rows', axis=0, tiled=True)  56.5 us
    dot_general x7, matrix products, contract(): lax.dot_general(left, right, (((left_dim,), (right_dim,)), ((), ())), pre...  54.3 us
    all_gather x1, local copies, waits for them, and re-layouts, per_device(): heads_parts = lax.all_gather(mine, ('groups', 'rows'), axis=0, tiled=False)  13.1 us
    convert_element_type x2, other arithmetic, split_bf16(): return (high.astype(jnp.bfloat16), low)  7.74 us
  transfers between devices with their start and end apart: 3, of which 3 were waited for; matrix products, arithmetic and copies ran while one was open for 8% of the time, Pallas kernels for 0%

profile of v9, /device:TPU:0, one launch (start us, length us, event | category | flops | bytes accessed | tf_op | source)
XLA Modules:
  0.0 374.5 jit_solution(5926245485444291288)
XLA Ops:
  7.2 0.0 all-gather.6.cloned.1.call-start
  7.2 1.9 constant_dynamic-slice_fusion
  9.1 0.0 all-gather.6.cloned.1.call-update
  9.1 0.0 reduce-scatter.4.cloned.1.call-start
  9.2 1.0 fusion.18
  10.3 7.4 %fusion.17 = f32[6144,512]{1,0:T(8,128)S(1)} fusion(f32[256,6144]{1,0:T(8,128)} %param.4, f32[256,512]{1,0:T(8,128)S(1)} %copy-done), kind=kOutput, calls=%fused_computation.36 | convolution fusion | flops 4831838208 | bytes 19398656 | tf_op jit(solution)/shard_map/dot_general | solution.py:11
  17.7 5.5 %pad_maximum_fusion = f32[16,416,512]{2,1,0:T(8,128)} fusion(f32[16,32,512]{2,1,0:T(8,128)S(1)} %bitcast.51, f32[16,384,512]{2,1,0:T(8,128)S(1)} %bitcast.40), kind=kLoop, calls=%fused_computation | loop fusion | flops 3407872 | bytes 27262976 | tf_op jit(solution)/shard_map/concatenate | solution.py:72
  23.2 68.6 %all-gather.6.cloned.1.call-done = bf16[16384,192]{1,0:T(8,128)(2,1)} async-done(((bf16[512,192]{1,0:T(8,128)(2,1)}), bf16[16384,192]{1,0:T(8,128)(2,1)}) %all-gather.6.cloned.1.call-update) | async-done | bytes 6291472 | tf_op jit(solution)/shard_map/all_gather | solution.py:67
  91.8 13.1 %copy.78 = bf16[32,512,192]{1,0,2:T(8,128)(2,1)} copy(bf16[32,512,192]{2,1,0:T(8,128)(2,1)} %bitcast.46) | data formatting | bytes 12582912 | tf_op jit(solution)/shard_map/all_gather | solution.py:67
  104.9 0.0 reduce-scatter.4.cloned.1.call-update
  104.9 0.2 all-gather.4.cloned.1.call-start
  105.1 140.5 %reduce-scatter.4.cloned.1.call-done = f32[416,512]{1,0:T(8,128)} async-done(((f32[6656,512]{1,0:T(8,128)}), f32[416,512]{1,0:T(8,128)}) %reduce-scatter.4.cloned.1.call-update) | async-done | bytes 851984 | tf_op jit(solution)/shard_map/reduce_scatter | solution.py:82
  245.6 0.8 reduce-precision_convert_fusion.1
  246.5 0.1 copy.67
  246.6 1.2 slice.44
  247.8 0.3 copy.85
  248.2 0.8 fusion.11
  249.0 6.9 %reduce-precision_convert_fusion = (bf16[256,6144]{1,0:T(8,128)(2,1)}, bf16[256,6144]{1,0:T(8,128)(2,1)}) fusion(f32[256,6144]{1,0:T(8,128)} %param.4), kind=kLoop, calls=%fused_computation.2 | loop fusion | flops 6291456 | bytes 12582912 | tf_op jit(solution)/shard_map/convert_element_type | solution.py:23
  255.9 3.5 copy.63
  259.5 7.3 %fusion.2 = f32[512,512]{0,1:T(8,128)} fusion(bf16[512,6144]{0,1:T(8,128)(2,1)S(1)} %bitcast.47, bf16[256,6144]{1,0:T(8,128)(2,1)} %get-tuple-element.19, bf16[256,6144]{1,0:T(8,128)(2,1)} %get-tuple-element.18), kind=kOutput, calls=%fused_computation.6 | convolution fusion | flops 3233808384 | bytes 13631488 | tf_op jit(solution)/shard_map/dot_general | solution.py:11
  266.8 56.5 %all-gather.4.cloned.1.call-done = bf16[6144,640]{0,1:T(8,128)(2,1)} async-done(((bf16[384,640]{0,1:T(8,128)(2,1)}), bf16[6144,640]{0,1:T(8,128)(2,1)}) %all-gather.4.cloned.1.call-update) | async-done | bytes 7864336 | tf_op jit(solution)/shard_map/all_gather | solution.py:92
  323.2 1.5 slice.46
  324.7 1.6 copy.81
  326.3 1.3 slice.47
  327.6 0.5 reshape.57
  328.1 0.1 convert_add_fusion
  328.3 2.9 fusion.5
  331.2 27.1 %fusion.4 = f32[512,512]{1,0:T(8,128)S(1)} fusion(f32[512,512]{1,0:T(8,128)S(1)} %bitcast.50, f32[512]{0:T(512)S(1)} %convert_add_fusion.1, bf16[512,16,2,192]{0,1,2,3:T(8,128)(2,1)} %bitcast.42), kind=kOutput, calls=%fused_computation.9 | convolution fusion | flops 3222536192 | bytes 8390656 | tf_op jit(solution)/shard_map/dot_general | solution.py:11
  358.3 7.6 %fusion.1 = f32[512,640]{0,1:T(8,128)S(1)} fusion(bf16[6144,640]{0,1:T(8,128)(2,1)} %all-gather.4.cloned.1.call-done, bf16[256,6144]{1,0:T(8,128)(2,1)S(1)} %copy-done.2, bf16[256,6144]{1,0:T(8,128)(2,1)S(1)} %copy-done.1), kind=kOutput, calls=%fused_computation.5 | convolution fusion | flops 4039114752 | bytes 15466496 | tf_op jit(solution)/shard_map/dot_general | solution.py:11
  365.9 0.1 fusion.16
  366.0 1.0 fusion.7
  367.0 1.0 copy.74
  (19 shorter events, 0.1 us)
Async XLA Ops:
  7.2 2.0 copy-start
  7.2 84.6 %all-gather.6.cloned.1.call-start = ((), (), s32[]{:S(2)}) async-start(), calls=%async_computation.2 | async-start | bytes 8650752 | tf_op jit(solution)/shard_map/all_gather | solution.py:67
  9.1 236.5 %reduce-scatter.4.cloned.1.call-start = ((), (), s32[]{:S(2)}) async-start(), calls=%async_computation.3 | async-start | bytes 14483456 | tf_op jit(solution)/shard_map/reduce_scatter | solution.py:82
  104.9 218.3 %all-gather.4.cloned.1.call-start = ((), (), s32[]{:S(2)}) async-start(), calls=%async_computation.1 | async-start | bytes 8355840 | tf_op jit(solution)/shard_map/all_gather | solution.py:92
  249.0 7.0 %slice-start = ((s8[6291456]{0:T(1024)(128)(4,1)}), s8[2097152]{0:T(1024)(128)(4,1)S(1)}, s32[]{:S(2)}) async-start(s8[6291456]{0:T(1024)(128)(4,1)} %bitcast.43), calls=%async_computation.4 | async-start | bytes 4194304
  249.0 6.9 %slice-start.1 = ((s8[6291456]{0:T(1024)(128)(4,1)}), s8[4194304]{0:T(1024)(128)(4,1)S(1)}, s32[]{:S(2)}) async-start(s8[6291456]{0:T(1024)(128)(4,1)} %bitcast.43), calls=%async_computation.5 | async-start | bytes 8388608
  331.2 27.1 %copy-start.1 = (bf16[256,6144]{1,0:T(8,128)(2,1)S(1)}, bf16[256,6144]{1,0:T(8,128)(2,1)}, u32[]{:S(2)}) copy-start(bf16[256,6144]{1,0:T(8,128)(2,1)} %get-tuple-element.18) | copy-start | bytes 9437188
  331.2 27.1 %copy-start.2 = (bf16[256,6144]{1,0:T(8,128)(2,1)S(1)}, bf16[256,6144]{1,0:T(8,128)(2,1)}, u32[]{:S(2)}) copy-start(bf16[256,6144]{1,0:T(8,128)(2,1)} %get-tuple-element.19) | copy-start | bytes 9437188
  358.3 7.7 %copy-start.3 = (f32[512,512]{0,1:T(8,128)S(1)}, f32[512,512]{0,1:T(8,128)}, u32[]{:S(2)}) copy-start(f32[512,512]{0,1:T(8,128)} %fusion.2) | copy-start | bytes 3145732
Sparse Core Ops, SparseCore 0:
  11.5 80.2 all-gather.5
  105.0 140.5 reduce-scatter.3
  249.1 74.0 all-gather.3

commit v10 on v1

--- a/solution.py
+++ b/solution.py
@@ -18,9 +18,9 @@
 
 
 def split_bf16(x):
-    high = x.astype(jnp.bfloat16)
-    low = (x - high.astype(jnp.float32)).astype(jnp.bfloat16)
-    return high, low
+    high = lax.reduce_precision(x, exponent_bits=8, mantissa_bits=7)
+    low = (x - high).astype(jnp.bfloat16)
+    return high.astype(jnp.bfloat16), low
 
 
 def per_device(student, teacher, heads):
@@ -49,6 +49,7 @@
         axis=2,
     ).reshape(rows_here, devices * (f_here + d_here))
     partial = contract(left, student, 0, 0, lax.Precision.HIGH)
+    heads_all, partial = lax.optimization_barrier((heads_all, partial))
     reduced = lax.psum_scatter(partial, "rows", scatter_dimension=0, tiled=True)
     cross_here = reduced[:f_here]
     moment_here = reduced[f_here:]
@@ -65,20 +66,19 @@
     ).reshape(model_width, model_width)
 
     grad_heads = head_scale * (
-        contract(moment, heads.astype(jnp.float32), 1, 0) - cross_here.T
+        contract(moment, heads.astype(jnp.float32), 1, 0, lax.Precision.HIGH) - cross_here.T
     )
 
     gram_heads = contract(heads_all, heads_all, 1, 1, lax.Precision.DEFAULT)
     teacher_high, teacher_low = split_bf16(teacher)
-    teacher_heads = contract(teacher_high, heads_all, 1, 1, lax.Precision.DEFAULT) + contract(
-        teacher_low, heads_all, 1, 1, lax.Precision.DEFAULT
-    )
-    teacher_cross = contract(teacher_high, cross_low, 1, 0, lax.Precision.DEFAULT) + contract(
-        teacher_low, cross_low, 1, 0, lax.Precision.DEFAULT
-    )
+    teacher_pair = jnp.concatenate([teacher_high, teacher_low], axis=0)
+    teacher_heads = contract(teacher_pair, heads_all, 1, 1, lax.Precision.DEFAULT)
+    teacher_heads = teacher_heads[:rows_here] + teacher_heads[rows_here:]
+    teacher_cross = contract(teacher_pair, cross_low, 1, 0, lax.Precision.DEFAULT)
+    teacher_cross = teacher_cross[:rows_here] + teacher_cross[rows_here:]
     student_side = reg_weight * gram_heads + gram_scale * (moment * nested)
     grad_student = (
-        contract(student, student_side, 1, 0)
+        contract(student, student_side, 1, 0, lax.Precision.HIGH)
         - reg_weight * teacher_heads
         - gram_scale * teacher_cross * weights[None, :]
     )

time: 340 us -> 324 us (0.953)
  waiting for transfers between devices: 264 us -> 249 us
  matrix products: 41.4 us -> 32.6 us
  local copies, waits for them, and re-layouts: 13.6 us -> 17.6 us
  other arithmetic: 6.48 us -> 10.2 us
    all_gather x1, waiting for transfers between devices: 64.2 us -> 50.9 us  [per_device(): heads_all = lax.all_gather(heads, 'rows', axis=1, tiled=True)]
    dot_general x8 -> x6, matrix products: 41.4 us -> 32.6 us  [contract(): lax.dot_general(left, right, (((left_dim,), (right_dim,)), ((), ())), pre...]
    convert_element_type x1 -> x2, other arithmetic: 0.93 us -> 4.79 us  [split_bf16(): return (high.astype(jnp.bfloat16), low)]
    unnamed x20 -> x16, local copies, waits for them, and re-layouts: 9.04 us -> 12.8 us
  transfers between devices with their start and end apart: 3 -> 3, of which waited for: 3 -> 3; matrix products, arithmetic and copies ran while one was open for 5% -> 10% of each run, Pallas kernels for 0% -> 0%
where the time goes in v10:
time: 324 us
  waiting for transfers between devices  249 us (77%)
  matrix products  32.6 us (10%)
  local copies, waits for them, and re-layouts  17.6 us (5%)
  between operations  13.9 us (4%)
  other arithmetic  10.2 us (3%)
    reduce_scatter x1, waiting for transfers between devices, per_device(): reduced = lax.psum_scatter(partial, 'rows', scatter_dimension=0, tiled=True)  144 us
    all_gather x1, waiting for transfers between devices, per_device(): gathered = lax.all_gather(packed, 'rows', axis=0, tiled=False)  53.4 us
    all_gather x1, waiting for transfers between devices, per_device(): heads_all = lax.all_gather(heads, 'rows', axis=1, tiled=True)  50.9 us
    dot_general x6, matrix products, contract(): lax.dot_general(left, right, (((left_dim,), (right_dim,)), ((), ())), pre...  32.6 us
    unnamed x16, local copies, waits for them, and re-layouts  12.8 us
  transfers between devices with their start and end apart: 3, of which 3 were waited for; matrix products, arithmetic and copies ran while one was open for 10% of the time, Pallas kernels for 0%

profile of v10, /device:TPU:0, one launch (start us, length us, event | category | flops | bytes accessed | tf_op | source)
XLA Modules:
  0.0 323.7 jit_solution(9397002974539703571)
XLA Ops:
  7.2 0.0 all-gather.4.cloned.1.call-start
  7.2 0.7 all-gather.4.cloned.1.call-update
  7.9 0.0 reduce-scatter.2.cloned.1.call-start
  7.9 1.2 copy.13
  9.2 6.6 %copy.12 = f32[256,6144]{0,1:T(8,128)} copy(f32[256,6144]{1,0:T(8,128)} %param.4) | data formatting | bytes 12582912 | tf_op args[1]
  15.8 3.3 %pad_maximum_fusion = f32[256,16,416]{0,2,1:T(8,128)S(1)} fusion(f32[256,16,32]{0,2,1:T(8,128)S(1)} %bitcast.31, f32[256,16,384]{0,2,1:T(8,128)} %bitcast.25), kind=kLoop, calls=%fused_computation.2 | loop fusion | flops 1703936 | bytes 13631488 | tf_op jit(solution)/shard_map/concatenate | solution.py:44
  19.0 0.0 copy-done
  19.1 8.6 %fusion.12 = f32[6656,512]{1,0:T(8,128)} fusion(f32[256,6656]{0,1:T(8,128)S(1)} %bitcast.24, f32[256,512]{1,0:T(8,128)S(1)} %copy-done), kind=kOutput, calls=%fused_computation.30 | convolution fusion | flops 5234491392 | bytes 20971520 | tf_op jit(solution)/shard_map/dot_general | solution.py:11
  27.7 50.9 %all-gather.4.cloned.1.call-done = bf16[512,6144]{1,0:T(8,128)(2,1)} async-done(((bf16[512,384]{1,0:T(8,128)(2,1)}), bf16[512,6144]{1,0:T(8,128)(2,1)}) %all-gather.4.cloned.1.call-update) | async-done | bytes 6291472 | tf_op jit(solution)/shard_map/all_gather | solution.py:42
  78.6 0.0 reduce-scatter.2.cloned.1.call-update
  78.6 0.2 all-gather.6.cloned.1.call-start
  78.8 144.0 %reduce-scatter.2.cloned.1.call-done = f32[416,512]{1,0:T(8,128)} async-done(((f32[6656,512]{1,0:T(8,128)}), f32[416,512]{1,0:T(8,128)}) %reduce-scatter.2.cloned.1.call-update) | async-done | bytes 851984 | tf_op jit(solution)/shard_map/reduce_scatter | solution.py:53
  222.8 0.8 reduce-precision_convert_fusion.1
  223.7 1.2 slice.63
  224.9 0.8 pad_maximum_fusion.4
  225.7 0.0 all-gather.6.cloned.1.call-update
  225.7 3.9 %reduce-precision_convert_fusion = (bf16[256,6144]{1,0:T(8,128)(2,1)S(1)}, bf16[256,6144]{1,0:T(8,128)(2,1)S(1)}) fusion(f32[256,6144]{1,0:T(8,128)} %param.4), kind=kLoop, calls=%fused_computation.1 | loop fusion | flops 6291456 | bytes 12582912 | tf_op jit(solution)/shard_map/convert_element_type | solution.py:23
  229.7 1.8 copy-done.1
  231.4 1.0 copy-done.3
  232.4 7.4 %fusion.2 = f32[512,512]{0,1:T(8,128)} fusion(bf16[512,6144]{1,0:T(8,128)(2,1)} %all-gather.4.cloned.1.call-done, bf16[256,6144]{1,0:T(8,128)(2,1)S(1)} %get-tuple-element.11, bf16[256,6144]{1,0:T(8,128)(2,1)S(1)} %get-tuple-element.10), kind=kOutput, calls=%fused_computation.6 | convolution fusion | flops 3233808384 | bytes 13631488 | tf_op jit(solution)/shard_map/dot_general | solution.py:11
  239.9 53.4 %all-gather.6.cloned.1.call-done = bf16[7168,512]{1,0:T(8,128)(2,1)} async-done(((bf16[448,512]{1,0:T(8,128)(2,1)}), bf16[7168,512]{1,0:T(8,128)(2,1)}) %all-gather.6.cloned.1.call-update) | async-done | bytes 7340048 | tf_op jit(solution)/shard_map/all_gather | solution.py:61
  293.3 1.4 convert_add_fusion
  294.7 3.6 %slice.42 = bf16[16,384,512]{2,1,0:T(8,128)(2,1)S(1)} slice(bf16[16,448,512]{2,1,0:T(8,128)(2,1)} %bitcast.27), slice={[0:16], [0:384], [0:512]} | slice | bytes 12582912 | tf_op jit(solution)/shard_map/slice | solution.py:62
  298.3 0.1 copy-done.2
  298.4 5.3 %fusion.1 = f32[512,512]{0,1:T(8,128)S(1)} fusion(bf16[6144,512]{1,0:T(8,128)(2,1)S(1)} %bitcast.28, bf16[256,6144]{1,0:T(8,128)(2,1)} %copy-done.3, bf16[256,6144]{1,0:T(8,128)(2,1)S(1)} %copy-done.2), kind=kOutput, calls=%fused_computation.5 | convolution fusion | flops 3233808384 | bytes 13631488 | tf_op jit(solution)/shard_map/dot_general | solution.py:11
  303.7 0.0 copy-start.5
  303.7 0.0 copy-start.4
  303.7 8.6 %fusion.3 = f32[512,512]{1,0:T(8,128)S(1)} fusion(bf16[512,6144]{1,0:T(8,128)(2,1)} %all-gather.4.cloned.1.call-done, f32[512,512]{1,0:T(8,128)S(1)} %bitcast.29, f32[512]{0:T(512)S(1)} %convert_add_fusion.1), kind=kOutput, calls=%fused_computation.8 | convolution fusion | flops 3222536192 | bytes 8390656 | tf_op jit(solution)/shard_map/dot_general | solution.py:11
  312.4 1.0 fusion.6
  313.4 1.0 copy.19
  314.4 1.6 fusion.4
  316.0 1.1 copy.20
  (8 shorter events, 0.0 us)
Async XLA Ops:
  7.2 71.4 %all-gather.4.cloned.1.call-start = ((), (), s32[]{:S(2)}) async-start(), calls=%async_computation.1 | async-start | bytes 6684672 | tf_op jit(solution)/shard_map/all_gather | solution.py:42
  7.9 214.9 %reduce-scatter.2.cloned.1.call-start = ((), (), s32[]{:S(2)}) async-start(), calls=%async_computation.2 | async-start | bytes 14483456 | tf_op jit(solution)/shard_map/reduce_scatter | solution.py:53
  15.8 3.3 %copy-start = (f32[256,512]{1,0:T(8,128)S(1)}, f32[256,512]{1,0:T(8,128)}, u32[]{:S(2)}) copy-start(f32[256,512]{1,0:T(8,128)} %param.3) | copy-start | bytes 1572868
  78.6 214.7 %all-gather.6.cloned.1.call-start = ((), (), s32[]{:S(2)}) async-start(), calls=%async_computation.3 | async-start | bytes 7798784 | tf_op jit(solution)/shard_map/all_gather | solution.py:61
  229.7 1.8 copy-start.1
  229.7 2.7 copy-start.3
  294.7 3.7 %copy-start.2 = (bf16[256,6144]{1,0:T(8,128)(2,1)S(1)}, bf16[256,6144]{1,0:T(8,128)(2,1)}, u32[]{:S(2)}) copy-start(bf16[256,6144]{1,0:T(8,128)(2,1)} %copy-done.1) | copy-start | bytes 9437188
  303.7 8.6 %copy-start.5 = (f32[512,512]{0,1:T(8,128)S(1)}, f32[512,512]{0,1:T(8,128)}, u32[]{:S(2)}) copy-start(f32[512,512]{0,1:T(8,128)} %fusion.2) | copy-start | bytes 3145732
  303.7 10.7 %copy-start.4 = (f32[416,512]{1,0:T(8,128)S(1)}, f32[416,512]{1,0:T(8,128)}, u32[]{:S(2)}) copy-start(f32[416,512]{1,0:T(8,128)} %reduce-scatter.2.cloned.1.call-done) | copy-start | bytes 2555908
Sparse Core Ops, SparseCore 0:
  10.2 68.3 all-gather.3
  82.7 140.1 reduce-scatter.1
  225.9 67.3 all-gather.5

commit v11 on v10

--- a/solution.py
+++ b/solution.py
@@ -58,6 +58,14 @@
     packed = jnp.concatenate(
         [cross_here.astype(jnp.bfloat16), moment_high, moment_low], axis=0
     )
+    gram_heads = contract(heads_all, heads_all, 1, 1, lax.Precision.DEFAULT)
+    teacher_high, teacher_low = split_bf16(teacher)
+    teacher_pair = jnp.concatenate([teacher_high, teacher_low], axis=0)
+    teacher_heads = contract(teacher_pair, heads_all, 1, 1, lax.Precision.DEFAULT)
+    teacher_heads = teacher_heads[:rows_here] + teacher_heads[rows_here:]
+    gram_heads, teacher_heads, packed = lax.optimization_barrier(
+        (gram_heads, teacher_heads, packed)
+    )
     gathered = lax.all_gather(packed, "rows", axis=0, tiled=False)
     cross_low = gathered[:, :f_here].reshape(teacher_width, model_width)
     moment = (
@@ -69,11 +77,6 @@
         contract(moment, heads.astype(jnp.float32), 1, 0, lax.Precision.HIGH) - cross_here.T
     )
 
-    gram_heads = contract(heads_all, heads_all, 1, 1, lax.Precision.DEFAULT)
-    teacher_high, teacher_low = split_bf16(teacher)
-    teacher_pair = jnp.concatenate([teacher_high, teacher_low], axis=0)
-    teacher_heads = contract(teacher_pair, heads_all, 1, 1, lax.Precision.DEFAULT)
-    teacher_heads = teacher_heads[:rows_here] + teacher_heads[rows_here:]
     teacher_cross = contract(teacher_pair, cross_low, 1, 0, lax.Precision.DEFAULT)
     teacher_cross = teacher_cross[:rows_here] + teacher_cross[rows_here:]
     student_side = reg_weight * gram_heads + gram_scale * (moment * nested)

time: 324 us -> 315 us (0.972)
  matrix products: 32.6 us -> 24.6 us
  local copies, waits for them, and re-layouts: 17.6 us -> 13.2 us
    all_gather x1, waiting for transfers between devices: 53.4 us -> 67.6 us  [per_device(): gathered = lax.all_gather(packed, 'rows', axis=0, tiled=False)]
    reduce_scatter x1, waiting for transfers between devices: 144 us -> 131 us  [per_device(): reduced = lax.psum_scatter(partial, 'rows', scatter_dimension=0, tiled=True)]
    dot_general x6, matrix products: 32.6 us -> 24.6 us  [contract(): lax.dot_general(left, right, (((left_dim,), (right_dim,)), ((), ())), pre...]
    unnamed x16 -> x19, local copies, waits for them, and re-layouts: 12.8 us -> 8.49 us
where the time goes in v11:
time: 315 us; the launch traced here: 314 us
  waiting for transfers between devices  252 us (80%)
  matrix products  24.6 us (8%)
  between operations  13.9 us (4%)
  local copies, waits for them, and re-layouts  13.2 us (4%)
  other arithmetic  10.5 us (3%)
    reduce_scatter x1, waiting for transfers between devices, per_device(): reduced = lax.psum_scatter(partial, 'rows', scatter_dimension=0, tiled=True)  131 us
    all_gather x1, waiting for transfers between devices, per_device(): gathered = lax.all_gather(packed, 'rows', axis=0, tiled=False)  67.6 us
    all_gather x1, waiting for transfers between devices, per_device(): heads_all = lax.all_gather(heads, 'rows', axis=1, tiled=True)  52 us
    dot_general x6, matrix products, contract(): lax.dot_general(left, right, (((left_dim,), (right_dim,)), ((), ())), pre...  24.6 us
    unnamed x19, local copies, waits for them, and re-layouts  8.49 us
  transfers between devices with their start and end apart: 3, of which 3 were waited for; matrix products, arithmetic and copies ran while one was open for 10% of the time, Pallas kernels for 0%

profile of v11, /device:TPU:0, one launch (start us, length us, event | category | flops | bytes accessed | tf_op | source)
XLA Modules:
  0.0 314.3 jit_solution(13169245265462521568)
XLA Ops:
  7.2 0.0 all-gather.4.cloned.1.call-start
  7.2 0.7 all-gather.4.cloned.1.call-update
  7.9 0.0 reduce-scatter.2.cloned.1.call-start
  8.0 6.6 %copy.8 = f32[256,6144]{0,1:T(8,128)} copy(f32[256,6144]{1,0:T(8,128)} %param.4) | data formatting | bytes 12582912 | tf_op args[1]
  14.6 0.0 copy-done
  14.6 0.2 copy.9
  14.8 3.2 %pad_maximum_fusion = f32[256,16,416]{0,2,1:T(8,128)S(1)} fusion(f32[256,16,32]{0,2,1:T(8,128)S(1)} %bitcast.30, f32[256,16,384]{0,2,1:T(8,128)} %bitcast.24), kind=kLoop, calls=%fused_computation.2 | loop fusion | flops 1703936 | bytes 13631488 | tf_op jit(solution)/shard_map/concatenate | solution.py:44
  18.0 8.6 %fusion.21 = f32[6656,512]{1,0:T(8,128)} fusion(f32[256,6656]{0,1:T(8,128)S(1)} %bitcast.23, f32[256,512]{1,0:T(8,128)S(1)} %copy-done), kind=kOutput, calls=%fused_computation.38 | convolution fusion | flops 5234491392 | bytes 20971520 | tf_op jit(solution)/shard_map/dot_general | solution.py:11
  26.6 52.0 %all-gather.4.cloned.1.call-done = bf16[512,6144]{1,0:T(8,128)(2,1)} async-done(((bf16[512,384]{1,0:T(8,128)(2,1)}), bf16[512,6144]{1,0:T(8,128)(2,1)}) %all-gather.4.cloned.1.call-update) | async-done | bytes 6291472 | tf_op jit(solution)/shard_map/all_gather | solution.py:42
  78.6 0.0 reduce-scatter.2.cloned.1.call-update
  78.6 0.2 all-gather.6.cloned.1.call-start
  78.8 4.1 %reduce-precision_convert_fusion = (bf16[256,6144]{1,0:T(8,128)(2,1)S(1)}, bf16[256,6144]{1,0:T(8,128)(2,1)S(1)}) fusion(f32[256,6144]{1,0:T(8,128)} %param.4), kind=kLoop, calls=%fused_computation.1 | loop fusion | flops 6291456 | bytes 12582912 | tf_op jit(solution)/shard_map/convert_element_type | solution.py:23
  82.9 0.5 copy-done.7
  83.4 3.4 %fusion.2 = f32[512,512]{1,0:T(8,128)S(1)} fusion(bf16[512,6144]{1,0:T(8,128)(2,1)S(1)} %copy-done.7, bf16[256,6144]{1,0:T(8,128)(2,1)S(1)} %get-tuple-element.17, bf16[256,6144]{1,0:T(8,128)(2,1)S(1)} %get-tuple-element.16), kind=kOutput, calls=%fused_computation.6 | convolution fusion | flops 3233808384 | bytes 13631488 | tf_op jit(solution)/shard_map/dot_general | solution.py:11
  86.9 0.1 slice_add_fusion.1
  87.0 4.4 %fusion.22 = f32[512,512]{1,0:T(8,128)} fusion(bf16[512,6144]{1,0:T(8,128)(2,1)S(1)} %copy-done.7), kind=kOutput, calls=%fused_computation.39 | convolution fusion | flops 3221225472 | bytes 7340032 | tf_op jit(solution)/shard_map/dot_general | solution.py:11
  91.4 131.5 %reduce-scatter.2.cloned.1.call-done = f32[416,512]{1,0:T(8,128)} async-done(((f32[6656,512]{1,0:T(8,128)}), f32[416,512]{1,0:T(8,128)}) %reduce-scatter.2.cloned.1.call-update) | async-done | bytes 851984 | tf_op jit(solution)/shard_map/reduce_scatter | solution.py:53
  222.8 0.8 reduce-precision_convert_fusion.1
  223.7 1.2 slice.59
  224.9 0.8 pad_maximum_fusion.4
  225.7 0.0 all-gather.6.cloned.1.call-update
  225.7 67.6 %all-gather.6.cloned.1.call-done = bf16[7168,512]{1,0:T(8,128)(2,1)} async-done(((bf16[448,512]{1,0:T(8,128)(2,1)}), bf16[7168,512]{1,0:T(8,128)(2,1)}) %all-gather.6.cloned.1.call-update) | async-done | bytes 7340048 | tf_op jit(solution)/shard_map/all_gather | solution.py:69
  293.3 3.6 %slice.42 = bf16[16,384,512]{2,1,0:T(8,128)(2,1)S(1)} slice(bf16[16,448,512]{2,1,0:T(8,128)(2,1)} %bitcast.27), slice={[0:16], [0:384], [0:512]} | slice | bytes 12582912 | tf_op jit(solution)/shard_map/slice | solution.py:70
  296.9 1.4 convert_add_fusion
  298.3 0.0 copy-done.2
  298.3 0.0 copy-done.4
  298.4 0.0 copy-start.5
  298.4 0.0 copy-start.6
  298.4 4.4 %fusion.1 = f32[512,512]{1,0:T(8,128)} fusion(bf16[6144,512]{1,0:T(8,128)(2,1)S(1)} %bitcast.29, bf16[256,6144]{1,0:T(8,128)(2,1)S(1)} %copy-done.4, bf16[256,6144]{1,0:T(8,128)(2,1)S(1)} %copy-done.2), kind=kOutput, calls=%fused_computation.5 | convolution fusion | flops 3233808384 | bytes 13631488 | tf_op jit(solution)/shard_map/dot_general | solution.py:11
  302.8 0.7 fusion.3
  303.5 1.1 copy.12
  304.6 3.2 %fusion.5 = f32[256,512]{1,0:T(8,128)} fusion(f32[256,512]{1,0:T(8,128)S(1)} %copy-done, f32[512,512]{1,0:T(8,128)S(1)} %bitcast.26, f32[512,512]{1,0:T(8,128)} %fusion.22, f32[512,512]{1,0:T(8,128)} %fusion.1, f32[256,512]{1,0:T(8,128)S(1)} %slice_add_fusion.1, f32[512]{0:T(512)S(1)} %get-tuple-element.20, f32[512]{0:T(512)S(1)} %get-tuple-element.21), kind=kOutput, calls=%fused_computation.11 | convolution fusion | flops 404619264 | bytes 4724736 | tf_op jit(solution)/shard_map/dot_general | solution.py:11
  (11 shorter events, 0.0 us)
Async XLA Ops:
  7.2 71.4 %all-gather.4.cloned.1.call-start = ((), (), s32[]{:S(2)}) async-start(), calls=%async_computation.1 | async-start | bytes 6684672 | tf_op jit(solution)/shard_map/all_gather | solution.py:42
  7.9 6.7 %copy-start = (f32[256,512]{1,0:T(8,128)S(1)}, f32[256,512]{1,0:T(8,128)}, u32[]{:S(2)}) copy-start(f32[256,512]{1,0:T(8,128)} %param.3) | copy-start | bytes 1572868
  7.9 214.9 %reduce-scatter.2.cloned.1.call-start = ((), (), s32[]{:S(2)}) async-start(), calls=%async_computation.2 | async-start | bytes 14483456 | tf_op jit(solution)/shard_map/reduce_scatter | solution.py:53
  78.6 214.7 %all-gather.6.cloned.1.call-start = ((), (), s32[]{:S(2)}) async-start(), calls=%async_computation.3 | async-start | bytes 7798784 | tf_op jit(solution)/shard_map/all_gather | solution.py:69
  78.8 4.6 %copy-start.7 = (bf16[512,6144]{1,0:T(8,128)(2,1)S(1)}, bf16[512,6144]{1,0:T(8,128)(2,1)}, u32[]{:S(2)}) copy-start(bf16[512,6144]{1,0:T(8,128)(2,1)} %all-gather.4.cloned.1.call-done) | copy-start | bytes 18874372
  82.9 3.9 %copy-start.1 = (bf16[256,6144]{1,0:T(8,128)(2,1)}, bf16[256,6144]{1,0:T(8,128)(2,1)S(1)}, u32[]{:S(2)}) copy-start(bf16[256,6144]{1,0:T(8,128)(2,1)S(1)} %get-tuple-element.16) | copy-start | bytes 9437188
  82.9 3.9 %copy-start.3 = (bf16[256,6144]{1,0:T(8,128)(2,1)}, bf16[256,6144]{1,0:T(8,128)(2,1)S(1)}, u32[]{:S(2)}) copy-start(bf16[256,6144]{1,0:T(8,128)(2,1)S(1)} %get-tuple-element.17) | copy-start | bytes 9437188
  293.3 5.0 %copy-start.2 = (bf16[256,6144]{1,0:T(8,128)(2,1)S(1)}, bf16[256,6144]{1,0:T(8,128)(2,1)}, u32[]{:S(2)}) copy-start(bf16[256,6144]{1,0:T(8,128)(2,1)} %copy-done.1) | copy-start | bytes 9437188
  293.3 5.0 %copy-start.4 = (bf16[256,6144]{1,0:T(8,128)(2,1)S(1)}, bf16[256,6144]{1,0:T(8,128)(2,1)}, u32[]{:S(2)}) copy-start(bf16[256,6144]{1,0:T(8,128)(2,1)} %copy-done.3) | copy-start | bytes 9437188
  298.4 4.4 %copy-start.5 = (f32[416,512]{1,0:T(8,128)S(1)}, f32[416,512]{1,0:T(8,128)}, u32[]{:S(2)}) copy-start(f32[416,512]{1,0:T(8,128)} %reduce-scatter.2.cloned.1.call-done) | copy-start | bytes 2555908
  298.4 4.4 %copy-start.6 = (bf16[512,384]{1,0:T(8,128)(2,1)S(1)}, bf16[512,384]{1,0:T(8,128)(2,1)}, u32[]{:S(2)}) copy-start(bf16[512,384]{1,0:T(8,128)(2,1)} %param.5) | copy-start | bytes 1179652
Sparse Core Ops, SparseCore 0:
  10.2 68.3 all-gather.3
  82.7 140.1 reduce-scatter.1
  225.9 67.3 all-gather.5

commit v12 on v11

--- a/solution.py
+++ b/solution.py
@@ -39,7 +39,10 @@
     nested = jnp.minimum(weights[:, None], weights[None, :])
     gram_scale = 0.5 / total_rows
 
-    heads_all = lax.all_gather(heads, "rows", axis=1, tiled=True)
+    group = lax.axis_index("groups")
+    half = heads.shape[1] // 2
+    mine = lax.dynamic_slice_in_dim(heads, group * half, half, axis=1)
+    mine = lax.all_gather(mine, "rows", axis=0, tiled=False)
 
     left = jnp.concatenate(
         [
@@ -49,7 +52,13 @@
         axis=2,
     ).reshape(rows_here, devices * (f_here + d_here))
     partial = contract(left, student, 0, 0, lax.Precision.HIGH)
-    heads_all, partial = lax.optimization_barrier((heads_all, partial))
+    mine, partial = lax.optimization_barrier((mine, partial))
+    theirs = lax.ppermute(mine, "groups", [(0, 1), (1, 0)])
+    first = group == 0
+    heads_all = jnp.stack(
+        [jnp.where(first, mine, theirs), jnp.where(first, theirs, mine)], axis=1
+    )
+    heads_all = heads_all.transpose(2, 0, 1, 3).reshape(model_width, teacher_width)
     reduced = lax.psum_scatter(partial, "rows", scatter_dimension=0, tiled=True)
     cross_here = reduced[:f_here]
     moment_here = reduced[f_here:]

time: 315 us -> 304 us (0.965)
  waiting for transfers between devices: 252 us -> 217 us
  local copies, waits for them, and re-layouts: 13.2 us -> 27.5 us
  other arithmetic: 10.5 us -> 18.6 us
    reduce_scatter x1, waiting for transfers between devices: 131 us -> 51.1 us  [per_device(): reduced = lax.psum_scatter(partial, 'rows', scatter_dimension=0, tiled=True)]
    ppermute x0 -> x1, waiting for transfers between devices: none -> 62.8 us  [per_device(): theirs = lax.ppermute(mine, 'groups', [(0, 1), (1, 0)])]
    all_gather x1, waiting for transfers between devices: 52 us -> 35.2 us  [per_device(): mine = lax.all_gather(mine, 'rows', axis=0, tiled=False)]
    all_gather x0 -> x1, local copies, waits for them, and re-layouts: none -> 6.1 us  [per_device(): mine = lax.all_gather(mine, 'rows', axis=0, tiled=False)]
    another operation x0 -> x2, other arithmetic: none -> 5.96 us  [per_device(): jnp.stack([jnp.where(first, mine, theirs), jnp.where(first, theirs, mine)...]
    unnamed x19, local copies, waits for them, and re-layouts: 8.49 us -> 12.1 us
    optimization_barrier x0 -> x1, local copies, waits for them, and re-layouts: none -> 3.45 us  [per_device(): mine, partial = lax.optimization_barrier((mine, partial))]
  transfers between devices with their start and end apart: 3 -> 4, of which waited for: 3 -> 4; matrix products, arithmetic and copies ran while one was open for 10% -> 14% of each run, Pallas kernels for 0% -> 0%
where the time goes in v12:
time: 304 us; the launch traced here: 303 us
  waiting for transfers between devices  217 us (71%)
  local copies, waits for them, and re-layouts  27.5 us (9%)
  matrix products  24.6 us (8%)
  other arithmetic  18.6 us (6%)
  between operations  13.9 us (5%)
    all_gather x1, waiting for transfers between devices, per_device(): gathered = lax.all_gather(packed, 'rows', axis=0, tiled=False)  67.6 us
    ppermute x1, waiting for transfers between devices, per_device(): theirs = lax.ppermute(mine, 'groups', [(0, 1), (1, 0)])  62.8 us
    reduce_scatter x1, waiting for transfers between devices, per_device(): reduced = lax.psum_scatter(partial, 'rows', scatter_dimension=0, tiled=True)  51.1 us
    all_gather x1, waiting for transfers between devices, per_device(): mine = lax.all_gather(mine, 'rows', axis=0, tiled=False)  35.2 us
    dot_general x6, matrix products, contract(): lax.dot_general(left, right, (((left_dim,), (right_dim,)), ((), ())), pre...  24.6 us
    unnamed x19, local copies, waits for them, and re-layouts  12.1 us
    convert_element_type x2, other arithmetic, split_bf16(): return (high.astype(jnp.bfloat16), low)  7.13 us
    all_gather x1, local copies, waits for them, and re-layouts, per_device(): mine = lax.all_gather(mine, 'rows', axis=0, tiled=False)  6.1 us
  transfers between devices with their start and end apart: 4, of which 4 were waited for; matrix products, arithmetic and copies ran while one was open for 14% of the time, Pallas kernels for 0%

profile of v12, /device:TPU:0, one launch (start us, length us, event | category | flops | bytes accessed | tf_op | source)
XLA Modules:
  0.0 303.2 jit_solution(15126685521905204255)
XLA Ops:
  7.2 0.9 copy-done
  8.2 0.8 constant_dynamic-slice_fusion
  9.0 0.0 reduce-scatter.2.cloned.1.call-start
  9.1 1.2 copy.11
  10.3 6.6 %copy.10 = f32[256,6144]{0,1:T(8,128)} copy(f32[256,6144]{1,0:T(8,128)} %param.4) | data formatting | bytes 12582912 | tf_op args[1]
  16.9 3.3 %pad_maximum_fusion = f32[256,16,416]{0,2,1:T(8,128)S(1)} fusion(f32[256,16,32]{0,2,1:T(8,128)S(1)} %bitcast.48, f32[256,16,384]{0,2,1:T(8,128)} %bitcast.40), kind=kLoop, calls=%fused_computation.2 | loop fusion | flops 1703936 | bytes 13631488 | tf_op jit(solution)/shard_map/concatenate | solution.py:47
  20.2 8.6 %fusion.26 = f32[6656,512]{1,0:T(8,128)} fusion(f32[256,6656]{0,1:T(8,128)S(1)} %bitcast.39, f32[256,512]{1,0:T(8,128)S(1)} %copy-done.1), kind=kOutput, calls=%fused_computation.45 | convolution fusion | flops 5234491392 | bytes 20971520 | tf_op jit(solution)/shard_map/dot_general | solution.py:11
  28.8 35.2 %all-gather.5.cloned.1.call-done = bf16[8192,192]{1,0:T(8,128)(2,1)} async-done(((bf16[512,192]{1,0:T(8,128)(2,1)}), bf16[8192,192]{1,0:T(8,128)(2,1)}) %all-gather.5.cloned.1.call-update) | async-done | bytes 3145744 | tf_op jit(solution)/shard_map/all_gather | solution.py:45
  64.0 6.1 %copy.22 = bf16[16,512,192]{1,0,2:T(8,128)(2,1)S(1)} copy(bf16[16,512,192]{2,1,0:T(8,128)(2,1)} %bitcast.47) | data formatting | bytes 6291456 | tf_op jit(solution)/shard_map/all_gather | solution.py:45
  70.2 0.2 all-gather.7.cloned.1.call-start
  70.4 3.5 %copy.13 = bf16[16,512,192]{1,2,0:T(8,128)(2,1)} copy(bf16[16,512,192]{1,0,2:T(8,128)(2,1)S(1)} %copy.22) | data formatting | bytes 6291456 | tf_op jit(solution)/shard_map/optimization_barrier | solution.py:55
  73.9 1.5 collective-permute-start
  75.3 6.3 %reduce-precision_convert_fusion = (bf16[256,6144]{1,0:T(8,128)(2,1)S(1)}, bf16[256,6144]{1,0:T(8,128)(2,1)}) fusion(f32[256,6144]{1,0:T(8,128)} %param.4), kind=kLoop, calls=%fused_computation.1 | loop fusion | flops 6291456 | bytes 12582912 | tf_op jit(solution)/shard_map/convert_element_type | solution.py:23
  81.6 62.8 %collective-permute-done = bf16[16,512,192]{1,2,0:T(8,128)(2,1)} collective-permute-done((bf16[16,512,192]{1,2,0:T(8,128)(2,1)}, bf16[16,512,192]{1,2,0:T(8,128)(2,1)}, u32[]{:S(2)}, u32[]{:S(2)}) %collective-permute-start) | collective-permute-done | bytes 3145760 | tf_op jit(solution)/shard_map/ppermute | solution.py:56
  144.4 5.4 %select_bitcast_fusion.1 = (bf16[16,1,512,192]{2,3,1,0:T(8,128)(2,1)S(1)}, bf16[16,1,512,192]{2,3,1,0:T(8,128)(2,1)S(1)}) fusion(bf16[16,512,192]{1,2,0:T(8,128)(2,1)} %collective-permute-done, pred[]{:T(512)S(6)} %eq.3, bf16[16,512,192]{1,0,2:T(8,128)(2,1)S(1)} %copy.22), kind=kLoop, calls=%fused_computation.11 | loop fusion | flops 3145728 | bytes 12582913 | tf_op jit(solution)/shard_map/stack | solution.py:58
  149.8 0.6 pad_maximum_fusion.1
  150.4 1.3 copy-done.5
  151.8 3.4 %fusion.4 = f32[512,512]{1,0:T(8,128)S(1)} fusion(bf16[512,6144]{0,1:T(8,128)(2,1)S(1)} %bitcast.46, bf16[256,6144]{1,0:T(8,128)(2,1)S(1)} %copy-done.5, bf16[256,6144]{1,0:T(8,128)(2,1)S(1)} %get-tuple-element.16), kind=kOutput, calls=%fused_computation.9 | convolution fusion | flops 3233808384 | bytes 13631488 | tf_op jit(solution)/shard_map/dot_general | solution.py:11
  155.2 0.1 slice_add_fusion.1
  155.3 4.4 %fusion.5 = f32[512,512]{1,0:T(8,128)} fusion(bf16[16,1,512,192]{2,3,1,0:T(8,128)(2,1)S(1)} %get-tuple-element.19, bf16[16,1,512,192]{2,3,1,0:T(8,128)(2,1)S(1)} %get-tuple-element.18), kind=kOutput, calls=%fused_computation.12 | convolution fusion | flops 3224371200 | bytes 7340032 | tf_op jit(solution)/shard_map/dot_general | solution.py:11
  159.7 51.1 %reduce-scatter.2.cloned.1.call-done = f32[416,512]{1,0:T(8,128)} async-done(((f32[6656,512]{1,0:T(8,128)}), f32[416,512]{1,0:T(8,128)}) %reduce-scatter.2.cloned.1.call-update) | async-done | bytes 851984 | tf_op jit(solution)/shard_map/reduce_scatter | solution.py:62
  210.8 0.8 reduce-precision_convert_fusion.1
  211.7 1.2 slice.59
  212.8 0.8 pad_maximum_fusion.5
  213.7 67.6 %all-gather.7.cloned.1.call-done = bf16[7168,512]{1,0:T(8,128)(2,1)} async-done(((bf16[448,512]{1,0:T(8,128)(2,1)}), bf16[7168,512]{1,0:T(8,128)(2,1)}) %all-gather.7.cloned.1.call-update) | async-done | bytes 7340048 | tf_op jit(solution)/shard_map/all_gather | solution.py:78
  281.3 1.4 convert_add_fusion
  282.7 3.8 %slice.42 = bf16[16,384,512]{2,1,0:T(8,128)(2,1)S(1)} slice(bf16[16,448,512]{2,1,0:T(8,128)(2,1)} %bitcast.44), slice={[0:16], [0:384], [0:512]} | slice | bytes 12582912 | tf_op jit(solution)/shard_map/slice | solution.py:79
  286.5 0.8 copy-done.6
  287.3 4.4 %fusion.3 = f32[512,512]{1,0:T(8,128)} fusion(bf16[6144,512]{1,0:T(8,128)(2,1)S(1)} %bitcast.45, bf16[256,6144]{1,0:T(8,128)(2,1)S(1)} %copy-done.6, bf16[256,6144]{1,0:T(8,128)(2,1)S(1)} %copy-done.4), kind=kOutput, calls=%fused_computation.8 | convolution fusion | flops 3233808384 | bytes 13631488 | tf_op jit(solution)/shard_map/dot_general | solution.py:11
  291.7 0.7 fusion.8
  292.4 1.1 copy.18
  293.5 3.2 %fusion.10 = f32[256,512]{1,0:T(8,128)} fusion(f32[256,512]{1,0:T(8,128)S(1)} %copy-done.2, f32[512,512]{1,0:T(8,128)S(1)} %bitcast.42, f32[512,512]{1,0:T(8,128)} %fusion.5, f32[512,512]{1,0:T(8,128)} %fusion.3, f32[256,512]{1,0:T(8,128)S(1)} %slice_add_fusion.1, f32[512]{0:T(512)S(1)} %get-tuple-element.22, f32[512]{0:T(512)S(1)} %get-tuple-element.23), kind=kOutput, calls=%fused_computation.17 | convolution fusion | flops 404619264 | bytes 4724736 | tf_op jit(solution)/shard_map/dot_general | solution.py:11
  (18 shorter events, 0.1 us)
Async XLA Ops:
  7.2 1.0 copy-start
  7.2 56.9 %all-gather.5.cloned.1.call-start = ((), (), s32[]{:S(2)}) async-start(), calls=%async_computation.2 | async-start | bytes 4456448 | tf_op jit(solution)/shard_map/all_gather | solution.py:45
  9.0 201.8 %reduce-scatter.2.cloned.1.call-start = ((), (), s32[]{:S(2)}) async-start(), calls=%async_computation.1 | async-start | bytes 14483456 | tf_op jit(solution)/shard_map/reduce_scatter | solution.py:62
  16.9 3.3 %copy-start.1 = (f32[256,512]{1,0:T(8,128)S(1)}, f32[256,512]{1,0:T(8,128)}, u32[]{:S(2)}) copy-start(f32[256,512]{1,0:T(8,128)} %param.3) | copy-start | bytes 1572868
  70.2 211.1 %all-gather.7.cloned.1.call-start = ((), (), s32[]{:S(2)}) async-start(), calls=%async_computation.3 | async-start | bytes 7798784 | tf_op jit(solution)/shard_map/all_gather | solution.py:78
  73.9 70.6 %collective-permute-start = (bf16[16,512,192]{1,2,0:T(8,128)(2,1)}, bf16[16,512,192]{1,2,0:T(8,128)(2,1)}, u32[]{:S(2)}, u32[]{:S(2)}) collective-permute-start(bf16[16,512,192]{1,2,0:T(8,128)(2,1)} %copy.13), channel_id=1, source_target_pairs={{0,16},{16,0},{1,17},{17,1},{2,18},{18,2},{3,19},{19,3},{4,20},{20... | collective-permute-start | bytes 9437192 | tf_op jit(solution)/shard_map/ppermute | solution.py:56
  81.6 68.8 %copy-start.3 = (bf16[256,6144]{1,0:T(8,128)(2,1)}, bf16[256,6144]{1,0:T(8,128)(2,1)S(1)}, u32[]{:S(2)}) copy-start(bf16[256,6144]{1,0:T(8,128)(2,1)S(1)} %get-tuple-element.16) | copy-start | bytes 9437188
  149.8 1.9 copy-start.5
  282.7 3.8 %copy-start.4 = (bf16[256,6144]{1,0:T(8,128)(2,1)S(1)}, bf16[256,6144]{1,0:T(8,128)(2,1)}, u32[]{:S(2)}) copy-start(bf16[256,6144]{1,0:T(8,128)(2,1)} %copy-done.3) | copy-start | bytes 9437188
  282.7 4.7 %copy-start.6 = (bf16[256,6144]{1,0:T(8,128)(2,1)S(1)}, bf16[256,6144]{1,0:T(8,128)(2,1)}, u32[]{:S(2)}) copy-start(bf16[256,6144]{1,0:T(8,128)(2,1)} %get-tuple-element.17) | copy-start | bytes 9437188
  287.3 4.4 %copy-start.7 = (f32[416,512]{1,0:T(8,128)S(1)}, f32[416,512]{1,0:T(8,128)}, u32[]{:S(2)}) copy-start(f32[416,512]{1,0:T(8,128)} %reduce-scatter.2.cloned.1.call-done) | copy-start | bytes 2555908
  287.3 6.2 %copy-start.2 = (f32[256,512]{1,0:T(8,128)S(1)}, f32[256,512]{1,0:T(8,128)}, u32[]{:S(2)}) copy-start(f32[256,512]{1,0:T(8,128)} %param.3) | copy-start | bytes 1572868
Sparse Core Ops, SparseCore 0:
  10.7 53.2 all-gather.4
  70.3 140.4 reduce-scatter.1
  213.9 67.3 all-gather.6

commit v13 on v12

--- a/solution.py
+++ b/solution.py
@@ -40,8 +40,8 @@
     gram_scale = 0.5 / total_rows
 
     group = lax.axis_index("groups")
-    half = heads.shape[1] // 2
-    mine = lax.dynamic_slice_in_dim(heads, group * half, half, axis=1)
+    half = f_here // 2
+    mine = lax.dynamic_slice_in_dim(heads.T, group * half, half, axis=0)
     mine = lax.all_gather(mine, "rows", axis=0, tiled=False)
 
     left = jnp.concatenate(
@@ -55,10 +55,15 @@
     mine, partial = lax.optimization_barrier((mine, partial))
     theirs = lax.ppermute(mine, "groups", [(0, 1), (1, 0)])
     first = group == 0
-    heads_all = jnp.stack(
-        [jnp.where(first, mine, theirs), jnp.where(first, theirs, mine)], axis=1
-    )
-    heads_all = heads_all.transpose(2, 0, 1, 3).reshape(model_width, teacher_width)
+    d_here = model_width // devices
+    heads_all = jnp.concatenate(
+        [
+            jnp.where(first, mine, theirs),
+            jnp.where(first, theirs, mine),
+            jnp.zeros((devices, 2 * d_here, model_width), mine.dtype),
+        ],
+        axis=1,
+    ).reshape(devices * (f_here + 2 * d_here), model_width)
     reduced = lax.psum_scatter(partial, "rows", scatter_dimension=0, tiled=True)
     cross_here = reduced[:f_here]
     moment_here = reduced[f_here:]
@@ -67,16 +72,18 @@
     packed = jnp.concatenate(
         [cross_here.astype(jnp.bfloat16), moment_high, moment_low], axis=0
     )
-    gram_heads = contract(heads_all, heads_all, 1, 1, lax.Precision.DEFAULT)
+    gram_heads = contract(heads_all, heads_all, 0, 0, lax.Precision.DEFAULT)
     teacher_high, teacher_low = split_bf16(teacher)
     teacher_pair = jnp.concatenate([teacher_high, teacher_low], axis=0)
-    teacher_heads = contract(teacher_pair, heads_all, 1, 1, lax.Precision.DEFAULT)
+    teacher_pair = jnp.pad(
+        teacher_pair.reshape(2 * rows_here, devices, f_here), ((0, 0), (0, 0), (0, 2 * d_here))
+    ).reshape(2 * rows_here, devices * (f_here + 2 * d_here))
+    teacher_heads = contract(teacher_pair, heads_all, 1, 0, lax.Precision.DEFAULT)
     teacher_heads = teacher_heads[:rows_here] + teacher_heads[rows_here:]
     gram_heads, teacher_heads, packed = lax.optimization_barrier(
         (gram_heads, teacher_heads, packed)
     )
     gathered = lax.all_gather(packed, "rows", axis=0, tiled=False)
-    cross_low = gathered[:, :f_here].reshape(teacher_width, model_width)
     moment = (
         gathered[:, f_here : f_here + d_here].astype(jnp.float32)
         + gathered[:, f_here + d_here :].astype(jnp.float32)
@@ -86,7 +93,9 @@
         contract(moment, heads.astype(jnp.float32), 1, 0, lax.Precision.HIGH) - cross_here.T
     )
 
-    teacher_cross = contract(teacher_pair, cross_low, 1, 0, lax.Precision.DEFAULT)
+    teacher_cross = contract(
+        teacher_pair, gathered.reshape(-1, model_width), 1, 0, lax.Precision.DEFAULT
+    )
     teacher_cross = teacher_cross[:rows_here] + teacher_cross[rows_here:]
     student_side = reg_weight * gram_heads + gram_scale * (moment * nested)
     grad_student = (

time: 304 us -> 298 us (0.980)
  matrix products: 24.6 us -> 31.8 us
  local copies, waits for them, and re-layouts: 27.5 us -> 21.1 us
  waiting for transfers between devices: 217 us -> 212 us
    reduce_scatter x1, waiting for transfers between devices: 51.1 us -> 61.4 us  [per_device(): reduced = lax.psum_scatter(partial, 'rows', scatter_dimension=0, tiled=True)]
    ppermute x1, waiting for transfers between devices: 62.8 us -> 52.7 us  [per_device(): theirs = lax.ppermute(mine, 'groups', [(0, 1), (1, 0)])]
    concatenate x0 -> x2, local copies, waits for them, and re-layouts: none -> 8.99 us  [the longest x1 8.98 us: per_device(): teacher_pair = jnp.concatenate([teacher_high, teacher_low], axis=0)]
    dot_general x6, matrix products: 24.6 us -> 31.8 us  [contract(): lax.dot_general(left, right, (((left_dim,), (right_dim,)), ((), ())), pre...]
    all_gather x1 -> x0, local copies, waits for them, and re-layouts: 6.1 us -> none  [per_device(): mine = lax.all_gather(mine, 'rows', axis=0, tiled=False)]
    another operation x2 -> x0, other arithmetic: 5.96 us -> none  [per_device(): jnp.stack([jnp.where(first, mine, theirs), jnp.where(first, theirs, mine)...]
    all_gather x1, waiting for transfers between devices: 35.2 us -> 29.9 us  [per_device(): mine = lax.all_gather(mine, 'rows', axis=0, tiled=False)]
    slice x1 -> x0, local copies, waits for them, and re-layouts: 3.79 us -> none  [per_device(): cross_low = gathered[:, :f_here].reshape(teacher_width, model_width)]
  transfers between devices with their start and end apart: 4 -> 4, of which waited for: 4 -> 4; matrix products, arithmetic and copies ran while one was open for 14% -> 16% of each run, Pallas kernels for 0% -> 0%
where the time goes in v13:
time: 298 us; the launch traced here: 297 us
  waiting for transfers between devices  212 us (71%)
  matrix products  31.8 us (11%)
  local copies, waits for them, and re-layouts  21.1 us (7%)
  other arithmetic  17 us (6%)
  between operations  13.9 us (5%)
    all_gather x1, waiting for transfers between devices, per_device(): gathered = lax.all_gather(packed, 'rows', axis=0, tiled=False)  67.6 us
    reduce_scatter x1, waiting for transfers between devices, per_device(): reduced = lax.psum_scatter(partial, 'rows', scatter_dimension=0, tiled=True)  61.4 us
    ppermute x1, waiting for transfers between devices, per_device(): theirs = lax.ppermute(mine, 'groups', [(0, 1), (1, 0)])  52.7 us
    dot_general x6, matrix products, contract(): lax.dot_general(left, right, (((left_dim,), (right_dim,)), ((), ())), pre...  31.8 us
    all_gather x1, waiting for transfers between devices, per_device(): mine = lax.all_gather(mine, 'rows', axis=0, tiled=False)  29.9 us
    unnamed x14, local copies, waits for them, and re-layouts  10.7 us
    concatenate x1, local copies, waits for them, and re-layouts, per_device(): teacher_pair = jnp.concatenate([teacher_high, teacher_low], axis=0)  8.98 us
  transfers between devices with their start and end apart: 4, of which 4 were waited for; matrix products, arithmetic and copies ran while one was open for 16% of the time, Pallas kernels for 0%

profile of v13, /device:TPU:0, one launch (start us, length us, event | category | flops | bytes accessed | tf_op | source)
XLA Modules:
  0.0 297.1 jit_solution(12757566463181883577)
XLA Ops:
  7.2 0.0 all-gather.5.cloned.1.call-start
  7.2 0.9 copy-done
  8.2 0.1 constant_dynamic-slice_fusion
  8.3 0.8 copy.26
  9.1 0.0 all-gather.5.cloned.1.call-update
  9.1 0.0 reduce-scatter.2.cloned.1.call-start
  9.2 1.2 copy.19
  10.4 6.6 %copy.18 = f32[256,6144]{0,1:T(8,128)} copy(f32[256,6144]{1,0:T(8,128)} %param.4) | data formatting | bytes 12582912 | tf_op args[1]
  17.0 3.3 %pad_maximum_fusion = f32[256,16,416]{0,2,1:T(8,128)S(1)} fusion(f32[256,16,32]{0,2,1:T(8,128)S(1)} %bitcast.38, f32[256,16,384]{0,2,1:T(8,128)} %bitcast.29), kind=kLoop, calls=%fused_computation.7 | loop fusion | flops 1703936 | bytes 13631488 | tf_op jit(solution)/shard_map/concatenate | solution.py:47
  20.3 8.6 %fusion.35 = f32[6656,512]{1,0:T(8,128)} fusion(f32[256,6656]{0,1:T(8,128)S(1)} %bitcast.28, f32[256,512]{1,0:T(8,128)S(1)} %copy-done.1), kind=kOutput, calls=%fused_computation.52 | convolution fusion | flops 5234491392 | bytes 20971520 | tf_op jit(solution)/shard_map/dot_general | solution.py:11
  28.9 29.9 %all-gather.5.cloned.1.call-done = bf16[3072,512]{1,0:T(8,128)(2,1)} async-done(((bf16[192,512]{1,0:T(8,128)(2,1)}), bf16[3072,512]{1,0:T(8,128)(2,1)}) %all-gather.5.cloned.1.call-update) | async-done | bytes 3145744 | tf_op jit(solution)/shard_map/all_gather | solution.py:45
  58.8 0.0 reduce-scatter.2.cloned.1.call-update
  58.8 0.0 all-gather.7.cloned.1.call-start
  58.9 1.5 collective-permute-start
  60.4 3.9 %reduce-precision_convert_fusion = (bf16[256,6144]{1,0:T(8,128)(2,1)S(1)}, bf16[256,6144]{1,0:T(8,128)(2,1)S(1)}) fusion(f32[256,6144]{1,0:T(8,128)} %param.4), kind=kLoop, calls=%fused_computation.1 | loop fusion | flops 6291456 | bytes 12582912 | tf_op jit(solution)/shard_map/convert_element_type | solution.py:23
  64.3 3.4 %pad_maximum_fusion.1 = bf16[512,6144]{1,0:T(8,128)(2,1)} fusion(bf16[256,6144]{1,0:T(8,128)(2,1)S(1)} %get-tuple-element.19, bf16[256,6144]{1,0:T(8,128)(2,1)S(1)} %get-tuple-element.18), kind=kLoop, calls=%fused_computation.9 | loop fusion | flops 12582912 | bytes 12582912 | tf_op jit(solution)/shard_map/concatenate | solution.py:77
  67.8 9.0 %copy.20 = bf16[512,6144]{0,1:T(8,128)(2,1)} copy(bf16[512,6144]{1,0:T(8,128)(2,1)} %pad_maximum_fusion.1) | data formatting | bytes 12582912 | tf_op jit(solution)/shard_map/concatenate | solution.py:77
  76.8 52.7 %collective-permute-done = bf16[16,192,512]{2,1,0:T(8,128)(2,1)} collective-permute-done((bf16[16,192,512]{2,1,0:T(8,128)(2,1)}, bf16[16,192,512]{2,1,0:T(8,128)(2,1)}, u32[]{:S(2)}, u32[]{:S(2)}) %collective-permute-start) | collective-permute-done | bytes 3145760 | tf_op jit(solution)/shard_map/ppermute | solution.py:56
  129.5 3.3 %broadcast_select_fusion.1 = (bf16[16,192,512]{2,1,0:T(8,128)(2,1)S(1)}, bf16[16,192,512]{2,1,0:T(8,128)(2,1)S(1)}) fusion(bf16[16,192,512]{2,1,0:T(8,128)(2,1)} %bitcast.37, bf16[16,192,512]{2,1,0:T(8,128)(2,1)} %collective-permute-done, pred[]{:T(512)S(6)} %eq.3), kind=kLoop, calls=%fused_computation.14 | loop fusion | flops 3145728 | bytes 12582913 | tf_op jit(solution)/shard_map/jit(_where)/select_n | solution.py:61
  132.8 4.1 %fusion.9 = f32[512,512]{1,0:T(8,128)S(1)} fusion(bf16[16,192,512]{2,1,0:T(8,128)(2,1)S(1)} %get-tuple-element.21, bf16[16,192,512]{2,1,0:T(8,128)(2,1)S(1)} %get-tuple-element.20, bf16[448]{0:T(512)(128)(2,1)S(1)} %pad.12.clone, bf16[512,16,384]{0,2,1:T(8,128)(2,1)S(1)} %bitcast.35), kind=kOutput, calls=%fused_computation.16 | convolution fusion | flops 3780116480 | bytes 13632384 | tf_op jit(solution)/shard_map/dot_general | solution.py:11
  136.9 0.1 slice_add_fusion.1
  137.0 5.3 %fusion.8 = f32[512,512]{1,0:T(8,128)} fusion(bf16[16,192,512]{2,1,0:T(8,128)(2,1)S(1)} %get-tuple-element.21, bf16[16,192,512]{2,1,0:T(8,128)(2,1)S(1)} %get-tuple-element.20, bf16[448]{0:T(512)(128)(2,1)S(1)} %pad.12.clone), kind=kOutput, calls=%fused_computation.15 | convolution fusion | flops 3780116480 | bytes 7340928 | tf_op jit(solution)/shard_map/dot_general | solution.py:11
  142.3 61.4 %reduce-scatter.2.cloned.1.call-done = f32[416,512]{1,0:T(8,128)} async-done(((f32[6656,512]{1,0:T(8,128)}), f32[416,512]{1,0:T(8,128)}) %reduce-scatter.2.cloned.1.call-update) | async-done | bytes 851984 | tf_op jit(solution)/shard_map/reduce_scatter | solution.py:67
  203.7 0.8 reduce-precision_convert_fusion.1
  204.5 1.2 slice.54
  205.7 0.8 pad_maximum_fusion.2
  206.5 67.6 %all-gather.7.cloned.1.call-done = bf16[7168,512]{1,0:T(8,128)(2,1)} async-done(((bf16[448,512]{1,0:T(8,128)(2,1)}), bf16[7168,512]{1,0:T(8,128)(2,1)}) %all-gather.7.cloned.1.call-update) | async-done | bytes 7340048 | tf_op jit(solution)/shard_map/all_gather | solution.py:86
  274.2 10.0 %fusion.12 = f32[512,512]{1,0:T(8,128)} fusion(bf16[16,448,512]{2,1,0:T(8,128)(2,1)} %bitcast.40, bf16[512,16,384]{0,2,1:T(8,128)(2,1)} %bitcast.32), kind=kOutput, calls=%fused_computation.17 | convolution fusion | flops 3758096384 | bytes 14680064 | tf_op jit(solution)/shard_map/dot_general | solution.py:11
  284.2 1.4 convert_add_fusion
  285.5 0.7 fusion.15
  286.2 1.1 copy.23
  287.4 3.2 %fusion.17 = f32[256,512]{1,0:T(8,128)} fusion(f32[256,512]{1,0:T(8,128)S(1)} %copy-done.1, f32[512,512]{1,0:T(8,128)S(1)} %bitcast.31, f32[512,512]{1,0:T(8,128)} %fusion.8, f32[512,512]{1,0:T(8,128)} %fusion.12, f32[256,512]{1,0:T(8,128)S(1)} %slice_add_fusion.1, f32[512]{0:T(512)S(1)} %get-tuple-element.24, f32[512]{0:T(512)S(1)} %get-tuple-element.25), kind=kOutput, calls=%fused_computation.22 | convolution fusion | flops 404619264 | bytes 4724736 | tf_op jit(solution)/shard_map/dot_general | solution.py:11
  (14 shorter events, 0.1 us)
Async XLA Ops:
  7.2 1.0 copy-start
  7.2 51.6 %all-gather.5.cloned.1.call-start = ((), (), s32[]{:S(2)}) async-start(), calls=%async_computation.2 | async-start | bytes 3342336 | tf_op jit(solution)/shard_map/all_gather | solution.py:45
  9.1 194.5 %reduce-scatter.2.cloned.1.call-start = ((), (), s32[]{:S(2)}) async-start(), calls=%async_computation.1 | async-start | bytes 14483456 | tf_op jit(solution)/shard_map/reduce_scatter | solution.py:67
  17.0 3.3 %copy-start.1 = (f32[256,512]{1,0:T(8,128)S(1)}, f32[256,512]{1,0:T(8,128)}, u32[]{:S(2)}) copy-start(f32[256,512]{1,0:T(8,128)} %param.3) | copy-start | bytes 1572868
  58.8 215.3 %all-gather.7.cloned.1.call-start = ((), (), s32[]{:S(2)}) async-start(), calls=%async_computation.3 | async-start | bytes 7798784 | tf_op jit(solution)/shard_map/all_gather | solution.py:86
  58.9 70.6 %collective-permute-start = (bf16[16,192,512]{2,1,0:T(8,128)(2,1)}, bf16[16,192,512]{2,1,0:T(8,128)(2,1)}, u32[]{:S(2)}, u32[]{:S(2)}) collective-permute-start(bf16[16,192,512]{2,1,0:T(8,128)(2,1)} %bitcast.36), channel_id=1, source_target_pairs={{0,16},{16,0},{1,17},{17,1},{2,18},{18,2},{3,19},{19,3},{4,20},{20... | collective-permute-start | bytes 9437192 | tf_op jit(solution)/shard_map/ppermute | solution.py:56
  76.8 56.0 %slice-start = ((s8[6291456]{0:T(1024)(128)(4,1)}), s8[4194304]{0:T(1024)(128)(4,1)S(1)}, s32[]{:S(2)}) async-start(s8[6291456]{0:T(1024)(128)(4,1)} %bitcast.33), calls=%async_computation.4 | async-start | bytes 8388608
  76.8 56.0 %slice-start.1 = ((s8[6291456]{0:T(1024)(128)(4,1)}), s8[2097152]{0:T(1024)(128)(4,1)S(1)}, s32[]{:S(2)}) async-start(s8[6291456]{0:T(1024)(128)(4,1)} %bitcast.33), calls=%async_computation.5 | async-start | bytes 4194304
  274.2 11.4 %copy-start.2 = (f32[416,512]{1,0:T(8,128)S(1)}, f32[416,512]{1,0:T(8,128)}, u32[]{:S(2)}) copy-start(f32[416,512]{1,0:T(8,128)} %reduce-scatter.2.cloned.1.call-done) | copy-start | bytes 2555908
Sparse Core Ops, SparseCore 0:
  10.9 47.8 all-gather.4
  62.9 140.7 reduce-scatter.1
  206.8 67.3 all-gather.6

commit v14 on v12

--- a/solution.py
+++ b/solution.py
@@ -40,8 +40,8 @@
     gram_scale = 0.5 / total_rows
 
     group = lax.axis_index("groups")
-    half = heads.shape[1] // 2
-    mine = lax.dynamic_slice_in_dim(heads, group * half, half, axis=1)
+    half = f_here // 2
+    mine = lax.dynamic_slice_in_dim(heads.T, group * half, half, axis=0)
     mine = lax.all_gather(mine, "rows", axis=0, tiled=False)
 
     left = jnp.concatenate(
@@ -55,10 +55,9 @@
     mine, partial = lax.optimization_barrier((mine, partial))
     theirs = lax.ppermute(mine, "groups", [(0, 1), (1, 0)])
     first = group == 0
-    heads_all = jnp.stack(
+    heads_all = jnp.concatenate(
         [jnp.where(first, mine, theirs), jnp.where(first, theirs, mine)], axis=1
-    )
-    heads_all = heads_all.transpose(2, 0, 1, 3).reshape(model_width, teacher_width)
+    ).reshape(teacher_width, model_width)
     reduced = lax.psum_scatter(partial, "rows", scatter_dimension=0, tiled=True)
     cross_here = reduced[:f_here]
     moment_here = reduced[f_here:]
@@ -67,16 +66,15 @@
     packed = jnp.concatenate(
         [cross_here.astype(jnp.bfloat16), moment_high, moment_low], axis=0
     )
-    gram_heads = contract(heads_all, heads_all, 1, 1, lax.Precision.DEFAULT)
+    gram_heads = contract(heads_all, heads_all, 0, 0, lax.Precision.DEFAULT)
     teacher_high, teacher_low = split_bf16(teacher)
     teacher_pair = jnp.concatenate([teacher_high, teacher_low], axis=0)
-    teacher_heads = contract(teacher_pair, heads_all, 1, 1, lax.Precision.DEFAULT)
+    teacher_heads = contract(teacher_pair, heads_all, 1, 0, lax.Precision.DEFAULT)
     teacher_heads = teacher_heads[:rows_here] + teacher_heads[rows_here:]
     gram_heads, teacher_heads, packed = lax.optimization_barrier(
         (gram_heads, teacher_heads, packed)
     )
     gathered = lax.all_gather(packed, "rows", axis=0, tiled=False)
-    cross_low = gathered[:, :f_here].reshape(teacher_width, model_width)
     moment = (
         gathered[:, f_here : f_here + d_here].astype(jnp.float32)
         + gathered[:, f_here + d_here :].astype(jnp.float32)
@@ -86,6 +84,7 @@
         contract(moment, heads.astype(jnp.float32), 1, 0, lax.Precision.HIGH) - cross_here.T
     )
 
+    cross_low = gathered[:, :f_here].reshape(teacher_width, model_width)
     teacher_cross = contract(teacher_pair, cross_low, 1, 0, lax.Precision.DEFAULT)
     teacher_cross = teacher_cross[:rows_here] + teacher_cross[rows_here:]
     student_side = reg_weight * gram_heads + gram_scale * (moment * nested)

time: 304 us -> 297 us (0.977)
  local copies, waits for them, and re-layouts: 27.5 us -> 18.3 us
    reduce_scatter x1, waiting for transfers between devices: 51.1 us -> 59 us  [per_device(): reduced = lax.psum_scatter(partial, 'rows', scatter_dimension=0, tiled=True)]
    all_gather x1 -> x0, local copies, waits for them, and re-layouts: 6.1 us -> none  [per_device(): mine = lax.all_gather(mine, 'rows', axis=0, tiled=False)]
    another operation x2 -> x0, other arithmetic: 5.96 us -> none  [per_device(): jnp.stack([jnp.where(first, mine, theirs), jnp.where(first, theirs, mine)...]
    all_gather x1, waiting for transfers between devices: 35.2 us -> 29.9 us  [per_device(): mine = lax.all_gather(mine, 'rows', axis=0, tiled=False)]
    optimization_barrier x1 -> x0, local copies, waits for them, and re-layouts: 3.45 us -> none  [per_device(): mine, partial = lax.optimization_barrier((mine, partial))]
    unnamed x19 -> x18, local copies, waits for them, and re-layouts: 12.1 us -> 13.4 us
where the time goes in v14:
time: 297 us; the launch traced here: 296 us
  waiting for transfers between devices  219 us (74%)
  matrix products  27.5 us (9%)
  local copies, waits for them, and re-layouts  18.3 us (6%)
  other arithmetic  16 us (5%)
  between operations  13.9 us (5%)
    all_gather x1, waiting for transfers between devices, per_device(): gathered = lax.all_gather(packed, 'rows', axis=0, tiled=False)  67.6 us
    ppermute x1, waiting for transfers between devices, per_device(): theirs = lax.ppermute(mine, 'groups', [(0, 1), (1, 0)])  62.1 us
    reduce_scatter x1, waiting for transfers between devices, per_device(): reduced = lax.psum_scatter(partial, 'rows', scatter_dimension=0, tiled=True)  59 us
    all_gather x1, waiting for transfers between devices, per_device(): mine = lax.all_gather(mine, 'rows', axis=0, tiled=False)  29.9 us
    dot_general x6, matrix products, contract(): lax.dot_general(left, right, (((left_dim,), (right_dim,)), ((), ())), pre...  27.5 us
    unnamed x18, local copies, waits for them, and re-layouts  13.4 us
    convert_element_type x2, other arithmetic, split_bf16(): return (high.astype(jnp.bfloat16), low)  7.67 us
  transfers between devices with their start and end apart: 4, of which 4 were waited for; matrix products, arithmetic and copies ran while one was open for 14% of the time, Pallas kernels for 0%

profile of v14, /device:TPU:0, one launch (start us, length us, event | category | flops | bytes accessed | tf_op | source)
XLA Modules:
  0.0 296.1 jit_solution(14790933805303187317)
XLA Ops:
  7.2 0.9 copy-done
  8.2 0.1 constant_dynamic-slice_fusion
  8.3 0.8 copy.27
  9.1 0.0 reduce-scatter.2.cloned.1.call-start
  9.2 1.2 copy.19
  10.4 6.6 %copy.18 = f32[256,6144]{0,1:T(8,128)} copy(f32[256,6144]{1,0:T(8,128)} %param.4) | data formatting | bytes 12582912 | tf_op args[1]
  17.0 3.3 %pad_maximum_fusion = f32[256,16,416]{0,2,1:T(8,128)S(1)} fusion(f32[256,16,32]{0,2,1:T(8,128)S(1)} %bitcast.36, f32[256,16,384]{0,2,1:T(8,128)} %bitcast.27), kind=kLoop, calls=%fused_computation.2 | loop fusion | flops 1703936 | bytes 13631488 | tf_op jit(solution)/shard_map/concatenate | solution.py:47
  20.3 8.6 %fusion.21 = f32[6656,512]{1,0:T(8,128)} fusion(f32[256,6656]{0,1:T(8,128)S(1)} %bitcast.26, f32[256,512]{1,0:T(8,128)S(1)} %copy-done.1), kind=kOutput, calls=%fused_computation.43 | convolution fusion | flops 5234491392 | bytes 20971520 | tf_op jit(solution)/shard_map/dot_general | solution.py:11
  28.9 29.9 %all-gather.5.cloned.1.call-done = bf16[3072,512]{1,0:T(8,128)(2,1)} async-done(((bf16[192,512]{1,0:T(8,128)(2,1)}), bf16[3072,512]{1,0:T(8,128)(2,1)}) %all-gather.5.cloned.1.call-update) | async-done | bytes 3145744 | tf_op jit(solution)/shard_map/all_gather | solution.py:45
  58.8 0.2 all-gather.7.cloned.1.call-start
  59.1 1.6 copy-done.5
  60.7 1.5 collective-permute-start
  62.2 6.8 %reduce-precision_convert_fusion = (bf16[256,6144]{1,0:T(8,128)(2,1)}, bf16[256,6144]{1,0:T(8,128)(2,1)}) fusion(f32[256,6144]{1,0:T(8,128)} %param.4), kind=kLoop, calls=%fused_computation.1 | loop fusion | flops 6291456 | bytes 12582912 | tf_op jit(solution)/shard_map/convert_element_type | solution.py:23
  69.0 62.1 %collective-permute-done = bf16[16,192,512]{2,1,0:T(8,128)(2,1)} collective-permute-done((bf16[16,192,512]{2,1,0:T(8,128)(2,1)S(1)}, bf16[16,192,512]{2,1,0:T(8,128)(2,1)}, u32[]{:S(2)}, u32[]{:S(2)}) %collective-permute-start) | collective-permute-done | bytes 3145760 | tf_op jit(solution)/shard_map/ppermute | solution.py:56
  131.0 2.3 broadcast_select_fusion.1
  133.4 0.6 pad_maximum_fusion.1
  133.9 6.3 %fusion.2 = f32[512,512]{1,0:T(8,128)S(1)} fusion(bf16[6144,512]{1,0:T(8,128)(2,1)S(1)} %bitcast.33, bf16[256,6144]{1,0:T(8,128)(2,1)} %get-tuple-element.19, bf16[256,6144]{1,0:T(8,128)(2,1)} %get-tuple-element.18), kind=kOutput, calls=%fused_computation.7 | convolution fusion | flops 3233808384 | bytes 13631488 | tf_op jit(solution)/shard_map/dot_general | solution.py:11
  140.2 0.1 slice_add_fusion.1
  140.3 4.4 %convolution_bitcast_fusion = f32[512,512]{1,0:T(8,128)} fusion(bf16[16,192,512]{2,1,0:T(8,128)(2,1)S(1)} %get-tuple-element.21, bf16[16,192,512]{2,1,0:T(8,128)(2,1)S(1)} %get-tuple-element.20), kind=kOutput, calls=%fused_computation.10 | convolution fusion | flops 3233808384 | bytes 7340032 | tf_op jit(solution)/shard_map/dot_general | solution.py:11
  144.7 59.0 %reduce-scatter.2.cloned.1.call-done = f32[416,512]{1,0:T(8,128)} async-done(((f32[6656,512]{1,0:T(8,128)}), f32[416,512]{1,0:T(8,128)}) %reduce-scatter.2.cloned.1.call-update) | async-done | bytes 851984 | tf_op jit(solution)/shard_map/reduce_scatter | solution.py:61
  203.7 0.8 reduce-precision_convert_fusion.1
  204.5 1.2 slice.59
  205.7 0.8 pad_maximum_fusion.5
  206.5 67.6 %all-gather.7.cloned.1.call-done = bf16[7168,512]{1,0:T(8,128)(2,1)} async-done(((bf16[448,512]{1,0:T(8,128)(2,1)}), bf16[7168,512]{1,0:T(8,128)(2,1)}) %all-gather.7.cloned.1.call-update) | async-done | bytes 7340048 | tf_op jit(solution)/shard_map/all_gather | solution.py:77
  274.1 1.4 convert_add_fusion
  275.5 3.6 %slice.42 = bf16[16,384,512]{2,1,0:T(8,128)(2,1)S(1)} slice(bf16[16,448,512]{2,1,0:T(8,128)(2,1)} %bitcast.31), slice={[0:16], [0:384], [0:512]} | slice | bytes 12582912 | tf_op jit(solution)/shard_map/slice | solution.py:87
  279.1 0.1 copy-done.3
  279.2 1.0 copy-done.4
  280.2 4.4 %fusion.1 = f32[512,512]{1,0:T(8,128)} fusion(bf16[6144,512]{1,0:T(8,128)(2,1)S(1)} %bitcast.32, bf16[256,6144]{1,0:T(8,128)(2,1)S(1)} %copy-done.4, bf16[256,6144]{1,0:T(8,128)(2,1)S(1)} %copy-done.3), kind=kOutput, calls=%fused_computation.6 | convolution fusion | flops 3233808384 | bytes 13631488 | tf_op jit(solution)/shard_map/dot_general | solution.py:11
  284.6 0.7 fusion.3
  285.2 1.1 copy.23
  286.4 3.2 %fusion.5 = f32[256,512]{1,0:T(8,128)} fusion(f32[256,512]{1,0:T(8,128)S(1)} %copy-done.2, f32[512,512]{1,0:T(8,128)S(1)} %bitcast.29, f32[512,512]{1,0:T(8,128)} %convolution_bitcast_fusion, f32[512,512]{1,0:T(8,128)} %fusion.1, f32[256,512]{1,0:T(8,128)S(1)} %slice_add_fusion.1, f32[512]{0:T(512)S(1)} %get-tuple-element.24, f32[512]{0:T(512)S(1)} %get-tuple-element.25), kind=kOutput, calls=%fused_computation.15 | convolution fusion | flops 404619264 | bytes 4724736 | tf_op jit(solution)/shard_map/dot_general | solution.py:11
  (15 shorter events, 0.1 us)
Async XLA Ops:
  7.2 1.0 copy-start
  7.2 51.6 %all-gather.5.cloned.1.call-start = ((), (), s32[]{:S(2)}) async-start(), calls=%async_computation.2 | async-start | bytes 3342336 | tf_op jit(solution)/shard_map/all_gather | solution.py:45
  9.1 194.5 %reduce-scatter.2.cloned.1.call-start = ((), (), s32[]{:S(2)}) async-start(), calls=%async_computation.1 | async-start | bytes 14483456 | tf_op jit(solution)/shard_map/reduce_scatter | solution.py:61
  17.0 3.3 %copy-start.1 = (f32[256,512]{1,0:T(8,128)S(1)}, f32[256,512]{1,0:T(8,128)}, u32[]{:S(2)}) copy-start(f32[256,512]{1,0:T(8,128)} %param.3) | copy-start | bytes 1572868
  58.8 1.9 copy-start.5
  58.8 215.3 %all-gather.7.cloned.1.call-start = ((), (), s32[]{:S(2)}) async-start(), calls=%async_computation.3 | async-start | bytes 7798784 | tf_op jit(solution)/shard_map/all_gather | solution.py:77
  60.7 70.4 %collective-permute-start = (bf16[16,192,512]{2,1,0:T(8,128)(2,1)S(1)}, bf16[16,192,512]{2,1,0:T(8,128)(2,1)}, u32[]{:S(2)}, u32[]{:S(2)}) collective-permute-start(bf16[16,192,512]{2,1,0:T(8,128)(2,1)S(1)} %bitcast.34), channel_id=1, source_target_pairs={{0,16},{16,0},{1,17},{17,1},{2,18},{18,2},{3,19},{19,3},{4,20},{20... | collective-permute-start | bytes 9437192 | tf_op jit(solution)/shard_map/ppermute | solution.py:56
  275.5 3.7 %copy-start.3 = (bf16[256,6144]{1,0:T(8,128)(2,1)S(1)}, bf16[256,6144]{1,0:T(8,128)(2,1)}, u32[]{:S(2)}) copy-start(bf16[256,6144]{1,0:T(8,128)(2,1)} %get-tuple-element.18) | copy-start | bytes 9437188
  275.5 4.7 %copy-start.4 = (bf16[256,6144]{1,0:T(8,128)(2,1)S(1)}, bf16[256,6144]{1,0:T(8,128)(2,1)}, u32[]{:S(2)}) copy-start(bf16[256,6144]{1,0:T(8,128)(2,1)} %get-tuple-element.19) | copy-start | bytes 9437188
  280.2 4.4 %copy-start.6 = (f32[416,512]{1,0:T(8,128)S(1)}, f32[416,512]{1,0:T(8,128)}, u32[]{:S(2)}) copy-start(f32[416,512]{1,0:T(8,128)} %reduce-scatter.2.cloned.1.call-done) | copy-start | bytes 2555908
  280.2 6.2 %copy-start.2 = (f32[256,512]{1,0:T(8,128)S(1)}, f32[256,512]{1,0:T(8,128)}, u32[]{:S(2)}) copy-start(f32[256,512]{1,0:T(8,128)} %param.3) | copy-start | bytes 1572868
Sparse Core Ops, SparseCore 0:
  10.9 47.8 all-gather.4
  62.9 140.7 reduce-scatter.1
  206.8 67.2 all-gather.6

commit v15 on v14

--- a/solution.py
+++ b/solution.py
@@ -84,8 +84,12 @@
         contract(moment, heads.astype(jnp.float32), 1, 0, lax.Precision.HIGH) - cross_here.T
     )
 
-    cross_low = gathered[:, :f_here].reshape(teacher_width, model_width)
-    teacher_cross = contract(teacher_pair, cross_low, 1, 0, lax.Precision.DEFAULT)
+    teacher_cross = lax.dot_general(
+        teacher_pair.reshape(2 * rows_here, devices, f_here),
+        gathered[:, :f_here],
+        (((1, 2), (0, 1)), ((), ())),
+        preferred_element_type=jnp.float32,
+    )
     teacher_cross = teacher_cross[:rows_here] + teacher_cross[rows_here:]
     student_side = reg_weight * gram_heads + gram_scale * (moment * nested)
     grad_student = (

time: 297 us -> 297 us (level)
  other arithmetic: 16 us -> 22.4 us
  local copies, waits for them, and re-layouts: 18.3 us -> 12 us
  waiting for transfers between devices: 219 us -> 214 us
  matrix products: 27.5 us -> 32.2 us
    dot_general x0 -> x1, matrix products: none -> 9.16 us  [per_device(): lax.dot_general(teacher_pair.reshape(2 * rows_here, devices, f_here), gat...]
    concatenate x0 -> x1, other arithmetic: none -> 5.06 us  [per_device(): teacher_pair = jnp.concatenate([teacher_high, teacher_low], axis=0)]
    all_gather x1, waiting for transfers between devices: 67.6 us -> 62.6 us  [per_device(): gathered = lax.all_gather(packed, 'rows', axis=0, tiled=False)]
    dot_general x6 -> x5, matrix products: 27.5 us -> 23 us  [contract(): lax.dot_general(left, right, (((left_dim,), (right_dim,)), ((), ())), pre...]
    slice x1 -> x0, local copies, waits for them, and re-layouts: 3.58 us -> none  [per_device(): cross_low = gathered[:, :f_here].reshape(teacher_width, model_width)]
    ppermute x1, waiting for transfers between devices: 62.1 us -> 65.3 us  [per_device(): theirs = lax.ppermute(mine, 'groups', [(0, 1), (1, 0)])]
    convert_element_type x2, other arithmetic: 7.67 us -> 4.6 us  [split_bf16(): return (high.astype(jnp.bfloat16), low)]
    unnamed x18 -> x16, local copies, waits for them, and re-layouts: 13.4 us -> 10.7 us
  transfers between devices with their start and end apart: 4 -> 4, of which waited for: 4 -> 4; matrix products, arithmetic and copies ran while one was open for 14% -> 16% of each run, Pallas kernels for 0% -> 0%
where the time goes in v15:
time: 297 us; the launch traced here: 296 us
  waiting for transfers between devices  214 us (72%)
  matrix products  32.2 us (11%)
  other arithmetic  22.4 us (8%)
  between operations  13.9 us (5%)
  local copies, waits for them, and re-layouts  12 us (4%)
    ppermute x1, waiting for transfers between devices, per_device(): theirs = lax.ppermute(mine, 'groups', [(0, 1), (1, 0)])  65.3 us
    all_gather x1, waiting for transfers between devices, per_device(): gathered = lax.all_gather(packed, 'rows', axis=0, tiled=False)  62.6 us
    reduce_scatter x1, waiting for transfers between devices, per_device(): reduced = lax.psum_scatter(partial, 'rows', scatter_dimension=0, tiled=True)  56 us
    all_gather x1, waiting for transfers between devices, per_device(): mine = lax.all_gather(mine, 'rows', axis=0, tiled=False)  29.9 us
    dot_general x5, matrix products, contract(): lax.dot_general(left, right, (((left_dim,), (right_dim,)), ((), ())), pre...  23 us
    unnamed x16, local copies, waits for them, and re-layouts  10.7 us
    dot_general x1, matrix products, per_device(): lax.dot_general(teacher_pair.reshape(2 * rows_here, devices, f_here), gat...  9.16 us
  transfers between devices with their start and end apart: 4, of which 4 were waited for; matrix products, arithmetic and copies ran while one was open for 16% of the time, Pallas kernels for 0%

profile of v15, /device:TPU:0, one launch (start us, length us, event | category | flops | bytes accessed | tf_op | source)
XLA Modules:
  0.0 296.2 jit_solution(12198514524596415362)
XLA Ops:
  7.2 0.0 all-gather.5.cloned.1.call-start
  7.2 0.9 copy-done
  8.2 0.1 constant_dynamic-slice_fusion
  8.3 0.8 copy.34
  9.1 0.0 reduce-scatter.2.cloned.1.call-start
  9.2 1.2 copy.22
  10.4 6.6 %copy.21 = f32[256,6144]{0,1:T(8,128)} copy(f32[256,6144]{1,0:T(8,128)} %param.4) | data formatting | bytes 12582912 | tf_op args[1]
  17.0 3.3 %pad_maximum_fusion = f32[256,16,416]{0,2,1:T(8,128)S(1)} fusion(f32[256,16,32]{0,2,1:T(8,128)S(1)} %bitcast.34, f32[256,16,384]{0,2,1:T(8,128)} %bitcast.28), kind=kLoop, calls=%fused_computation.2 | loop fusion | flops 1703936 | bytes 13631488 | tf_op jit(solution)/shard_map/concatenate | solution.py:47
  20.3 8.6 %fusion.23 = f32[6656,512]{1,0:T(8,128)} fusion(f32[256,6656]{0,1:T(8,128)S(1)} %bitcast.29, f32[256,512]{1,0:T(8,128)S(1)} %copy-done.2), kind=kOutput, calls=%fused_computation.43 | convolution fusion | flops 5234491392 | bytes 20971520 | tf_op jit(solution)/shard_map/dot_general | solution.py:11
  28.9 29.9 %all-gather.5.cloned.1.call-done = bf16[3072,512]{1,0:T(8,128)(2,1)} async-done(((bf16[192,512]{1,0:T(8,128)(2,1)}), bf16[3072,512]{1,0:T(8,128)(2,1)}) %all-gather.5.cloned.1.call-update) | async-done | bytes 3145744 | tf_op jit(solution)/shard_map/all_gather | solution.py:45
  58.8 0.0 reduce-scatter.2.cloned.1.call-update
  58.8 0.2 all-gather.7.cloned.1.call-start
  59.0 1.5 collective-permute-start
  60.6 3.8 %reduce-precision_convert_fusion = (bf16[256,6144]{0,1:T(8,128)(2,1)S(1)}, bf16[256,6144]{0,1:T(8,128)(2,1)S(1)}) fusion(f32[256,6144]{0,1:T(8,128)} %copy.21), kind=kLoop, calls=%fused_computation.1 | loop fusion | flops 6291456 | bytes 12582912 | tf_op jit(solution)/shard_map/convert_element_type | solution.py:23
  64.3 65.3 %collective-permute-done = bf16[16,192,512]{2,1,0:T(8,128)(2,1)} collective-permute-done((bf16[16,192,512]{2,1,0:T(8,128)(2,1)}, bf16[16,192,512]{2,1,0:T(8,128)(2,1)}, u32[]{:S(2)}, u32[]{:S(2)}) %collective-permute-start) | collective-permute-done | bytes 3145760 | tf_op jit(solution)/shard_map/ppermute | solution.py:56
  129.7 3.3 %broadcast_select_fusion.1 = (bf16[16,192,512]{2,1,0:T(8,128)(2,1)S(1)}, bf16[16,192,512]{2,1,0:T(8,128)(2,1)S(1)}) fusion(bf16[16,192,512]{2,1,0:T(8,128)(2,1)} %bitcast.1, bf16[16,192,512]{2,1,0:T(8,128)(2,1)} %collective-permute-done, pred[]{:T(512)S(6)} %eq.3), kind=kLoop, calls=%fused_computation.9 | loop fusion | flops 3145728 | bytes 12582913 | tf_op jit(solution)/shard_map/jit(_where)/select_n | solution.py:59
  132.9 3.1 %pad_maximum_fusion.1 = bf16[16,384,512]{2,1,0:T(8,128)(2,1)} fusion(bf16[16,192,512]{2,1,0:T(8,128)(2,1)S(1)} %get-tuple-element.21, bf16[16,192,512]{2,1,0:T(8,128)(2,1)S(1)} %get-tuple-element.20), kind=kLoop, calls=%fused_computation.6 | loop fusion | flops 12582912 | bytes 12582912 | tf_op jit(solution)/shard_map/concatenate | solution.py:58
  136.1 6.3 %fusion.22 = f32[512,512]{1,0:T(8,128)S(1)} fusion(bf16[6144,512]{1,0:T(8,128)(2,1)} %bitcast.33, bf16[256,6144]{0,1:T(8,128)(2,1)S(1)} %get-tuple-element.19, bf16[256,6144]{0,1:T(8,128)(2,1)S(1)} %get-tuple-element.18), kind=kOutput, calls=%fused_computation.42 | convolution fusion | flops 3233808384 | bytes 13631488 | tf_op jit(solution)/shard_map/dot_general | solution.py:11
  142.4 0.9 slice_add_fusion.1
  143.2 4.4 %convolution_bitcast_fusion = f32[512,512]{1,0:T(8,128)} fusion(bf16[16,192,512]{2,1,0:T(8,128)(2,1)S(1)} %get-tuple-element.21, bf16[16,192,512]{2,1,0:T(8,128)(2,1)S(1)} %get-tuple-element.20), kind=kOutput, calls=%fused_computation.11 | convolution fusion | flops 3233808384 | bytes 7340032 | tf_op jit(solution)/shard_map/dot_general | solution.py:11
  147.6 56.0 %reduce-scatter.2.cloned.1.call-done = f32[416,512]{1,0:T(8,128)} async-done(((f32[6656,512]{1,0:T(8,128)}), f32[416,512]{1,0:T(8,128)}) %reduce-scatter.2.cloned.1.call-update) | async-done | bytes 851984 | tf_op jit(solution)/shard_map/reduce_scatter | solution.py:61
  203.7 0.8 reduce-precision_convert_fusion.1
  204.5 1.2 slice.63
  205.7 0.8 pad_maximum_fusion.3
  206.5 0.0 all-gather.7.cloned.1.call-update
  206.5 5.1 %pad_maximum_fusion.2 = bf16[512,6144]{0,1:T(8,128)(2,1)} fusion(bf16[256,6144]{0,1:T(8,128)(2,1)} %copy-done.1, bf16[256,6144]{0,1:T(8,128)(2,1)S(1)} %get-tuple-element.18), kind=kLoop, calls=%fused_computation.7 | loop fusion | flops 12582912 | bytes 12582912 | tf_op jit(solution)/shard_map/concatenate | solution.py:71
  211.6 62.6 %all-gather.7.cloned.1.call-done = bf16[7168,512]{1,0:T(8,128)(2,1)} async-done(((bf16[448,512]{1,0:T(8,128)(2,1)}), bf16[7168,512]{1,0:T(8,128)(2,1)}) %all-gather.7.cloned.1.call-update) | async-done | bytes 7340048 | tf_op jit(solution)/shard_map/all_gather | solution.py:77
  274.2 1.4 convert_add_fusion
  275.6 9.2 %fusion.3 = f32[512,512]{1,0:T(8,128)} fusion(bf16[512,16,384]{0,2,1:T(8,128)(2,1)} %bitcast.32, bf16[16,448,512]{2,1,0:T(8,128)(2,1)} %bitcast.37), kind=kOutput, calls=%fused_computation.10 | convolution fusion | flops 3221225472 | bytes 13631488 | tf_op jit(solution)/shard_map/dot_general | solution.py:87
  284.7 0.6 fusion.6
  285.3 1.1 copy.29
  286.5 3.2 %fusion.8 = f32[256,512]{1,0:T(8,128)} fusion(f32[256,512]{1,0:T(8,128)S(1)} %copy-done.3, f32[512,512]{1,0:T(8,128)S(1)} %bitcast.31, f32[512,512]{1,0:T(8,128)} %convolution_bitcast_fusion, f32[512,512]{1,0:T(8,128)} %fusion.3, f32[256,512]{1,0:T(8,128)S(1)} %copy-done.4, f32[512]{0:T(512)S(1)} %get-tuple-element.24, f32[512]{0:T(512)S(1)} %get-tuple-element.25), kind=kOutput, calls=%fused_computation.16 | convolution fusion | flops 404619264 | bytes 4724736 | tf_op jit(solution)/shard_map/dot_general | solution.py:11
  (13 shorter events, 0.1 us)
Async XLA Ops:
  7.2 1.0 copy-start
  7.2 51.6 %all-gather.5.cloned.1.call-start = ((), (), s32[]{:S(2)}) async-start(), calls=%async_computation.2 | async-start | bytes 3342336 | tf_op jit(solution)/shard_map/all_gather | solution.py:45
  9.1 194.5 %reduce-scatter.2.cloned.1.call-start = ((), (), s32[]{:S(2)}) async-start(), calls=%async_computation.1 | async-start | bytes 14483456 | tf_op jit(solution)/shard_map/reduce_scatter | solution.py:61
  17.0 3.3 %copy-start.2 = (f32[256,512]{1,0:T(8,128)S(1)}, f32[256,512]{1,0:T(8,128)}, u32[]{:S(2)}) copy-start(f32[256,512]{1,0:T(8,128)} %param.3) | copy-start | bytes 1572868
  58.8 215.3 %all-gather.7.cloned.1.call-start = ((), (), s32[]{:S(2)}) async-start(), calls=%async_computation.3 | async-start | bytes 7798784 | tf_op jit(solution)/shard_map/all_gather | solution.py:77
  59.0 70.6 %collective-permute-start = (bf16[16,192,512]{2,1,0:T(8,128)(2,1)}, bf16[16,192,512]{2,1,0:T(8,128)(2,1)}, u32[]{:S(2)}, u32[]{:S(2)}) collective-permute-start(bf16[16,192,512]{2,1,0:T(8,128)(2,1)} %bitcast.1), channel_id=1, source_target_pairs={{0,16},{16,0},{1,17},{17,1},{2,18},{18,2},{3,19},{19,3},{4,20},{20... | collective-permute-start | bytes 9437192 | tf_op jit(solution)/shard_map/ppermute | solution.py:56
  64.3 71.8 %copy-start.1 = (bf16[256,6144]{0,1:T(8,128)(2,1)}, bf16[256,6144]{0,1:T(8,128)(2,1)S(1)}, u32[]{:S(2)}) copy-start(bf16[256,6144]{0,1:T(8,128)(2,1)S(1)} %get-tuple-element.19) | copy-start | bytes 9437188
  275.5 9.2 %copy-start.5 = (f32[416,512]{1,0:T(8,128)S(1)}, f32[416,512]{1,0:T(8,128)}, u32[]{:S(2)}) copy-start(f32[416,512]{1,0:T(8,128)} %reduce-scatter.2.cloned.1.call-done) | copy-start | bytes 2555908
  275.5 11.0 %copy-start.3 = (f32[256,512]{1,0:T(8,128)S(1)}, f32[256,512]{1,0:T(8,128)}, u32[]{:S(2)}) copy-start(f32[256,512]{1,0:T(8,128)} %param.3) | copy-start | bytes 1572868
  275.5 11.0 %copy-start.4 = (f32[256,512]{1,0:T(8,128)S(1)}, f32[256,512]{1,0:T(8,128)}, u32[]{:S(2)}) copy-start(f32[256,512]{1,0:T(8,128)} %slice_add_fusion.1) | copy-start | bytes 1572868
Sparse Core Ops, SparseCore 0:
  10.9 47.8 all-gather.4
  62.9 140.7 reduce-scatter.1
  206.8 67.3 all-gather.6

commit v16 on v15

--- a/solution.py
+++ b/solution.py
@@ -71,9 +71,10 @@
     teacher_pair = jnp.concatenate([teacher_high, teacher_low], axis=0)
     teacher_heads = contract(teacher_pair, heads_all, 1, 0, lax.Precision.DEFAULT)
     teacher_heads = teacher_heads[:rows_here] + teacher_heads[rows_here:]
-    gram_heads, teacher_heads, packed = lax.optimization_barrier(
-        (gram_heads, teacher_heads, packed)
+    heads_terms = reg_weight * (
+        contract(student, gram_heads, 1, 0, lax.Precision.HIGH) - teacher_heads
     )
+    heads_terms, packed = lax.optimization_barrier((heads_terms, packed))
     gathered = lax.all_gather(packed, "rows", axis=0, tiled=False)
     moment = (
         gathered[:, f_here : f_here + d_here].astype(jnp.float32)
@@ -91,11 +92,9 @@
         preferred_element_type=jnp.float32,
     )
     teacher_cross = teacher_cross[:rows_here] + teacher_cross[rows_here:]
-    student_side = reg_weight * gram_heads + gram_scale * (moment * nested)
-    grad_student = (
-        contract(student, student_side, 1, 0, lax.Precision.HIGH)
-        - reg_weight * teacher_heads
-        - gram_scale * teacher_cross * weights[None, :]
+    grad_student = heads_terms + gram_scale * (
+        contract(student, moment * nested, 1, 0, lax.Precision.HIGH)
+        - teacher_cross * weights[None, :]
     )
     return (grad_student, grad_heads)
 

time: 297 us -> 294 us (0.990)
  matrix products: 32.2 us -> 26.9 us
  waiting for transfers between devices: 214 us -> 217 us
    dot_general x5 -> x6, matrix products: 23 us -> 19.1 us  [contract(): lax.dot_general(left, right, (((left_dim,), (right_dim,)), ((), ())), pre...]
    unnamed x16 -> x21, local copies, waits for them, and re-layouts: 10.7 us -> 11.7 us
  transfers between devices with their start and end apart: 4 -> 4, of which waited for: 4 -> 4; matrix products, arithmetic and copies ran while one was open for 16% -> 15% of each run, Pallas kernels for 0% -> 0%
where the time goes in v16:
time: 294 us
  waiting for transfers between devices  217 us (74%)
  matrix products  26.9 us (9%)
  other arithmetic  21.5 us (7%)
  between operations  13.9 us (5%)
  local copies, waits for them, and re-layouts  13 us (4%)
    ppermute x1, waiting for transfers between devices, per_device(): theirs = lax.ppermute(mine, 'groups', [(0, 1), (1, 0)])  65.3 us
    all_gather x1, waiting for transfers between devices, per_device(): gathered = lax.all_gather(packed, 'rows', axis=0, tiled=False)  62.5 us
    reduce_scatter x1, waiting for transfers between devices, per_device(): reduced = lax.psum_scatter(partial, 'rows', scatter_dimension=0, tiled=True)  58.8 us
    all_gather x1, waiting for transfers between devices, per_device(): mine = lax.all_gather(mine, 'rows', axis=0, tiled=False)  29.9 us
    dot_general x6, matrix products, contract(): lax.dot_general(left, right, (((left_dim,), (right_dim,)), ((), ())), pre...  19.1 us
    unnamed x21, local copies, waits for them, and re-layouts  11.7 us
    dot_general x1, matrix products, per_device(): lax.dot_general(teacher_pair.reshape(2 * rows_here, devices, f_here), gat...  7.82 us
  transfers between devices with their start and end apart: 4, of which 4 were waited for; matrix products, arithmetic and copies ran while one was open for 15% of the time, Pallas kernels for 0%

profile of v16, /device:TPU:0, one launch (start us, length us, event | category | flops | bytes accessed | tf_op | source)
XLA Modules:
  0.0 293.9 jit_solution(3549632195208263150)
XLA Ops:
  7.2 0.0 all-gather.5.cloned.1.call-start
  7.2 0.9 copy-done
  8.2 0.1 constant_dynamic-slice_fusion
  8.3 0.8 copy.31
  9.1 0.0 all-gather.5.cloned.1.call-update
  9.1 0.0 reduce-scatter.2.cloned.1.call-start
  9.2 1.2 copy.14
  10.4 6.5 %copy.13 = f32[256,6144]{0,1:T(8,128)} copy(f32[256,6144]{1,0:T(8,128)} %param.4) | data formatting | bytes 12582912 | tf_op args[1]
  17.0 3.3 %pad_maximum_fusion = f32[256,16,416]{0,2,1:T(8,128)S(1)} fusion(f32[256,16,32]{0,2,1:T(8,128)S(1)} %bitcast.46, f32[256,16,384]{0,2,1:T(8,128)} %bitcast.40), kind=kLoop, calls=%fused_computation.2 | loop fusion | flops 1703936 | bytes 13631488 | tf_op jit(solution)/shard_map/concatenate | solution.py:47
  20.3 8.6 %fusion.19 = f32[6656,512]{1,0:T(8,128)} fusion(f32[256,6656]{0,1:T(8,128)S(1)} %bitcast.41, f32[256,512]{1,0:T(8,128)S(1)} %copy-done.2), kind=kOutput, calls=%fused_computation.39 | convolution fusion | flops 5234491392 | bytes 20971520 | tf_op jit(solution)/shard_map/dot_general | solution.py:11
  28.9 29.9 %all-gather.5.cloned.1.call-done = bf16[3072,512]{1,0:T(8,128)(2,1)} async-done(((bf16[192,512]{1,0:T(8,128)(2,1)}), bf16[3072,512]{1,0:T(8,128)(2,1)}) %all-gather.5.cloned.1.call-update) | async-done | bytes 3145744 | tf_op jit(solution)/shard_map/all_gather | solution.py:45
  58.8 0.2 all-gather.7.cloned.1.call-start
  59.0 1.5 collective-permute-start
  60.6 3.8 %reduce-precision_convert_fusion = (bf16[256,6144]{0,1:T(8,128)(2,1)S(1)}, bf16[256,6144]{0,1:T(8,128)(2,1)S(1)}) fusion(f32[256,6144]{0,1:T(8,128)} %copy.13), kind=kLoop, calls=%fused_computation.1 | loop fusion | flops 6291456 | bytes 12582912 | tf_op jit(solution)/shard_map/convert_element_type | solution.py:23
  64.3 65.3 %collective-permute-done = bf16[16,192,512]{2,1,0:T(8,128)(2,1)} collective-permute-done((bf16[16,192,512]{2,1,0:T(8,128)(2,1)}, bf16[16,192,512]{2,1,0:T(8,128)(2,1)}, u32[]{:S(2)}, u32[]{:S(2)}) %collective-permute-start) | collective-permute-done | bytes 3145760 | tf_op jit(solution)/shard_map/ppermute | solution.py:56
  129.7 3.3 %broadcast_select_fusion.1 = (bf16[16,192,512]{2,1,0:T(8,128)(2,1)S(1)}, bf16[16,192,512]{2,1,0:T(8,128)(2,1)S(1)}) fusion(bf16[16,192,512]{2,1,0:T(8,128)(2,1)} %bitcast.1, bf16[16,192,512]{2,1,0:T(8,128)(2,1)} %collective-permute-done, pred[]{:T(512)S(6)} %eq.3), kind=kLoop, calls=%fused_computation.9 | loop fusion | flops 3145728 | bytes 12582913 | tf_op jit(solution)/shard_map/jit(_where)/select_n | solution.py:59
  132.9 3.1 %pad_maximum_fusion.1 = bf16[16,384,512]{2,1,0:T(8,128)(2,1)} fusion(bf16[16,192,512]{2,1,0:T(8,128)(2,1)S(1)} %get-tuple-element.17, bf16[16,192,512]{2,1,0:T(8,128)(2,1)S(1)} %get-tuple-element.16), kind=kLoop, calls=%fused_computation.6 | loop fusion | flops 12582912 | bytes 12582912 | tf_op jit(solution)/shard_map/concatenate | solution.py:58
  136.1 3.4 %convolution_bitcast_fusion = f32[512,512]{1,0:T(8,128)S(1)} fusion(bf16[16,192,512]{2,1,0:T(8,128)(2,1)S(1)} %get-tuple-element.17, bf16[16,192,512]{2,1,0:T(8,128)(2,1)S(1)} %get-tuple-element.16), kind=kOutput, calls=%fused_computation.11 | convolution fusion | flops 3233808384 | bytes 7340032 | tf_op jit(solution)/shard_map/dot_general | solution.py:11
  139.6 3.4 %fusion.18 = f32[512,512]{0,1:T(8,128)S(1)} fusion(bf16[6144,512]{1,0:T(8,128)(2,1)S(1)} %bitcast.45, bf16[256,6144]{0,1:T(8,128)(2,1)S(1)} %get-tuple-element.15, bf16[256,6144]{0,1:T(8,128)(2,1)S(1)} %get-tuple-element.14), kind=kOutput, calls=%fused_computation.38 | convolution fusion | flops 3233808384 | bytes 13631488 | tf_op jit(solution)/shard_map/dot_general | solution.py:11
  143.0 1.8 fusion.10
  144.8 58.8 %reduce-scatter.2.cloned.1.call-done = f32[416,512]{1,0:T(8,128)} async-done(((f32[6656,512]{1,0:T(8,128)}), f32[416,512]{1,0:T(8,128)}) %reduce-scatter.2.cloned.1.call-update) | async-done | bytes 851984 | tf_op jit(solution)/shard_map/reduce_scatter | solution.py:61
  203.7 0.8 reduce-precision_convert_fusion.1
  204.5 1.2 slice.65
  205.7 0.8 pad_maximum_fusion.3
  206.5 5.1 %pad_maximum_fusion.2 = bf16[512,6144]{0,1:T(8,128)(2,1)} fusion(bf16[256,6144]{0,1:T(8,128)(2,1)} %copy-done.1, bf16[256,6144]{0,1:T(8,128)(2,1)S(1)} %get-tuple-element.14), kind=kLoop, calls=%fused_computation.7 | loop fusion | flops 12582912 | bytes 12582912 | tf_op jit(solution)/shard_map/concatenate | solution.py:71
  211.6 62.5 %all-gather.7.cloned.1.call-done = bf16[7168,512]{1,0:T(8,128)(2,1)} async-done(((bf16[448,512]{1,0:T(8,128)(2,1)}), bf16[7168,512]{1,0:T(8,128)(2,1)}) %all-gather.7.cloned.1.call-update) | async-done | bytes 7340048 | tf_op jit(solution)/shard_map/all_gather | solution.py:78
  274.2 1.4 convert_add_fusion
  275.6 7.8 %fusion.3 = f32[512,512]{0,1:T(8,128)S(1)} fusion(bf16[512,16,384]{0,2,1:T(8,128)(2,1)} %bitcast.44, bf16[16,448,512]{2,1,0:T(8,128)(2,1)} %bitcast.49), kind=kOutput, calls=%fused_computation.10 | convolution fusion | flops 3221225472 | bytes 13631488 | tf_op jit(solution)/shard_map/dot_general | solution.py:88
  283.4 1.2 fusion.11
  284.6 1.0 copy.23
  285.6 0.6 fusion.6
  286.2 1.1 copy.24
  (18 shorter events, 0.1 us)
Async XLA Ops:
  7.2 1.0 copy-start
  7.2 51.6 %all-gather.5.cloned.1.call-start = ((), (), s32[]{:S(2)}) async-start(), calls=%async_computation.2 | async-start | bytes 3342336 | tf_op jit(solution)/shard_map/all_gather | solution.py:45
  9.1 194.5 %reduce-scatter.2.cloned.1.call-start = ((), (), s32[]{:S(2)}) async-start(), calls=%async_computation.1 | async-start | bytes 14483456 | tf_op jit(solution)/shard_map/reduce_scatter | solution.py:61
  17.0 3.3 %copy-start.2 = (f32[256,512]{1,0:T(8,128)S(1)}, f32[256,512]{1,0:T(8,128)}, u32[]{:S(2)}) copy-start(f32[256,512]{1,0:T(8,128)} %param.3) | copy-start | bytes 1572868
  58.8 215.3 %all-gather.7.cloned.1.call-start = ((), (), s32[]{:S(2)}) async-start(), calls=%async_computation.3 | async-start | bytes 7798784 | tf_op jit(solution)/shard_map/all_gather | solution.py:78
  59.0 70.6 %collective-permute-start = (bf16[16,192,512]{2,1,0:T(8,128)(2,1)}, bf16[16,192,512]{2,1,0:T(8,128)(2,1)}, u32[]{:S(2)}, u32[]{:S(2)}) collective-permute-start(bf16[16,192,512]{2,1,0:T(8,128)(2,1)} %bitcast.1), channel_id=1, source_target_pairs={{0,16},{16,0},{1,17},{17,1},{2,18},{18,2},{3,19},{19,3},{4,20},{20... | collective-permute-start | bytes 9437192 | tf_op jit(solution)/shard_map/ppermute | solution.py:56
  64.3 75.2 %copy-start.1 = (bf16[256,6144]{0,1:T(8,128)(2,1)}, bf16[256,6144]{0,1:T(8,128)(2,1)S(1)}, u32[]{:S(2)}) copy-start(bf16[256,6144]{0,1:T(8,128)(2,1)S(1)} %get-tuple-element.15) | copy-start | bytes 9437188
  136.1 3.4 %copy-start.5 = (bf16[16,384,512]{2,1,0:T(8,128)(2,1)S(1)}, bf16[16,384,512]{2,1,0:T(8,128)(2,1)}, u32[]{:S(2)}) copy-start(bf16[16,384,512]{2,1,0:T(8,128)(2,1)} %pad_maximum_fusion.1) | copy-start | bytes 18874372
  139.5 3.5 %copy-start.3 = (f32[256,512]{1,0:T(8,128)S(1)}, f32[256,512]{1,0:T(8,128)}, u32[]{:S(2)}) copy-start(f32[256,512]{1,0:T(8,128)} %param.3) | copy-start | bytes 1572868
  275.5 7.9 %copy-start.4 = (f32[256,512]{1,0:T(8,128)S(1)}, f32[256,512]{1,0:T(8,128)}, u32[]{:S(2)}) copy-start(f32[256,512]{1,0:T(8,128)} %param.3) | copy-start | bytes 1572868
  275.5 7.9 %copy-start.6 = (f32[256,512]{0,1:T(8,128)S(1)}, f32[256,512]{0,1:T(8,128)}, u32[]{:S(2)}) copy-start(f32[256,512]{0,1:T(8,128)} %fusion.10) | copy-start | bytes 1572868
  275.5 10.0 %copy-start.7 = (f32[416,512]{1,0:T(8,128)S(1)}, f32[416,512]{1,0:T(8,128)}, u32[]{:S(2)}) copy-start(f32[416,512]{1,0:T(8,128)} %reduce-scatter.2.cloned.1.call-done) | copy-start | bytes 2555908
Sparse Core Ops, SparseCore 0:
  10.9 47.8 all-gather.4
  62.9 140.7 reduce-scatter.1
  206.8 67.3 all-gather.6

commit v17 on v16

--- a/solution.py
+++ b/solution.py
@@ -76,14 +76,14 @@
     )
     heads_terms, packed = lax.optimization_barrier((heads_terms, packed))
     gathered = lax.all_gather(packed, "rows", axis=0, tiled=False)
-    moment = (
-        gathered[:, f_here : f_here + d_here].astype(jnp.float32)
-        + gathered[:, f_here + d_here :].astype(jnp.float32)
-    ).reshape(model_width, model_width)
+    moment_high = gathered[:, f_here : f_here + d_here].reshape(model_width, model_width)
+    moment_low = gathered[:, f_here + d_here :].reshape(model_width, model_width)
+    moment = moment_high.astype(jnp.float32) + moment_low.astype(jnp.float32)
 
-    grad_heads = head_scale * (
-        contract(moment, heads.astype(jnp.float32), 1, 0, lax.Precision.HIGH) - cross_here.T
+    moment_heads = contract(moment_high, heads, 1, 0, lax.Precision.DEFAULT) + contract(
+        moment_low, heads, 1, 0, lax.Precision.DEFAULT
     )
+    grad_heads = head_scale * (moment_heads - cross_here.T)
 
     teacher_cross = lax.dot_general(
         teacher_pair.reshape(2 * rows_here, devices, f_here),

time: 294 us -> 296 us (level)
    dot_general x6 -> x7, matrix products: 19.1 us -> 20.4 us  [contract(): lax.dot_general(left, right, (((left_dim,), (right_dim,)), ((), ())), pre...]
    unnamed x21 -> x19, local copies, waits for them, and re-layouts: 11.7 us -> 11.7 us
where the time goes in v17:
time: 296 us; the launch traced here: 295 us
  waiting for transfers between devices  217 us (73%)
  matrix products  28.2 us (10%)
  other arithmetic  20.2 us (7%)
  local copies, waits for them, and re-layouts  14.3 us (5%)
  between operations  13.9 us (5%)
    ppermute x1, waiting for transfers between devices, per_device(): theirs = lax.ppermute(mine, 'groups', [(0, 1), (1, 0)])  65.3 us
    all_gather x1, waiting for transfers between devices, per_device(): gathered = lax.all_gather(packed, 'rows', axis=0, tiled=False)  62.5 us
    reduce_scatter x1, waiting for transfers between devices, per_device(): reduced = lax.psum_scatter(partial, 'rows', scatter_dimension=0, tiled=True)  58.8 us
    all_gather x1, waiting for transfers between devices, per_device(): mine = lax.all_gather(mine, 'rows', axis=0, tiled=False)  29.9 us
    dot_general x7, matrix products, contract(): lax.dot_general(left, right, (((left_dim,), (right_dim,)), ((), ())), pre...  20.4 us
    unnamed x19, local copies, waits for them, and re-layouts  11.7 us
    dot_general x1, matrix products, per_device(): lax.dot_general(teacher_pair.reshape(2 * rows_here, devices, f_here), gat...  7.74 us
  transfers between devices with their start and end apart: 4, of which 4 were waited for; matrix products, arithmetic and copies ran while one was open for 15% of the time, Pallas kernels for 0%

profile of v17, /device:TPU:0, one launch (start us, length us, event | category | flops | bytes accessed | tf_op | source)
XLA Modules:
  0.0 295.1 jit_solution(6506281715525761967)
XLA Ops:
  7.2 0.0 all-gather.5.cloned.1.call-start
  7.2 0.9 copy-done
  8.2 0.1 constant_dynamic-slice_fusion
  8.3 0.8 copy.34
  9.1 0.0 reduce-scatter.2.cloned.1.call-start
  9.2 1.2 copy.15
  10.4 6.5 %copy.14 = f32[256,6144]{0,1:T(8,128)} copy(f32[256,6144]{1,0:T(8,128)} %param.4) | data formatting | bytes 12582912 | tf_op args[1]
  17.0 3.3 %pad_maximum_fusion = f32[256,16,416]{0,2,1:T(8,128)S(1)} fusion(f32[256,16,32]{0,2,1:T(8,128)S(1)} %bitcast.51, f32[256,16,384]{0,2,1:T(8,128)} %bitcast.43), kind=kLoop, calls=%fused_computation.2 | loop fusion | flops 1703936 | bytes 13631488 | tf_op jit(solution)/shard_map/concatenate | solution.py:47
  20.3 8.6 %fusion.24 = f32[6656,512]{1,0:T(8,128)} fusion(f32[256,6656]{0,1:T(8,128)S(1)} %bitcast.44, f32[256,512]{1,0:T(8,128)S(1)} %copy-done.2), kind=kOutput, calls=%fused_computation.43 | convolution fusion | flops 5234491392 | bytes 20971520 | tf_op jit(solution)/shard_map/dot_general | solution.py:11
  28.9 29.9 %all-gather.5.cloned.1.call-done = bf16[3072,512]{1,0:T(8,128)(2,1)} async-done(((bf16[192,512]{1,0:T(8,128)(2,1)}), bf16[3072,512]{1,0:T(8,128)(2,1)}) %all-gather.5.cloned.1.call-update) | async-done | bytes 3145744 | tf_op jit(solution)/shard_map/all_gather | solution.py:45
  58.8 0.2 all-gather.7.cloned.1.call-start
  59.0 1.5 collective-permute-start
  60.6 3.8 %reduce-precision_convert_fusion = (bf16[256,6144]{0,1:T(8,128)(2,1)S(1)}, bf16[256,6144]{0,1:T(8,128)(2,1)S(1)}) fusion(f32[256,6144]{0,1:T(8,128)} %copy.14), kind=kLoop, calls=%fused_computation.1 | loop fusion | flops 6291456 | bytes 12582912 | tf_op jit(solution)/shard_map/convert_element_type | solution.py:23
  64.3 65.3 %collective-permute-done = bf16[16,192,512]{2,1,0:T(8,128)(2,1)} collective-permute-done((bf16[16,192,512]{2,1,0:T(8,128)(2,1)}, bf16[16,192,512]{2,1,0:T(8,128)(2,1)}, u32[]{:S(2)}, u32[]{:S(2)}) %collective-permute-start) | collective-permute-done | bytes 3145760 | tf_op jit(solution)/shard_map/ppermute | solution.py:56
  129.7 3.3 %broadcast_select_fusion.1 = (bf16[16,192,512]{2,1,0:T(8,128)(2,1)S(1)}, bf16[16,192,512]{2,1,0:T(8,128)(2,1)S(1)}) fusion(bf16[16,192,512]{2,1,0:T(8,128)(2,1)} %bitcast.1, bf16[16,192,512]{2,1,0:T(8,128)(2,1)} %collective-permute-done, pred[]{:T(512)S(6)} %eq.3), kind=kLoop, calls=%fused_computation.9 | loop fusion | flops 3145728 | bytes 12582913 | tf_op jit(solution)/shard_map/jit(_where)/select_n | solution.py:59
  132.9 3.1 %pad_maximum_fusion.1 = bf16[16,384,512]{2,1,0:T(8,128)(2,1)} fusion(bf16[16,192,512]{2,1,0:T(8,128)(2,1)S(1)} %get-tuple-element.19, bf16[16,192,512]{2,1,0:T(8,128)(2,1)S(1)} %get-tuple-element.18), kind=kLoop, calls=%fused_computation.6 | loop fusion | flops 12582912 | bytes 12582912 | tf_op jit(solution)/shard_map/concatenate | solution.py:58
  136.1 3.4 %convolution_bitcast_fusion = f32[512,512]{1,0:T(8,128)S(1)} fusion(bf16[16,192,512]{2,1,0:T(8,128)(2,1)S(1)} %get-tuple-element.19, bf16[16,192,512]{2,1,0:T(8,128)(2,1)S(1)} %get-tuple-element.18), kind=kOutput, calls=%fused_computation.11 | convolution fusion | flops 3233808384 | bytes 7340032 | tf_op jit(solution)/shard_map/dot_general | solution.py:11
  139.6 3.4 %fusion.22 = f32[512,512]{0,1:T(8,128)S(1)} fusion(bf16[6144,512]{1,0:T(8,128)(2,1)S(1)} %bitcast.46, bf16[256,6144]{0,1:T(8,128)(2,1)S(1)} %get-tuple-element.17, bf16[256,6144]{0,1:T(8,128)(2,1)S(1)} %get-tuple-element.16), kind=kOutput, calls=%fused_computation.41 | convolution fusion | flops 3233808384 | bytes 13631488 | tf_op jit(solution)/shard_map/dot_general | solution.py:11
  143.0 1.8 fusion.11
  144.8 58.8 %reduce-scatter.2.cloned.1.call-done = f32[416,512]{1,0:T(8,128)} async-done(((f32[6656,512]{1,0:T(8,128)}), f32[416,512]{1,0:T(8,128)}) %reduce-scatter.2.cloned.1.call-update) | async-done | bytes 851984 | tf_op jit(solution)/shard_map/reduce_scatter | solution.py:61
  203.7 0.8 reduce-precision_convert_fusion.1
  204.5 1.2 slice.63
  205.7 0.8 pad_maximum_fusion.3
  206.5 5.1 %pad_maximum_fusion.2 = bf16[512,6144]{0,1:T(8,128)(2,1)} fusion(bf16[256,6144]{0,1:T(8,128)(2,1)} %copy-done.1, bf16[256,6144]{0,1:T(8,128)(2,1)S(1)} %get-tuple-element.16), kind=kLoop, calls=%fused_computation.7 | loop fusion | flops 12582912 | bytes 12582912 | tf_op jit(solution)/shard_map/concatenate | solution.py:71
  211.6 62.5 %all-gather.7.cloned.1.call-done = bf16[7168,512]{1,0:T(8,128)(2,1)} async-done(((bf16[448,512]{1,0:T(8,128)(2,1)}), bf16[7168,512]{1,0:T(8,128)(2,1)}) %all-gather.7.cloned.1.call-update) | async-done | bytes 7340048 | tf_op jit(solution)/shard_map/all_gather | solution.py:78
  274.2 1.3 fusion.23
  275.5 7.7 %fusion.3 = f32[512,512]{0,1:T(8,128)S(1)} fusion(bf16[512,16,384]{0,2,1:T(8,128)(2,1)} %bitcast.45, bf16[16,448,512]{2,1,0:T(8,128)(2,1)} %bitcast.54), kind=kOutput, calls=%fused_computation.10 | convolution fusion | flops 3221225472 | bytes 13631488 | tf_op jit(solution)/shard_map/dot_general | solution.py:88
  283.2 0.4 fusion.25
  283.7 1.2 fusion.12
  284.8 1.0 copy.25
  285.8 1.5 fusion.7
  287.4 1.1 copy.26
  (17 shorter events, 0.1 us)
Async XLA Ops:
  7.2 1.0 copy-start
  7.2 51.6 %all-gather.5.cloned.1.call-start = ((), (), s32[]{:S(2)}) async-start(), calls=%async_computation.2 | async-start | bytes 3342336 | tf_op jit(solution)/shard_map/all_gather | solution.py:45
  9.1 194.5 %reduce-scatter.2.cloned.1.call-start = ((), (), s32[]{:S(2)}) async-start(), calls=%async_computation.1 | async-start | bytes 14483456 | tf_op jit(solution)/shard_map/reduce_scatter | solution.py:61
  17.0 3.3 %copy-start.2 = (f32[256,512]{1,0:T(8,128)S(1)}, f32[256,512]{1,0:T(8,128)}, u32[]{:S(2)}) copy-start(f32[256,512]{1,0:T(8,128)} %param.3) | copy-start | bytes 1572868
  58.8 215.3 %all-gather.7.cloned.1.call-start = ((), (), s32[]{:S(2)}) async-start(), calls=%async_computation.3 | async-start | bytes 7798784 | tf_op jit(solution)/shard_map/all_gather | solution.py:78
  59.0 70.6 %collective-permute-start = (bf16[16,192,512]{2,1,0:T(8,128)(2,1)}, bf16[16,192,512]{2,1,0:T(8,128)(2,1)}, u32[]{:S(2)}, u32[]{:S(2)}) collective-permute-start(bf16[16,192,512]{2,1,0:T(8,128)(2,1)} %bitcast.1), channel_id=1, source_target_pairs={{0,16},{16,0},{1,17},{17,1},{2,18},{18,2},{3,19},{19,3},{4,20},{20... | collective-permute-start | bytes 9437192 | tf_op jit(solution)/shard_map/ppermute | solution.py:56
  64.3 75.2 %copy-start.1 = (bf16[256,6144]{0,1:T(8,128)(2,1)}, bf16[256,6144]{0,1:T(8,128)(2,1)S(1)}, u32[]{:S(2)}) copy-start(bf16[256,6144]{0,1:T(8,128)(2,1)S(1)} %get-tuple-element.17) | copy-start | bytes 9437188
  136.1 3.4 %copy-start.5 = (bf16[16,384,512]{2,1,0:T(8,128)(2,1)S(1)}, bf16[16,384,512]{2,1,0:T(8,128)(2,1)}, u32[]{:S(2)}) copy-start(bf16[16,384,512]{2,1,0:T(8,128)(2,1)} %pad_maximum_fusion.1) | copy-start | bytes 18874372
  139.5 3.5 %copy-start.3 = (f32[256,512]{1,0:T(8,128)S(1)}, f32[256,512]{1,0:T(8,128)}, u32[]{:S(2)}) copy-start(f32[256,512]{1,0:T(8,128)} %param.3) | copy-start | bytes 1572868
  275.4 8.2 %copy-start.4 = (f32[256,512]{1,0:T(8,128)S(1)}, f32[256,512]{1,0:T(8,128)}, u32[]{:S(2)}) copy-start(f32[256,512]{1,0:T(8,128)} %param.3) | copy-start | bytes 1572868
  275.4 8.2 %copy-start.6 = (f32[256,512]{0,1:T(8,128)S(1)}, f32[256,512]{0,1:T(8,128)}, u32[]{:S(2)}) copy-start(f32[256,512]{0,1:T(8,128)} %fusion.11) | copy-start | bytes 1572868
Sparse Core Ops, SparseCore 0:
  10.9 47.8 all-gather.4
  62.9 140.7 reduce-scatter.1
  206.8 67.3 all-gather.6
